TPU v7x, 256 devices: a whole 4x4x8 slice. The times are simulated.
256 devices in a mesh: section: 16 (over y, x), dp: 16 (over z, core).
Axes of the slice: x: 4, y: 4, z: 8, core: 2. Of those that a mesh axis runs over, the one named last changes fastest.
Arguments:
- hidden: bfloat16 [16, 256, 8192], P('dp', 'section'), may hold values from -1500 to 1500
- head: bfloat16 [65536, 8192], P('section', 'dp'), may hold values from -0.0625 to 0.0625
- block_id: int32 [16, 16], P(None, 'section'), may hold values from 0 to 7
- block_live: int32 [16, 16], P(None, 'section'), may hold values from 0 to 1, as said below
- teacher: bfloat16 [16, 256, 8192], P('dp', None, 'section'), may hold values from -400 to 400
Outputs:
- grad_hidden: bfloat16 [16, 256, 8192], P('dp', 'section')
- grad_head: bfloat16 [65536, 8192], P('section', 'dp')
Inputs may be any that keep to these rules, and one draw needn't show every extreme that they name: `block_live`: every micro-batch has at least one live section.
All inputs are finite; a program needn't handle non-finite values.
Results may differ from a plain program's by a relative error of at most 0.0056.
Values may be sent and summed in bfloat16 or wider, within the bound.
No kernel may reach another device: no remote copies, remote signals or barrier semaphores. Data moves between devices by JAX's collectives and lax.ppermute only.
A program may use at most 128 MiB of HBM per device.

v0:
```python
import jax
import jax.numpy as jnp
from jax import lax
from jax.sharding import PartitionSpec as P

neg_fill = -1e30


def local(hidden, head, block_id, block_live, teacher):
    my_replica = lax.axis_index("dp")
    tok_local = hidden.shape[1]
    model_width = hidden.shape[2]
    block_rows = teacher.shape[2]
    col_width = head.shape[1]
    blocks = head.shape[0] // block_rows
    table = head.reshape(blocks, block_rows, col_width)
    block_ids = block_id[:, 0]
    live_flags = block_live[:, 0]
    picked = jnp.take(table, block_ids, axis=0)
    whole = lax.all_gather(hidden, "section", axis=1, tiled=True)
    hidden_rows = whole[0]
    own_live = lax.dynamic_index_in_dim(live_flags, my_replica, 0, keepdims=False) > 0
    full_rows = lax.all_to_all(picked, "dp", split_axis=0, concat_axis=2, tiled=True)[0]
    logits = jnp.einsum("td,rd->tr", hidden_rows, full_rows, preferred_element_type=jnp.float32)
    teach = teacher[0].astype(jnp.float32)
    live_value = jnp.where(own_live, 1.0, 0.0).astype(jnp.float32)
    stud_local = jnp.where(own_live, jnp.max(logits, axis=1), neg_fill)
    teach_local = jnp.where(own_live, jnp.max(teach, axis=1), neg_fill)
    stud_top, teach_top = lax.pmax((stud_local, teach_local), "section")
    stud_part = jnp.where(own_live, jnp.sum(jnp.exp(logits - stud_top[:, None]), axis=1), 0.0)
    teach_part = jnp.where(own_live, jnp.sum(jnp.exp(teach - teach_top[:, None]), axis=1), 0.0)
    stud_total, teach_total, live_count = lax.psum((stud_part, teach_part, live_value), "section")
    student = jnp.where(own_live, jnp.exp(logits - stud_top[:, None]) / stud_total[:, None], 0.0)
    teach_prob = jnp.where(
        own_live, jnp.exp(teach - teach_top[:, None]) / teach_total[:, None], 0.0
    )
    logit_grad = (block_rows * live_count * (student - teach_prob)).astype(jnp.bfloat16)
    summed = lax.psum_scatter(
        jnp.dot(logit_grad, full_rows, preferred_element_type=jnp.float32),
        "section",
        scatter_dimension=0,
        tiled=True,
    )
    grad_hidden = summed.astype(jnp.bfloat16).reshape(1, tok_local, model_width)
    contrib = jnp.einsum(
        "tr,td->rd", logit_grad, hidden_rows, preferred_element_type=jnp.float32
    ).astype(jnp.bfloat16)
    returned = lax.all_to_all(contrib[None], "dp", split_axis=2, concat_axis=0, tiled=True)
    block_range = jnp.arange(blocks, dtype=jnp.int32)[None, :]
    selector = jnp.where(
        (live_flags[:, None] > 0) & (block_ids[:, None] == block_range), 1.0, 0.0
    ).astype(jnp.bfloat16)
    grad_head = jnp.einsum("mb,mrc->brc", selector, returned, preferred_element_type=jnp.float32)
    grad_head = grad_head.astype(jnp.bfloat16).reshape(blocks * block_rows, col_width)
    return (grad_hidden, grad_head)


def solution(mesh):
    placed = (
        P("dp", "section", None),
        P("section", "dp"),
        P(None, "section"),
        P(None, "section"),
        P("dp", None, "section"),
    )
    return jax.shard_map(
        local,
        mesh=mesh,
        in_specs=placed,
        out_specs=(P("dp", "section", None), P("section", "dp")),
        check_vma=False,
    )
```

profile of v0, /device:TPU:2, one launch (start us, length us, event | category | flops | bytes accessed | tf_op | source)
XLA Modules:
  0.0 687.0 jit_solution(2337014340000765486)
XLA Ops:
  7.2 0.7 fusion.26
  7.8 0.7 and_bitcast_fusion
  8.5 6.9 %gather_fusion = bf16[16,512,512]{2,1,0:T(8,128)(2,1)} fusion(bf16[8,512,512]{2,1,0:T(8,128)(2,1)} %bitcast.57, s32[1024]{0:T(1024)S(1)} %pad_clamp_fusion), kind=kCustom, calls=%fused_computation | custom fusion | bytes 16777280 | tf_op jit(solution)/shard_map/jit(_take)/gather | solution.py:19
  15.4 7.5 %broadcast_select_fusion = bf16[16,512,512]{2,1,0:T(8,128)(2,1)} fusion(bf16[16,512,512]{2,1,0:T(8,128)(2,1)} %gather_fusion, pred[16]{0:T(512)(128)(4,1)S(1)} %and_bitcast_fusion), kind=kLoop, calls=%fused_computation.5 | loop fusion | flops 4194304 | bytes 16777232 | tf_op jit(solution)/shard_map/jit(_take)/select_n | solution.py:19
  22.9 8.8 %all-to-all-start = ((bf16[16,512,512]{2,1,0:T(8,128)(2,1)}), bf16[16,512,512]{2,1,0:T(8,128)(2,1)}, u32[]{:S(2)}, u32[]{:S(2)}) async-start(bf16[16,512,512]{2,1,0:T(8,128)(2,1)} %broadcast_select_fusion), calls=%async_computation | async-start | bytes 16777216 | tf_op jit(solution)/shard_map/all_to_all | solution.py:23
  31.7 0.7 all-gather.2.cloned.1.call-update
  34.0 181.9 %all-to-all-done = bf16[16,512,512]{2,1,0:T(8,128)(2,1)} async-done(((bf16[16,512,512]{2,1,0:T(8,128)(2,1)}), bf16[16,512,512]{2,1,0:T(8,128)(2,1)}, u32[]{:S(2)}, u32[]{:S(2)}) %all-to-all-start) | async-done | bytes 8388640 | tf_op jit(solution)/shard_map/all_to_all | solution.py:23
  215.9 12.3 %copy.13 = bf16[1,512,16,512]{1,3,2,0:T(8,128)(2,1)} copy(bf16[1,512,16,512]{3,1,2,0:T(8,128)(2,1)} %bitcast.5) | data formatting | bytes 16777216 | tf_op jit(solution)/shard_map/all_to_all | solution.py:23
  228.2 7.0 %fusion.31 = (f32[256]{0:T(256)S(1)}, f32[512,256]{1,0:T(8,128)S(1)}) fusion(bf16[512,8192]{0,1:T(8,128)(2,1)} %bitcast.55, bf16[1,256,8192]{2,1,0:T(8,128)(2,1)} %all-gather.2.cloned.1.call-done), kind=kOutput, calls=%fused_computation.43 | convolution fusion | flops 2147614464 | bytes 13108224 | tf_op jit(solution)/shard_map/td,rd->tr/dot_general | solution.py:24
  235.8 36.6 %all-reduce.1 = (f32[256]{0:T(256)S(1)}, f32[256]{0:T(256)S(1)}) all-reduce(f32[256]{0:T(256)S(1)} %get-tuple-element.9, f32[256]{0:T(256)S(1)} %get-tuple-element.10), channel_id=1, replica_groups=mesh['section'=16,'dp'=16] {'section'}, use_global_device_ids=true, to_apply=%region_6.7 | all-reduce | flops 512 | bytes 4096 | tf_op jit(solution)/shard_map/pmax | solution.py:29
  274.0 40.7 %all-reduce = (f32[256]{0:T(256)S(1)}, f32[256]{0:T(256)S(1)}, f32[]{:T(128)}) all-reduce(f32[256]{0:T(256)S(1)} %broadcast_select_fusion.1, f32[256]{0:T(256)S(1)} %broadcast_select_fusion.2, f32[]{:T(128)S(6)} %select_n.61), channel_id=1, replica_groups=mesh['section'=16,'dp'=16] {'section'}, use_global_device_ids=true, to_apply=%region_8.9 | all-reduce | flops 513 | bytes 4104 | tf_op jit(solution)/shard_map/psum | solution.py:32
  315.3 9.8 %fusion.28 = f32[256,8192]{1,0:T(8,128)} fusion(bf16[512,8192]{0,1:T(8,128)(2,1)} %bitcast.56, f32[512,256]{1,0:T(8,128)S(1)} %get-tuple-element.8, bf16[1,256,512]{1,2,0:T(8,128)(2,1)S(1)} %copy.14, f32[256]{0:T(256)S(1)} %get-tuple-element.2, f32[256]{0:T(256)S(1)} %get-tuple-element.5, f32[256]{0:T(256)S(1)} %get-tuple-element.3, ...), kind=kOutput, calls=%fused_computation.41 | convolution fusion | flops 2148794368 | bytes 17567748 | tf_op jit(solution)/shard_map/dot_general | solution.py:39
  325.2 8.5 %fusion = bf16[1,512,8192]{2,1,0:T(8,128)(2,1)} fusion(bf16[1,256,8192]{2,1,0:T(8,128)(2,1)} %all-gather.2.cloned.1.call-done, f32[512,256]{1,0:T(8,128)S(1)} %get-tuple-element.8, bf16[1,256,512]{1,2,0:T(8,128)(2,1)S(1)} %copy.14, f32[256]{0:T(256)S(1)} %get-tuple-element.2, f32[256]{0:T(256)S(1)} %get-tuple-element.5, f32[256]{0:T(256)S(1)} %get-tuple-element.3, ...), kind=kOutput, calls=%fused_computation.2 | convolution fusion | flops 2152988672 | bytes 13373445 | tf_op jit(solution)/shard_map/tr,td->rd/dot_general | solution.py:45
  333.7 34.8 %copy.15 = bf16[1,512,8192]{1,0,2:T(2,128)(2,1)} copy(bf16[1,512,8192]{2,1,0:T(8,128)(2,1)} %fusion) | data formatting | bytes 16777216 | tf_op jit(solution)/shard_map/broadcast_in_dim | solution.py:48
  369.0 54.6 %reduce.4 = bf16[8192,512]{1,0:T(8,128)(2,1)} reduce(bf16[8192,1,512]{2,1,0:T(2,128)(2,1)} %bitcast.53, bf16[]{:T(256)} %broadcast.31), dimensions={1}, to_apply=%bitcast.46.reduce_sub_computation | reduce | bytes 16777218
  423.6 14.6 %reshape.42 = bf16[16,2,131072]{2,1,0:T(2,128)(2,1)} reshape(bf16[8192,512]{1,0:T(8,128)(2,1)} %reduce.4) | data formatting | bytes 16777216
  438.2 5.0 all-to-all-start.1
  443.3 184.0 %all-to-all-done.1 = bf16[16,2,131072]{2,1,0:T(2,128)(2,1)} async-done(((bf16[16,2,131072]{2,1,0:T(2,128)(2,1)}), bf16[16,2,131072]{2,1,0:T(2,128)(2,1)}, u32[]{:S(2)}, u32[]{:S(2)}) %all-to-all-start.1) | async-done | bytes 8388640 | tf_op jit(solution)/shard_map/all_to_all | solution.py:48
  627.3 16.5 %reshape.43 = bf16[8192,1,512]{2,1,0:T(2,128)(2,1)} reshape(bf16[16,2,131072]{2,1,0:T(2,128)(2,1)} %all-to-all-done.1) | data formatting | bytes 16777216
  643.8 11.6 %copy.19 = bf16[1,512,8192]{1,2,0:T(8,128)(2,1)} copy(bf16[1,512,8192]{1,0,2:T(2,128)(2,1)} %bitcast.52) | data formatting | bytes 16777216
  655.4 14.9 %copy.18 = bf16[1,512,16,512]{3,2,1,0:T(8,128)(2,1)} copy(bf16[1,512,16,512]{1,3,2,0:T(8,128)(2,1)} %bitcast.54) | data formatting | bytes 16777216 | tf_op jit(solution)/shard_map/all_to_all | solution.py:48
  670.3 4.6 fusion.6
  674.9 3.5 copy.17
  678.4 1.8 convert_bitcast_fusion
  (22 shorter events, 3.7 us)
Async XLA Ops:
  22.9 9.6 %copy-start = (bf16[1,256,512]{2,1,0:T(8,128)(2,1)S(1)}, bf16[1,256,512]{2,1,0:T(8,128)(2,1)}, u32[]{:S(2)}) copy-start(bf16[1,256,512]{2,1,0:T(8,128)(2,1)} %param.9) | copy-start | bytes 786436
  22.9 9.8 %copy-start.2 = (s32[16,1]{0,1:T(1,128)S(1)}, s32[16,1]{0,1:T(1,128)}, u32[]{:S(2)}) copy-start(s32[16,1]{0,1:T(1,128)} %param.8) | copy-start | bytes 196
  22.9 193.0 %all-to-all-start = ((bf16[16,512,512]{2,1,0:T(8,128)(2,1)}), bf16[16,512,512]{2,1,0:T(8,128)(2,1)}, u32[]{:S(2)}, u32[]{:S(2)}) async-start(bf16[16,512,512]{2,1,0:T(8,128)(2,1)} %broadcast_select_fusion), calls=%async_computation | async-start | bytes 16777216 | tf_op jit(solution)/shard_map/all_to_all | solution.py:23
  31.6 196.5 %all-gather.2.cloned.1.call-start = ((), (), s32[]{:S(2)}) async-start(), calls=%async_computation.3 | async-start | bytes 4456448 | tf_op jit(solution)/shard_map/all_gather | solution.py:20
  32.4 646.0 %reduce-scatter.2.cloned.1.call-start = ((), (), s32[]{:S(2)}) async-start(), calls=%async_computation.4 | async-start | bytes 8912896 | tf_op jit(solution)/shard_map/reduce_scatter | solution.py:38
  438.2 189.0 %all-to-all-start.1 = ((bf16[16,2,131072]{2,1,0:T(2,128)(2,1)}), bf16[16,2,131072]{2,1,0:T(2,128)(2,1)}, u32[]{:S(2)}, u32[]{:S(2)}) async-start(bf16[16,2,131072]{2,1,0:T(2,128)(2,1)} %reshape.42), calls=%async_computation.2 | async-start | bytes 16777216 | tf_op jit(solution)/shard_map/all_to_all | solution.py:48
  655.4 14.9 %copy-start.1 = (s32[16,1]{0,1:T(1,128)S(1)}, s32[16,1]{0,1:T(1,128)}, u32[]{:S(2)}) copy-start(s32[16,1]{0,1:T(1,128)} %param.7) | copy-start | bytes 196
Sparse Core Ops, SparseCore 0:
  34.9 58.0 all-gather.1
  325.3 85.0 reduce-scatter.1
where the time goes:
time: 690 us; the launch traced here: 687 us
  waiting for transfers between devices  367 us (53%)
  local copies, waits for them, and re-layouts  116 us (17%)
  blocking collectives  77.3 us (11%)
  other arithmetic  68.1 us (10%)
  matrix products  30 us (4%)
  between operations  15.4 us (2%)
  starting transfers between devices  13.9 us (2%)
    all_to_all x1, waiting for transfers between devices, local(): lax.all_to_all(contrib[None], 'dp', split_axis=2, concat_axis=0, tiled=True)  184 us
    all_to_all x1, waiting for transfers between devices, local(): lax.all_to_all(picked, 'dp', split_axis=0, concat_axis=2, tiled=True)[0]  182 us
    unnamed x1, other arithmetic  54.6 us
    unnamed x11, local copies, waits for them, and re-layouts  43.4 us
    psum x1, blocking collectives, local(): lax.psum((stud_part, teach_part, live_value), 'section')  40.7 us
    pmax x1, blocking collectives, local(): stud_top, teach_top = lax.pmax((stud_local, teach_local), 'section')  36.6 us
    broadcast_in_dim x1, local copies, waits for them, and re-layouts, local(): contrib[None]  34.8 us
    all_to_all x1, local copies, waits for them, and re-layouts, local(): lax.all_to_all(contrib[None], 'dp', split_axis=2, concat_axis=0, tiled=True)  14.9 us
  transfers between devices with their start and end apart: 4, of which 2 were waited for; matrix products, arithmetic and copies ran while one was open for 26% of the time, Pallas kernels for 0%

commit v1 on v0

--- a/solution.py
+++ b/solution.py
@@ -8,6 +8,7 @@
 
 def local(hidden, head, block_id, block_live, teacher):
     my_replica = lax.axis_index("dp")
+    n_dp = lax.axis_size("dp")
     tok_local = hidden.shape[1]
     model_width = hidden.shape[2]
     block_rows = teacher.shape[2]
@@ -16,12 +17,17 @@
     table = head.reshape(blocks, block_rows, col_width)
     block_ids = block_id[:, 0]
     live_flags = block_live[:, 0]
+    n_mb = block_ids.shape[0]
+
+    pieces = hidden.reshape(1, tok_local, n_dp, col_width)
+    pieces = lax.all_to_all(pieces, "dp", split_axis=2, concat_axis=0, tiled=True)
+    hid_w = lax.all_gather(pieces, "section", axis=1, tiled=True).reshape(n_mb, -1, col_width)
+
     picked = jnp.take(table, block_ids, axis=0)
-    whole = lax.all_gather(hidden, "section", axis=1, tiled=True)
-    hidden_rows = whole[0]
+    part = jnp.einsum("mtw,mrw->mtr", hid_w, picked, preferred_element_type=jnp.float32)
+    logits = lax.psum_scatter(part, "dp", scatter_dimension=0, tiled=True)[0]
+
     own_live = lax.dynamic_index_in_dim(live_flags, my_replica, 0, keepdims=False) > 0
-    full_rows = lax.all_to_all(picked, "dp", split_axis=0, concat_axis=2, tiled=True)[0]
-    logits = jnp.einsum("td,rd->tr", hidden_rows, full_rows, preferred_element_type=jnp.float32)
     teach = teacher[0].astype(jnp.float32)
     live_value = jnp.where(own_live, 1.0, 0.0).astype(jnp.float32)
     stud_local = jnp.where(own_live, jnp.max(logits, axis=1), neg_fill)
@@ -35,23 +41,22 @@
         own_live, jnp.exp(teach - teach_top[:, None]) / teach_total[:, None], 0.0
     )
     logit_grad = (block_rows * live_count * (student - teach_prob)).astype(jnp.bfloat16)
-    summed = lax.psum_scatter(
-        jnp.dot(logit_grad, full_rows, preferred_element_type=jnp.float32),
-        "section",
-        scatter_dimension=0,
-        tiled=True,
-    )
-    grad_hidden = summed.astype(jnp.bfloat16).reshape(1, tok_local, model_width)
+    grads = lax.all_gather(logit_grad[None], "dp", axis=0, tiled=True)
+
     contrib = jnp.einsum(
-        "tr,td->rd", logit_grad, hidden_rows, preferred_element_type=jnp.float32
+        "mtr,mtw->mrw", grads, hid_w, preferred_element_type=jnp.float32
     ).astype(jnp.bfloat16)
-    returned = lax.all_to_all(contrib[None], "dp", split_axis=2, concat_axis=0, tiled=True)
     block_range = jnp.arange(blocks, dtype=jnp.int32)[None, :]
     selector = jnp.where(
         (live_flags[:, None] > 0) & (block_ids[:, None] == block_range), 1.0, 0.0
     ).astype(jnp.bfloat16)
-    grad_head = jnp.einsum("mb,mrc->brc", selector, returned, preferred_element_type=jnp.float32)
+    grad_head = jnp.einsum("mb,mrw->brw", selector, contrib, preferred_element_type=jnp.float32)
     grad_head = grad_head.astype(jnp.bfloat16).reshape(blocks * block_rows, col_width)
+
+    ghid = jnp.einsum("mtr,mrw->mtw", grads, picked, preferred_element_type=jnp.float32)
+    ghid = lax.psum_scatter(ghid, "section", scatter_dimension=1, tiled=True).astype(jnp.bfloat16)
+    ghid = lax.all_to_all(ghid, "dp", split_axis=0, concat_axis=2, tiled=True)
+    grad_hidden = ghid.reshape(1, tok_local, model_width)
     return (grad_hidden, grad_head)
 
 

time: 690 us -> 413 us (0.60)
  waiting for transfers between devices: 367 us -> 231 us
  local copies, waits for them, and re-layouts: 116 us -> 13.9 us
  other arithmetic: 68.1 us -> 9.45 us
  blocking collectives: 77.3 us -> 96.5 us
  matrix products: 30 us -> 37.7 us
    all_to_all x2 -> x1, waiting for transfers between devices: 366 us -> 0.01 us  [local(): ghid = lax.all_to_all(ghid, 'dp', split_axis=0, concat_axis=2, tiled=True)]
    reduce_scatter x1 -> x2, waiting for transfers between devices: 0.01 us -> 147 us  [the longest x1 79.9 us: local(): lax.psum_scatter(ghid, 'section', scatter_dimension=1, tiled=True)]
    all_gather x1 -> x2, waiting for transfers between devices: 0.01 us -> 84 us  [the longest x1 46.9 us: local(): lax.all_gather(pieces, 'section', axis=1, tiled=True)]
    unnamed x1 -> x0, other arithmetic: 54.6 us -> none
    unnamed x11 -> x7, local copies, waits for them, and re-layouts: 43.4 us -> 1.01 us
    broadcast_in_dim x1 -> x0, local copies, waits for them, and re-layouts: 34.8 us -> none  [local(): contrib[None]]
    all_to_all x2 -> x1, local copies, waits for them, and re-layouts: 27.2 us -> 0.72 us  [local(): ghid = lax.all_to_all(ghid, 'dp', split_axis=0, concat_axis=2, tiled=True)]
    all_to_all x0 -> x1, blocking collectives: none -> 19.7 us  [local(): lax.all_to_all(pieces, 'dp', split_axis=2, concat_axis=0, tiled=True)]
  transfers between devices with their start and end apart: 4 -> 5, of which waited for: 2 -> 4; matrix products, arithmetic and copies ran while one was open for 26% -> 7% of each run, Pallas kernels for 0% -> 0%
where the time goes in v1:
time: 413 us; the launch traced here: 411 us
  waiting for transfers between devices  231 us (56%)
  blocking collectives  96.5 us (23%)
  matrix products  37.7 us (9%)
  between operations  15.1 us (4%)
  local copies, waits for them, and re-layouts  13.9 us (3%)
  other arithmetic  9.45 us (2%)
  starting transfers between devices  7.36 us (2%)
    reduce_scatter x1, waiting for transfers between devices, local(): lax.psum_scatter(ghid, 'section', scatter_dimension=1, tiled=True)  79.9 us
    reduce_scatter x1, waiting for transfers between devices, local(): logits = lax.psum_scatter(part, 'dp', scatter_dimension=0, tiled=True)[0]  67.3 us
    all_gather x1, waiting for transfers between devices, local(): lax.all_gather(pieces, 'section', axis=1, tiled=True)  46.9 us
    psum x1, blocking collectives, local(): lax.psum((stud_part, teach_part, live_value), 'section')  40.5 us
    all_gather x1, waiting for transfers between devices, local(): grads = lax.all_gather(logit_grad[None], 'dp', axis=0, tiled=True)  37.1 us
    pmax x1, blocking collectives, local(): stud_top, teach_top = lax.pmax((stud_local, teach_local), 'section')  36.4 us
    all_to_all x1, blocking collectives, local(): lax.all_to_all(pieces, 'dp', split_axis=2, concat_axis=0, tiled=True)  19.7 us
    dot_general x1, matrix products, local(): jnp.einsum('mtr,mrw->mtw', grads, picked, preferred_element_type=jnp.floa...  10.3 us
  transfers between devices with their start and end apart: 5, of which 4 were waited for; matrix products, arithmetic and copies ran while one was open for 7% of the time, Pallas kernels for 0%

profile of v1, /device:TPU:2, one launch (start us, length us, event | category | flops | bytes accessed | tf_op | source)
XLA Modules:
  0.0 411.3 jit_solution(15351352990721341709)
XLA Ops:
  7.2 1.0 copy.29
  8.2 19.7 %all_to_all.36 = bf16[1,16,16,512]{3,1,0,2:T(8,128)(2,1)} all-to-all(bf16[1,16,16,512]{3,1,0,2:T(8,128)(2,1)S(1)} %bitcast.54), channel_id=1, replica_groups=mesh['section'=16,'dp'=16] {'dp'}, dimensions={2} | all-to-all | bytes 524288 | tf_op jit(solution)/shard_map/all_to_all | solution.py:23
  27.9 0.7 fusion.34
  28.6 6.9 %gather_fusion = bf16[16,512,512]{2,1,0:T(8,128)(2,1)} fusion(bf16[8,512,512]{2,1,0:T(8,128)(2,1)} %bitcast.50, s32[1024]{0:T(1024)S(1)} %pad_clamp_fusion), kind=kCustom, calls=%fused_computation | custom fusion | bytes 16777280 | tf_op jit(solution)/shard_map/jit(_take)/gather | solution.py:26
  35.5 46.9 %all-gather.6.cloned.1.call-done = bf16[16,1,256,1,512]{4,2,0,3,1:T(8,128)(2,1)} async-done(((bf16[16,1,16,1,512]{4,2,0,3,1:T(8,128)(2,1)}), bf16[16,1,256,1,512]{4,2,0,3,1:T(8,128)(2,1)}) %all-gather.6.cloned.1.call-update) | async-done | bytes 4194320 | tf_op jit(solution)/shard_map/all_gather | solution.py:24
  82.4 10.2 %fusion.6 = f32[16,256,512]{1,2,0:T(8,128)} fusion(bf16[16,1,256,1,512]{4,2,0,3,1:T(8,128)(2,1)} %all-gather.6.cloned.1.call-done, bf16[16,512,512]{2,1,0:T(8,128)(2,1)} %gather_fusion, pred[16]{0:T(512)(128)(4,1)S(1)} %and_bitcast_fusion), kind=kOutput, calls=%fused_computation.9 | convolution fusion | flops 2151677952 | bytes 20971536 | tf_op jit(solution)/shard_map/mtw,mrw->mtr/dot_general | solution.py:27
  92.7 0.9 copy-done
  95.1 0.6 convert_select_fusion
  95.7 67.3 %reduce-scatter.3.cloned.1.call-done = f32[1,256,512]{1,2,0:T(8,128)} async-done(((f32[16,256,512]{1,2,0:T(8,128)}), f32[1,256,512]{1,2,0:T(8,128)}) %reduce-scatter.3.cloned.1.call-update) | async-done | bytes 524304 | tf_op jit(solution)/shard_map/reduce_scatter | solution.py:28
  163.1 1.1 reduce_max.23
  164.9 36.4 %all-reduce.1 = (f32[256]{0:T(256)S(1)}, f32[256]{0:T(256)S(1)}) all-reduce(f32[256]{0:T(256)S(1)} %convert_select_fusion, f32[256]{0:T(256)S(1)} %broadcast_select_fusion.7), channel_id=1, replica_groups=mesh['section'=16,'dp'=16] {'section'}, use_global_device_ids=true, to_apply=%region_7.8 | all-reduce | flops 512 | bytes 4096 | tf_op jit(solution)/shard_map/pmax | solution.py:35
  201.4 1.2 fusion.21
  203.2 40.5 %all-reduce = (f32[256]{0:T(256)S(1)}, f32[256]{0:T(256)S(1)}, f32[]{:T(128)}) all-reduce(f32[256]{0:T(256)S(1)} %get-tuple-element.7, f32[256]{0:T(256)S(1)} %get-tuple-element.8, f32[]{:T(128)S(6)} %select_n.58), channel_id=1, replica_groups=mesh['section'=16,'dp'=16] {'section'}, use_global_device_ids=true, to_apply=%region_9.10 | all-reduce | flops 513 | bytes 4104 | tf_op jit(solution)/shard_map/psum | solution.py:38
  244.3 1.9 fusion.22
  246.2 0.8 copy.16
  247.2 37.1 %all-gather.4.cloned.1.call-done = bf16[16,256,512]{2,1,0:T(8,128)(2,1)} async-done(((bf16[1,256,512]{2,1,0:T(8,128)(2,1)}), bf16[16,256,512]{2,1,0:T(8,128)(2,1)}) %all-gather.4.cloned.1.call-update) | async-done | bytes 4194320 | tf_op jit(solution)/shard_map/all_gather | solution.py:44
  284.2 10.3 %fusion.5 = f32[16,256,512]{2,1,0:T(8,128)} fusion(bf16[16,256,512]{2,1,0:T(8,128)(2,1)} %all-gather.4.cloned.1.call-done, bf16[16,512,512]{2,1,0:T(8,128)(2,1)} %gather_fusion, pred[16]{0:T(512)(128)(4,1)S(1)} %and_bitcast_fusion), kind=kOutput, calls=%fused_computation.8 | convolution fusion | flops 2151677952 | bytes 20971536 | tf_op jit(solution)/shard_map/mtr,mrw->mtw/dot_general | solution.py:56
  294.5 9.1 %convolution_convert_fusion = bf16[16,512,512]{2,1,0:T(8,128)(2,1)} fusion(bf16[16,256,512]{2,1,0:T(8,128)(2,1)} %all-gather.4.cloned.1.call-done, bf16[16,1,256,1,512]{4,2,0,3,1:T(8,128)(2,1)} %all-gather.6.cloned.1.call-done), kind=kOutput, calls=%fused_computation.4 | convolution fusion | flops 2151677952 | bytes 16777216 | tf_op jit(solution)/shard_map/mtr,mtw->mrw/dot_general | solution.py:46
  303.6 79.9 %reduce-scatter.5.cloned.1.call-done = f32[16,16,512]{2,1,0:T(8,128)} async-done(((f32[16,256,512]{2,1,0:T(8,128)}), f32[16,16,512]{2,1,0:T(8,128)}) %reduce-scatter.5.cloned.1.call-update) | async-done | bytes 524304 | tf_op jit(solution)/shard_map/reduce_scatter | solution.py:57
  383.5 1.8 convert_element_type.29
  385.3 7.2 %all-to-all-start.1 = ((bf16[16,16,512]{2,1,0:T(8,128)(2,1)}), bf16[16,16,512]{2,1,0:T(8,128)(2,1)S(1)}, u32[]{:S(2)}, u32[]{:S(2)}) async-start(bf16[16,16,512]{2,1,0:T(8,128)(2,1)} %convert_element_type.29), calls=%async_computation.3 | async-start | bytes 524288 | tf_op jit(solution)/shard_map/all_to_all | solution.py:58
  392.5 8.1 %fusion.9 = bf16[8,512,512]{2,0,1:T(8,128)(2,1)S(1)} fusion(bf16[16,512,512]{2,1,0:T(8,128)(2,1)} %convolution_convert_fusion, s32[16]{0:T(128)S(1)} %bitcast.57, pred[16]{0:T(512)(128)(4,1)S(1)} %compare_bitcast_fusion), kind=kOutput, calls=%fused_computation.10 | convolution fusion | flops 69206528 | bytes 12582992 | tf_op jit(solution)/shard_map/mb,mrw->brw/dot_general | solution.py:53
  400.6 3.5 copy.20
  404.0 0.7 copy.23
  (23 shorter events, 2.5 us)
Async XLA Ops:
  7.2 75.3 %all-gather.6.cloned.1.call-start = ((), (), s32[]{:S(2)}) async-start(), calls=%async_computation.7 | async-start | bytes 4456448 | tf_op jit(solution)/shard_map/all_gather | solution.py:24
  27.9 135.2 %reduce-scatter.3.cloned.1.call-start = ((), (), s32[]{:S(2)}) async-start(), calls=%async_computation.4 | async-start | bytes 8912896 | tf_op jit(solution)/shard_map/reduce_scatter | solution.py:28
  28.6 6.9 %copy-start.1 = (s32[16,1]{0,1:T(1,128)S(1)}, s32[16,1]{0,1:T(1,128)}, u32[]{:S(2)}) copy-start(s32[16,1]{0,1:T(1,128)} %param.7) | copy-start | bytes 196
  92.6 0.9 copy-start
  92.6 1.2 copy-start.2
  92.6 191.6 %all-gather.4.cloned.1.call-start = ((), (), s32[]{:S(2)}) async-start(), calls=%async_computation.5 | async-start | bytes 4456448 | tf_op jit(solution)/shard_map/all_gather | solution.py:44
  247.1 136.4 %reduce-scatter.5.cloned.1.call-start = ((), (), s32[]{:S(2)}) async-start(), calls=%async_computation.6 | async-start | bytes 8912896 | tf_op jit(solution)/shard_map/reduce_scatter | solution.py:57
  385.3 18.8 %all-to-all-start.1 = ((bf16[16,16,512]{2,1,0:T(8,128)(2,1)}), bf16[16,16,512]{2,1,0:T(8,128)(2,1)S(1)}, u32[]{:S(2)}, u32[]{:S(2)}) async-start(bf16[16,16,512]{2,1,0:T(8,128)(2,1)} %convert_element_type.29), calls=%async_computation.3 | async-start | bytes 524288 | tf_op jit(solution)/shard_map/all_to_all | solution.py:58
Sparse Core Ops, SparseCore 0:
  28.0 54.4 all-gather.5
  92.8 70.2 reduce-scatter.2
  247.2 36.9 all-gather.3
  294.7 88.7 reduce-scatter.4

commit v2 on v1

--- a/solution.py
+++ b/solution.py
@@ -30,12 +30,26 @@
     own_live = lax.dynamic_index_in_dim(live_flags, my_replica, 0, keepdims=False) > 0
     teach = teacher[0].astype(jnp.float32)
     live_value = jnp.where(own_live, 1.0, 0.0).astype(jnp.float32)
-    stud_local = jnp.where(own_live, jnp.max(logits, axis=1), neg_fill)
-    teach_local = jnp.where(own_live, jnp.max(teach, axis=1), neg_fill)
-    stud_top, teach_top = lax.pmax((stud_local, teach_local), "section")
-    stud_part = jnp.where(own_live, jnp.sum(jnp.exp(logits - stud_top[:, None]), axis=1), 0.0)
-    teach_part = jnp.where(own_live, jnp.sum(jnp.exp(teach - teach_top[:, None]), axis=1), 0.0)
-    stud_total, teach_total, live_count = lax.psum((stud_part, teach_part, live_value), "section")
+
+    def local_stats(values):
+        top = jnp.where(own_live, jnp.max(values, axis=1), neg_fill)
+        total = jnp.where(own_live, jnp.sum(jnp.exp(values - top[:, None]), axis=1), 0.0)
+        return top, total
+
+    def merged(tops, totals):
+        top = jnp.max(tops, axis=0)
+        return top, jnp.sum(totals * jnp.exp(tops - top[None, :]), axis=0)
+
+    teach_top_s, teach_sum_s = local_stats(teach)
+    live_row = jnp.broadcast_to(live_value, teach_top_s.shape)
+    teach_all = lax.all_gather(jnp.stack([teach_top_s, teach_sum_s, live_row]), "section")
+    teach_top, teach_total = merged(teach_all[:, 0], teach_all[:, 1])
+    live_count = jnp.sum(teach_all[:, 2, 0])
+
+    stud_top_s, stud_sum_s = local_stats(logits)
+    stud_all = lax.all_gather(jnp.stack([stud_top_s, stud_sum_s]), "section")
+    stud_top, stud_total = merged(stud_all[:, 0], stud_all[:, 1])
+
     student = jnp.where(own_live, jnp.exp(logits - stud_top[:, None]) / stud_total[:, None], 0.0)
     teach_prob = jnp.where(
         own_live, jnp.exp(teach - teach_top[:, None]) / teach_total[:, None], 0.0

time: 413 us -> 385 us (0.932)
  blocking collectives: 96.5 us -> 64.1 us
    all_gather x0 -> x2, blocking collectives: none -> 44.4 us  [the longest x1 23.3 us: local(): lax.all_gather(jnp.stack([teach_top_s, teach_sum_s, live_row]), 'section')]
    psum x1 -> x0, blocking collectives: 40.5 us -> none  [local(): lax.psum((stud_part, teach_part, live_value), 'section')]
    pmax x1 -> x0, blocking collectives: 36.4 us -> none  [local(): stud_top, teach_top = lax.pmax((stud_local, teach_local), 'section')]
  transfers between devices with their start and end apart: 5 -> 5, of which waited for: 4 -> 4; matrix products, arithmetic and copies ran while one was open for 7% -> 8% of each run, Pallas kernels for 0% -> 0%
where the time goes in v2:
time: 385 us; the launch traced here: 383 us
  waiting for transfers between devices  235 us (61%)
  blocking collectives  64.1 us (17%)
  matrix products  37.7 us (10%)
  between operations  15.2 us (4%)
  local copies, waits for them, and re-layouts  14 us (4%)
  other arithmetic  10.3 us (3%)
  starting transfers between devices  7.34 us (2%)
    reduce_scatter x1, waiting for transfers between devices, local(): lax.psum_scatter(ghid, 'section', scatter_dimension=1, tiled=True)  79.6 us
    reduce_scatter x1, waiting for transfers between devices, local(): logits = lax.psum_scatter(part, 'dp', scatter_dimension=0, tiled=True)[0]  67.9 us
    all_gather x1, waiting for transfers between devices, local(): lax.all_gather(pieces, 'section', axis=1, tiled=True)  46.9 us
    all_gather x1, waiting for transfers between devices, local(): grads = lax.all_gather(logit_grad[None], 'dp', axis=0, tiled=True)  40.1 us
    all_gather x1, blocking collectives, local(): lax.all_gather(jnp.stack([teach_top_s, teach_sum_s, live_row]), 'section')  23.3 us
    all_gather x1, blocking collectives, local(): stud_all = lax.all_gather(jnp.stack([stud_top_s, stud_sum_s]), 'section')  21.1 us
    all_to_all x1, blocking collectives, local(): lax.all_to_all(pieces, 'dp', split_axis=2, concat_axis=0, tiled=True)  19.7 us
    dot_general x1, matrix products, local(): jnp.einsum('mtr,mrw->mtw', grads, picked, preferred_element_type=jnp.floa...  10.3 us
  transfers between devices with their start and end apart: 5, of which 4 were waited for; matrix products, arithmetic and copies ran while one was open for 8% of the time, Pallas kernels for 0%

profile of v2, /device:TPU:2, one launch (start us, length us, event | category | flops | bytes accessed | tf_op | source)
XLA Modules:
  0.0 383.1 jit_solution(4583945800723972607)
XLA Ops:
  7.2 1.0 copy.51
  8.2 19.7 %all_to_all.36 = bf16[1,16,16,512]{3,1,0,2:T(8,128)(2,1)} all-to-all(bf16[1,16,16,512]{3,1,0,2:T(8,128)(2,1)S(1)} %bitcast.87), channel_id=1, replica_groups=mesh['section'=16,'dp'=16] {'dp'}, dimensions={2} | all-to-all | bytes 524288 | tf_op jit(solution)/shard_map/all_to_all | solution.py:23
  27.9 0.7 fusion.40
  28.6 6.9 %gather_fusion = bf16[16,512,512]{2,1,0:T(8,128)(2,1)} fusion(bf16[8,512,512]{2,1,0:T(8,128)(2,1)} %bitcast.83, s32[1024]{0:T(1024)S(1)} %pad_clamp_fusion), kind=kCustom, calls=%fused_computation | custom fusion | bytes 16777280 | tf_op jit(solution)/shard_map/jit(_take)/gather | solution.py:26
  35.5 46.9 %all-gather.10.cloned.1.call-done = bf16[16,1,256,1,512]{4,2,0,3,1:T(8,128)(2,1)} async-done(((bf16[16,1,16,1,512]{4,2,0,3,1:T(8,128)(2,1)}), bf16[16,1,256,1,512]{4,2,0,3,1:T(8,128)(2,1)}) %all-gather.10.cloned.1.call-update) | async-done | bytes 4194320 | tf_op jit(solution)/shard_map/all_gather | solution.py:24
  82.4 10.2 %fusion.6 = f32[16,256,512]{1,2,0:T(8,128)} fusion(bf16[16,1,256,1,512]{4,2,0,3,1:T(8,128)(2,1)} %all-gather.10.cloned.1.call-done, bf16[16,512,512]{2,1,0:T(8,128)(2,1)} %gather_fusion, pred[16]{0:T(512)(128)(4,1)S(1)} %and_bitcast_fusion), kind=kOutput, calls=%fused_computation.9 | convolution fusion | flops 2151677952 | bytes 20971536 | tf_op jit(solution)/shard_map/mtw,mrw->mtr/dot_general | solution.py:27
  92.7 0.9 copy-done
  95.1 67.9 %reduce-scatter.3.cloned.1.call-done = f32[1,256,512]{1,2,0:T(8,128)} async-done(((f32[16,256,512]{1,2,0:T(8,128)}), f32[1,256,512]{1,2,0:T(8,128)}) %reduce-scatter.3.cloned.1.call-update) | async-done | bytes 524304 | tf_op jit(solution)/shard_map/reduce_scatter | solution.py:28
  163.1 1.1 reduce_max.43
  164.9 1.2 fusion.21
  166.8 0.6 broadcast_select_fusion.7
  167.5 23.3 %all-gather.3 = f32[16,3,256]{2,1,0:T(4,128)S(1)} all-gather(f32[1,3,256]{2,1,0:T(4,128)S(1)} %maximum_bitcast_fusion), channel_id=2, replica_groups=mesh['section'=16,'dp'=16] {'section'}, dimensions={0}, use_global_device_ids=true | all-gather | bytes 52224 | tf_op jit(solution)/shard_map/all_gather | solution.py:45
  191.5 21.1 %all-gather.4 = f32[16,2,256]{2,1,0:T(2,128)S(1)} all-gather(f32[1,2,256]{2,1,0:T(2,128)S(1)} %maximum_bitcast_fusion.1), channel_id=4, replica_groups=mesh['section'=16,'dp'=16] {'section'}, dimensions={0}, use_global_device_ids=true | all-gather | bytes 34816 | tf_op jit(solution)/shard_map/all_gather | solution.py:50
  213.4 1.9 fusion.22
  215.3 0.8 copy.22
  216.2 40.1 %all-gather.8.cloned.1.call-done = bf16[16,256,512]{2,1,0:T(8,128)(2,1)} async-done(((bf16[1,256,512]{2,1,0:T(8,128)(2,1)}), bf16[16,256,512]{2,1,0:T(8,128)(2,1)}) %all-gather.8.cloned.1.call-update) | async-done | bytes 4194320 | tf_op jit(solution)/shard_map/all_gather | solution.py:58
  256.3 10.3 %fusion.5 = f32[16,256,512]{2,1,0:T(8,128)} fusion(bf16[16,256,512]{2,1,0:T(8,128)(2,1)} %all-gather.8.cloned.1.call-done, bf16[16,512,512]{2,1,0:T(8,128)(2,1)} %gather_fusion, pred[16]{0:T(512)(128)(4,1)S(1)} %and_bitcast_fusion), kind=kOutput, calls=%fused_computation.8 | convolution fusion | flops 2151677952 | bytes 20971536 | tf_op jit(solution)/shard_map/mtr,mrw->mtw/dot_general | solution.py:70
  266.6 9.1 %convolution_convert_fusion = bf16[16,512,512]{2,1,0:T(8,128)(2,1)} fusion(bf16[16,256,512]{2,1,0:T(8,128)(2,1)} %all-gather.8.cloned.1.call-done, bf16[16,1,256,1,512]{4,2,0,3,1:T(8,128)(2,1)} %all-gather.10.cloned.1.call-done), kind=kOutput, calls=%fused_computation.4 | convolution fusion | flops 2151677952 | bytes 16777216 | tf_op jit(solution)/shard_map/mtr,mtw->mrw/dot_general | solution.py:60
  275.7 79.6 %reduce-scatter.5.cloned.1.call-done = f32[16,16,512]{2,1,0:T(8,128)} async-done(((f32[16,256,512]{2,1,0:T(8,128)}), f32[16,16,512]{2,1,0:T(8,128)}) %reduce-scatter.5.cloned.1.call-update) | async-done | bytes 524304 | tf_op jit(solution)/shard_map/reduce_scatter | solution.py:71
  355.3 1.8 convert_element_type.29
  357.1 7.2 %all-to-all-start.1 = ((bf16[16,16,512]{2,1,0:T(8,128)(2,1)}), bf16[16,16,512]{2,1,0:T(8,128)(2,1)S(1)}, u32[]{:S(2)}, u32[]{:S(2)}) async-start(bf16[16,16,512]{2,1,0:T(8,128)(2,1)} %convert_element_type.29), calls=%async_computation.3 | async-start | bytes 524288 | tf_op jit(solution)/shard_map/all_to_all | solution.py:72
  364.3 8.1 %fusion.9 = bf16[8,512,512]{2,0,1:T(8,128)(2,1)S(1)} fusion(bf16[16,512,512]{2,1,0:T(8,128)(2,1)} %convolution_convert_fusion, s32[16]{0:T(128)S(1)} %bitcast.94, pred[16]{0:T(512)(128)(4,1)S(1)} %compare_bitcast_fusion), kind=kOutput, calls=%fused_computation.10 | convolution fusion | flops 69206528 | bytes 12582992 | tf_op jit(solution)/shard_map/mb,mrw->brw/dot_general | solution.py:67
  372.4 3.5 copy.26
  375.9 0.7 copy.33
  (31 shorter events, 3.4 us)
Async XLA Ops:
  7.2 75.3 %all-gather.10.cloned.1.call-start = ((), (), s32[]{:S(2)}) async-start(), calls=%async_computation.7 | async-start | bytes 4456448 | tf_op jit(solution)/shard_map/all_gather | solution.py:24
  27.9 135.2 %reduce-scatter.3.cloned.1.call-start = ((), (), s32[]{:S(2)}) async-start(), calls=%async_computation.4 | async-start | bytes 8912896 | tf_op jit(solution)/shard_map/reduce_scatter | solution.py:28
  28.6 6.9 %copy-start.1 = (s32[16,1]{0,1:T(1,128)S(1)}, s32[16,1]{0,1:T(1,128)}, u32[]{:S(2)}) copy-start(s32[16,1]{0,1:T(1,128)} %param.7) | copy-start | bytes 196
  92.6 0.9 copy-start
  92.6 1.2 copy-start.2
  92.6 163.7 %all-gather.8.cloned.1.call-start = ((), (), s32[]{:S(2)}) async-start(), calls=%async_computation.5 | async-start | bytes 4456448 | tf_op jit(solution)/shard_map/all_gather | solution.py:58
  216.2 139.2 %reduce-scatter.5.cloned.1.call-start = ((), (), s32[]{:S(2)}) async-start(), calls=%async_computation.6 | async-start | bytes 8912896 | tf_op jit(solution)/shard_map/reduce_scatter | solution.py:71
  357.1 18.8 %all-to-all-start.1 = ((bf16[16,16,512]{2,1,0:T(8,128)(2,1)}), bf16[16,16,512]{2,1,0:T(8,128)(2,1)S(1)}, u32[]{:S(2)}, u32[]{:S(2)}) async-start(bf16[16,16,512]{2,1,0:T(8,128)(2,1)} %convert_element_type.29), calls=%async_computation.3 | async-start | bytes 524288 | tf_op jit(solution)/shard_map/all_to_all | solution.py:72
Sparse Core Ops, SparseCore 0:
  28.0 54.4 all-gather.9
  92.8 70.2 reduce-scatter.2
  216.3 39.9 all-gather.7
  266.7 88.5 reduce-scatter.4

commit v3 on v2

v3 whole, which is shorter than its diff:
```python
import jax
import jax.numpy as jnp
from jax import lax
from jax.sharding import Mesh, PartitionSpec as P

neg_fill = -1e30


def local(hidden, head, block_id, block_live, teacher):
    z_at = lax.axis_index("z")
    core_at = lax.axis_index("core")
    n_z = lax.axis_size("z")
    n_core = lax.axis_size("core")
    my_replica = z_at * n_core + core_at
    odd = core_at == 1
    tok_local = hidden.shape[1]
    model_width = hidden.shape[2]
    block_rows = teacher.shape[2]
    col_width = head.shape[1]
    blocks = head.shape[0] // block_rows
    table = head.reshape(blocks, block_rows, col_width)
    block_ids = block_id[:, 0]
    live_flags = block_live[:, 0]
    swap = [(0, 1), (1, 0)]

    ids_by = block_ids.reshape(n_z, n_core)
    own_ids = lax.dynamic_index_in_dim(ids_by, core_at, 1, keepdims=False)
    sib_ids = lax.dynamic_index_in_dim(ids_by, 1 - core_at, 1, keepdims=False)

    pieces = hidden[0].reshape(tok_local, n_z, n_core, col_width)
    pieces = jnp.where(odd, pieces[:, :, ::-1, :], pieces)
    pieces = pieces.reshape(1, tok_local, n_z, n_core * col_width)
    pieces = lax.all_to_all(pieces, "z", split_axis=2, concat_axis=0, tiled=True)
    hid_w = lax.all_gather(pieces, "section", axis=1, tiled=True).reshape(n_z, -1, n_core * col_width)
    hid_own = hid_w[:, :, :col_width]
    hid_sib = hid_w[:, :, col_width:]

    own_rows = jnp.take(table, own_ids, axis=0)
    sib_rows = lax.ppermute(jnp.take(table, sib_ids, axis=0), "core", swap)

    own_live = lax.dynamic_index_in_dim(live_flags, my_replica, 0, keepdims=False) > 0
    teach = teacher[0].astype(jnp.float32)
    live_value = jnp.where(own_live, 1.0, 0.0).astype(jnp.float32)

    def local_stats(values):
        top = jnp.where(own_live, jnp.max(values, axis=1), neg_fill)
        total = jnp.where(own_live, jnp.sum(jnp.exp(values - top[:, None]), axis=1), 0.0)
        return top, total

    def merged(tops, totals):
        top = jnp.max(tops, axis=0)
        return top, jnp.sum(totals * jnp.exp(tops - top[None, :]), axis=0)

    teach_top_s, teach_sum_s = local_stats(teach)
    live_row = jnp.broadcast_to(live_value, teach_top_s.shape)
    teach_all = lax.all_gather(jnp.stack([teach_top_s, teach_sum_s, live_row]), "section")
    teach_all, hid_own, hid_sib = lax.optimization_barrier((teach_all, hid_own, hid_sib))
    teach_top, teach_total = merged(teach_all[:, 0], teach_all[:, 1])
    live_count = jnp.sum(teach_all[:, 2, 0])

    part = jnp.einsum("mtw,mrw->mtr", hid_own, own_rows, preferred_element_type=jnp.float32)
    part = part + jnp.einsum("mtw,mrw->mtr", hid_sib, sib_rows, preferred_element_type=jnp.float32)
    logits = lax.psum_scatter(part, "z", scatter_dimension=0, tiled=True)[0]

    stud_top_s, stud_sum_s = local_stats(logits)
    stud_all = lax.all_gather(jnp.stack([stud_top_s, stud_sum_s]), "section")
    stud_top, stud_total = merged(stud_all[:, 0], stud_all[:, 1])

    student = jnp.where(own_live, jnp.exp(logits - stud_top[:, None]) / stud_total[:, None], 0.0)
    teach_prob = jnp.where(
        own_live, jnp.exp(teach - teach_top[:, None]) / teach_total[:, None], 0.0
    )
    logit_grad = (block_rows * live_count * (student - teach_prob)).astype(jnp.bfloat16)
    grads = lax.all_gather(logit_grad[None], "z", axis=0, tiled=True)

    ghid = jnp.concatenate(
        [
            jnp.einsum("mtr,mrw->mtw", grads, own_rows, preferred_element_type=jnp.float32),
            jnp.einsum("mtr,mrw->mtw", grads, sib_rows, preferred_element_type=jnp.float32),
        ],
        axis=2,
    )
    ghid = lax.psum_scatter(ghid, "section", scatter_dimension=1, tiled=True).astype(jnp.bfloat16)
    ghid = lax.all_to_all(ghid[:, :, None], "z", split_axis=0, concat_axis=2, tiled=True)
    ghid = ghid.reshape(tok_local, n_z, n_core, col_width)
    ghid = jnp.where(odd, ghid[:, :, ::-1, :], ghid)
    grad_hidden = ghid.reshape(1, tok_local, model_width)

    contrib_own = jnp.einsum(
        "mtr,mtw->mrw", grads, hid_own, preferred_element_type=jnp.float32
    ).astype(jnp.bfloat16)
    contrib_sib = jnp.einsum(
        "mtr,mtw->mrw", grads, hid_sib, preferred_element_type=jnp.float32
    ).astype(jnp.bfloat16)
    contrib_got = lax.ppermute(contrib_sib, "core", swap)
    block_range = jnp.arange(blocks, dtype=jnp.int32)[None, :]
    selector = jnp.where(
        (live_flags[:, None] > 0) & (block_ids[:, None] == block_range), 1.0, 0.0
    ).astype(jnp.bfloat16)
    sel_by = selector.reshape(n_z, n_core, blocks)
    sel_own = lax.dynamic_index_in_dim(sel_by, core_at, 1, keepdims=False)
    sel_sib = lax.dynamic_index_in_dim(sel_by, 1 - core_at, 1, keepdims=False)
    grad_head = jnp.einsum("mb,mrw->brw", sel_own, contrib_own, preferred_element_type=jnp.float32)
    grad_head = grad_head + jnp.einsum(
        "mb,mrw->brw", sel_sib, contrib_got, preferred_element_type=jnp.float32
    )
    grad_head = grad_head.astype(jnp.bfloat16).reshape(blocks * block_rows, col_width)
    return (grad_hidden, grad_head)


def solution(mesh):
    n_section, n_dp = mesh.devices.shape
    chips = Mesh(mesh.devices.reshape(n_section, n_dp // 2, 2), ("section", "z", "core"))
    dp = ("z", "core")
    placed = (
        P(dp, "section", None),
        P("section", dp),
        P(None, "section"),
        P(None, "section"),
        P(dp, None, "section"),
    )
    return jax.shard_map(
        local,
        mesh=chips,
        in_specs=placed,
        out_specs=(P(dp, "section", None), P("section", dp)),
        check_vma=False,
    )
```

time: 385 us -> 348 us (0.904)
  waiting for transfers between devices: 235 us -> 178 us
  other arithmetic: 10.3 us -> 22.1 us
  local copies, waits for them, and re-layouts: 14 us -> 23.8 us
  matrix products: 37.7 us -> 33.7 us
    all_gather x1, waiting for transfers between devices: 46.9 us -> 9.14 us  [local(): lax.all_gather(pieces, 'section', axis=1, tiled=True)]
    reduce_scatter x1, waiting for transfers between devices: 67.9 us -> 53.8 us  [local(): logits = lax.psum_scatter(part, 'z', scatter_dimension=0, tiled=True)[0]]
    concatenate x0 -> x1, other arithmetic: none -> 4.47 us  [local(): jnp.concatenate([jnp.einsum('mtr,mrw->mtw', grads, own_rows, preferred_el...]
    select_n x1 -> x5, other arithmetic: 0.66 us -> 5.08 us  [the longest x2 4.77 us: local(): sib_rows = lax.ppermute(jnp.take(table, sib_ids, axis=0), 'core', swap)]
    dot_general x4 -> x8, matrix products: 37.7 us -> 33.7 us  [the longest x1 6.44 us: local(): jnp.einsum('mb,mrw->brw', sel_sib, contrib_got, preferred_element_type=jn...]
    gather x1 -> x2, local copies, waits for them, and re-layouts: 6.93 us -> 10.1 us  [the longest x1 5.07 us: local(): own_rows = jnp.take(table, own_ids, axis=0)]
  transfers between devices with their start and end apart: 5 -> 7, of which waited for: 4 -> 5; matrix products, arithmetic and copies ran while one was open for 8% -> 14% of each run, Pallas kernels for 0% -> 0%
where the time goes in v3:
time: 348 us; the launch traced here: 347 us
  waiting for transfers between devices  178 us (51%)
  blocking collectives  67.1 us (19%)
  matrix products  33.7 us (10%)
  local copies, waits for them, and re-layouts  23.8 us (7%)
  other arithmetic  22.1 us (6%)
  between operations  15.3 us (4%)
  starting transfers between devices  7.25 us (2%)
    reduce_scatter x1, waiting for transfers between devices, local(): lax.psum_scatter(ghid, 'section', scatter_dimension=1, tiled=True)  76 us
    reduce_scatter x1, waiting for transfers between devices, local(): logits = lax.psum_scatter(part, 'z', scatter_dimension=0, tiled=True)[0]  53.8 us
    all_gather x1, waiting for transfers between devices, local(): grads = lax.all_gather(logit_grad[None], 'z', axis=0, tiled=True)  38.3 us
    all_gather x1, blocking collectives, local(): lax.all_gather(jnp.stack([teach_top_s, teach_sum_s, live_row]), 'section')  23.9 us
    all_gather x1, blocking collectives, local(): stud_all = lax.all_gather(jnp.stack([stud_top_s, stud_sum_s]), 'section')  23 us
    all_to_all x1, blocking collectives, local(): lax.all_to_all(pieces, 'z', split_axis=2, concat_axis=0, tiled=True)  20.2 us
    all_gather x1, waiting for transfers between devices, local(): lax.all_gather(pieces, 'section', axis=1, tiled=True)  9.14 us
    all_to_all x1, starting transfers between devices, local(): lax.all_to_all(ghid[:, :, None], 'z', split_axis=0, concat_axis=2, tiled=...  7.08 us
  transfers between devices with their start and end apart: 7, of which 5 were waited for; matrix products, arithmetic and copies ran while one was open for 14% of the time, Pallas kernels for 0%

profile of v3, /device:TPU:2, one launch (start us, length us, event | category | flops | bytes accessed | tf_op | source)
XLA Modules:
  0.0 347.3 jit_solution(6730358039042658439)
XLA Ops:
  10.4 20.2 %all_to_all.33 = bf16[1,16,8,1024]{3,1,0,2:T(8,128)(2,1)} all-to-all(bf16[1,16,8,1024]{3,1,0,2:T(8,128)(2,1)S(1)} %reshape.125), channel_id=1, replica_groups=mesh['section'=16,'z'=8,'core'=2] {'z'}, dimensions={2} | all-to-all | bytes 524288 | tf_op jit(solution)/shard_map/all_to_all | solution.py:33
  32.9 5.0 %gather_fusion.1 = bf16[8,512,512]{2,1,0:T(8,128)(2,1)} fusion(bf16[8,512,512]{2,1,0:T(8,128)(2,1)} %bitcast.89, s32[1024]{0:T(1024)S(1)} %pad_clamp_fusion), kind=kCustom, calls=%fused_computation.1.clone | custom fusion | bytes 8388640 | tf_op jit(solution)/shard_map/jit(_take)/gather | solution.py:39
  37.9 4.8 %broadcast_select_fusion = bf16[8,512,512]{2,1,0:T(8,128)(2,1)} fusion(bf16[8,512,512]{2,1,0:T(8,128)(2,1)} %gather_fusion.1, pred[8]{0:T(512)(128)(4,1)S(1)} %compare_and_fusion), kind=kLoop, calls=%fused_computation.8 | loop fusion | flops 2097152 | bytes 8388616 | tf_op jit(solution)/shard_map/jit(_take)/select_n | solution.py:39
  42.7 5.1 %gather_fusion = bf16[8,512,512]{2,1,0:T(8,128)(2,1)} fusion(bf16[8,512,512]{2,1,0:T(8,128)(2,1)} %bitcast.90, s32[1024]{0:T(1024)S(1)} %pad_clamp_fusion.1), kind=kCustom, calls=%fused_computation.clone | custom fusion | bytes 8388640 | tf_op jit(solution)/shard_map/jit(_take)/gather | solution.py:38
  50.8 23.9 %all-gather.3 = f32[16,3,256]{2,1,0:T(4,128)S(1)} all-gather(f32[1,3,256]{2,1,0:T(4,128)S(1)} %maximum_bitcast_fusion), channel_id=2, replica_groups=mesh['section'=16,'z'=8,'core'=2] {'section'}, dimensions={0}, use_global_device_ids=true | all-gather | bytes 52224 | tf_op jit(solution)/shard_map/all_gather | solution.py:56
  74.6 9.1 %all-gather.10.cloned.1.call-done = bf16[8,1,256,1,1024]{4,2,0,3,1:T(8,128)(2,1)} async-done(((bf16[8,1,16,1,1024]{4,2,0,3,1:T(8,128)(2,1)}), bf16[8,1,256,1,1024]{4,2,0,3,1:T(8,128)(2,1)}) %all-gather.10.cloned.1.call-update) | async-done | bytes 4194320 | tf_op jit(solution)/shard_map/all_gather | solution.py:34
  83.8 2.7 fusion.33
  88.6 5.6 %convolution_add_fusion = f32[8,256,512]{2,1,0:T(8,128)} fusion(f32[8,256,512]{2,1,0:T(8,128)S(1)} %fusion.7, bf16[8,256,512]{2,1,0:T(8,128)(2,1)S(1)} %get-tuple-element.8, bf16[8,512,512]{2,1,0:T(8,128)(2,1)} %collective-permute-done), kind=kOutput, calls=%fused_computation.12 | convolution fusion | flops 1074790400 | bytes 14680064 | tf_op jit(solution)/shard_map/mtw,mrw->mtr/dot_general | solution.py:62
  95.7 53.8 %reduce-scatter.3.cloned.1.call-done = f32[1,256,512]{2,1,0:T(8,128)} async-done(((f32[8,256,512]{2,1,0:T(8,128)}), f32[1,256,512]{2,1,0:T(8,128)}) %reduce-scatter.3.cloned.1.call-update) | async-done | bytes 524304 | tf_op jit(solution)/shard_map/reduce_scatter | solution.py:63
  153.2 23.0 %all-gather.4 = f32[16,2,256]{2,1,0:T(2,128)S(1)} all-gather(f32[1,2,256]{2,1,0:T(2,128)S(1)} %maximum_bitcast_fusion.1), channel_id=4, replica_groups=mesh['section'=16,'z'=8,'core'=2] {'section'}, dimensions={0}, use_global_device_ids=true | all-gather | bytes 34816 | tf_op jit(solution)/shard_map/all_gather | solution.py:66
  176.3 2.7 fusion.18
  179.0 38.3 %all-gather.8.cloned.1.call-done = bf16[8,256,512]{2,1,0:T(8,128)(2,1)} async-done(((bf16[1,256,512]{2,1,0:T(8,128)(2,1)}), bf16[8,256,512]{2,1,0:T(8,128)(2,1)}) %all-gather.8.cloned.1.call-update) | async-done | bytes 2097168 | tf_op jit(solution)/shard_map/all_gather | solution.py:74
  217.3 4.3 %fusion.6 = f32[8,256,512]{2,1,0:T(8,128)S(1)} fusion(bf16[8,256,512]{2,1,0:T(8,128)(2,1)} %all-gather.8.cloned.1.call-done, bf16[8,512,512]{2,1,0:T(8,128)(2,1)} %gather_fusion, pred[8]{0:T(512)(128)(4,1)S(1)} %compare_and_fusion.1), kind=kOutput, calls=%fused_computation.13 | convolution fusion | flops 1075838976 | bytes 10485768 | tf_op jit(solution)/shard_map/mtr,mrw->mtw/dot_general | solution.py:78
  221.6 3.4 fusion.35
  225.0 4.5 %pad_maximum_fusion = f32[8,256,1024]{2,1,0:T(8,128)} fusion(f32[8,256,512]{2,1,0:T(8,128)S(1)} %fusion.35, f32[8,256,512]{2,1,0:T(8,128)S(1)} %fusion.6), kind=kLoop, calls=%fused_computation.2 | loop fusion | flops 2097152 | bytes 16777216 | tf_op jit(solution)/shard_map/concatenate | solution.py:76
  229.5 4.9 %convolution_convert_fusion = bf16[8,512,512]{2,1,0:T(8,128)(2,1)} fusion(bf16[8,256,512]{2,1,0:T(8,128)(2,1)S(1)} %copy-done, bf16[8,256,512]{2,1,0:T(8,128)(2,1)} %copy-done.1), kind=kOutput, calls=%fused_computation.10 | convolution fusion | flops 1075838976 | bytes 8388608 | tf_op jit(solution)/shard_map/mtr,mtw->mrw/dot_general | solution.py:92
  234.8 2.9 convolution_convert_fusion.1
  237.7 4.8 %fusion.2 = f32[8,512,512]{2,0,1:T(8,128)} fusion(bf16[8,512,512]{2,1,0:T(8,128)(2,1)S(1)} %convolution_convert_fusion.1, bf16[8,2,8]{2,0,1:T(8,128)(2,1)S(1)} %select_convert_fusion, s32[]{:T(128)S(6)} %select_n.134), kind=kOutput, calls=%fused_computation.6 | convolution fusion | flops 33554432 | bytes 12584964 | tf_op jit(solution)/shard_map/mb,mrw->brw/dot_general | solution.py:103
  242.5 76.0 %reduce-scatter.5.cloned.1.call-done = f32[8,16,1024]{2,1,0:T(8,128)} async-done(((f32[8,256,1024]{2,1,0:T(8,128)}), f32[8,16,1024]{2,1,0:T(8,128)}) %reduce-scatter.5.cloned.1.call-update) | async-done | bytes 524304 | tf_op jit(solution)/shard_map/reduce_scatter | solution.py:83
  318.5 1.8 convert_bitcast_fusion.1
  320.3 7.1 %all-to-all-start.1 = ((bf16[8,16,1,1024]{3,1,2,0:T(8,128)(2,1)}), bf16[8,16,1,1024]{3,1,2,0:T(8,128)(2,1)S(1)}, u32[]{:S(2)}, u32[]{:S(2)}) async-start(bf16[8,16,1,1024]{3,1,2,0:T(8,128)(2,1)} %convert_bitcast_fusion.1), calls=%async_computation.3 | async-start | bytes 524288 | tf_op jit(solution)/shard_map/all_to_all | solution.py:84
  327.4 6.4 %add_convert_fusion = bf16[8,512,512]{2,0,1:T(8,128)(2,1)S(1)} fusion(f32[8,512,512]{2,0,1:T(8,128)} %fusion.2, bf16[8,512,512]{2,1,0:T(8,128)(2,1)} %collective-permute-done.1, bf16[8,2,8]{2,0,1:T(8,128)(2,1)S(1)} %select_convert_fusion, s32[]{:T(128)S(6)} %select_n.135), kind=kOutput, calls=%fused_computation.3 | convolution fusion | flops 37748736 | bytes 16779268 | tf_op jit(solution)/shard_map/mb,mrw->brw/dot_general | solution.py:104
  333.8 3.5 copy.40
  338.2 1.4 rev.7
  (69 shorter events, 17.0 us)
Async XLA Ops:
  7.2 76.6 %all-gather.10.cloned.1.call-start = ((), (), s32[]{:S(2)}) async-start(), calls=%async_computation.7 | async-start | bytes 4456448 | tf_op jit(solution)/shard_map/all_gather | solution.py:34
  30.7 118.8 %reduce-scatter.3.cloned.1.call-start = ((), (), s32[]{:S(2)}) async-start(), calls=%async_computation.4 | async-start | bytes 4718592 | tf_op jit(solution)/shard_map/reduce_scatter | solution.py:63
  42.7 45.9 %collective-permute-start = (bf16[8,512,512]{2,1,0:T(8,128)(2,1)}, bf16[8,512,512]{2,1,0:T(8,128)(2,1)}, u32[]{:S(2)}, u32[]{:S(2)}) collective-permute-start(bf16[8,512,512]{2,1,0:T(8,128)(2,1)} %broadcast_select_fusion), channel_id=1, source_target_pairs={{0,1},{1,0},{2,3},{3,2},{4,5},{5,4},{6,7},{7,6},{8,9},{9,8},{10,11... | collective-permute-start | bytes 12582920 | tf_op jit(solution)/shard_map/ppermute | solution.py:39
  42.7 5.1 %copy-start.5 = (s32[16,1]{0,1:T(1,128)S(1)}, s32[16,1]{0,1:T(1,128)}, u32[]{:S(2)}) copy-start(s32[16,1]{0,1:T(1,128)} %param.10) | copy-start | bytes 196
  42.7 6.4 %copy-start.4 = (bf16[1,256,512]{2,1,0:T(8,128)(2,1)S(1)}, bf16[1,256,512]{2,1,0:T(8,128)(2,1)}, u32[]{:S(2)}) copy-start(bf16[1,256,512]{2,1,0:T(8,128)(2,1)} %param.11) | copy-start | bytes 786436
  83.8 3.4 copy-start.3
  86.5 2.2 copy-start.2
  86.5 2.2 copy-start.1
  94.2 123.1 %all-gather.8.cloned.1.call-start = ((), (), s32[]{:S(2)}) async-start(), calls=%async_computation.5 | async-start | bytes 2359296 | tf_op jit(solution)/shard_map/all_gather | solution.py:74
  179.0 139.6 %reduce-scatter.5.cloned.1.call-start = ((), (), s32[]{:S(2)}) async-start(), calls=%async_computation.6 | async-start | bytes 8912896 | tf_op jit(solution)/shard_map/reduce_scatter | solution.py:83
  217.3 4.3 %copy-start = (bf16[8,256,512]{2,1,0:T(8,128)(2,1)S(1)}, bf16[8,256,512]{2,1,0:T(8,128)(2,1)}, u32[]{:S(2)}) copy-start(bf16[8,256,512]{2,1,0:T(8,128)(2,1)} %all-gather.8.cloned.1.call-done) | copy-start | bytes 6291460
  234.4 92.9 %collective-permute-start.1 = (bf16[8,512,512]{2,1,0:T(8,128)(2,1)}, bf16[8,512,512]{2,1,0:T(8,128)(2,1)}, u32[]{:S(2)}, u32[]{:S(2)}) collective-permute-start(bf16[8,512,512]{2,1,0:T(8,128)(2,1)} %convolution_convert_fusion), channel_id=1, source_target_pairs={{0,1},{1,0},{2,3},{3,2},{4,5},{5,4},{6,7},{7,6},{8,9},{9,8},{10,11... | collective-permute-start | bytes 12582920 | tf_op jit(solution)/shard_map/ppermute | solution.py:95
  320.3 17.8 %all-to-all-start.1 = ((bf16[8,16,1,1024]{3,1,2,0:T(8,128)(2,1)}), bf16[8,16,1,1024]{3,1,2,0:T(8,128)(2,1)S(1)}, u32[]{:S(2)}, u32[]{:S(2)}) async-start(bf16[8,16,1,1024]{3,1,2,0:T(8,128)(2,1)} %convert_bitcast_fusion.1), calls=%async_computation.3 | async-start | bytes 524288 | tf_op jit(solution)/shard_map/all_to_all | solution.py:84
Sparse Core Ops, SparseCore 0:
  30.8 52.9 all-gather.9
  94.4 55.0 reduce-scatter.2
  179.1 38.1 all-gather.7
  229.7 88.8 reduce-scatter.4

commit v4 on v3

--- a/solution.py
+++ b/solution.py
@@ -32,11 +32,10 @@
     pieces = pieces.reshape(1, tok_local, n_z, n_core * col_width)
     pieces = lax.all_to_all(pieces, "z", split_axis=2, concat_axis=0, tiled=True)
     hid_w = lax.all_gather(pieces, "section", axis=1, tiled=True).reshape(n_z, -1, n_core * col_width)
-    hid_own = hid_w[:, :, :col_width]
-    hid_sib = hid_w[:, :, col_width:]
 
     own_rows = jnp.take(table, own_ids, axis=0)
     sib_rows = lax.ppermute(jnp.take(table, sib_ids, axis=0), "core", swap)
+    rows = jnp.concatenate([own_rows, sib_rows], axis=2)
 
     own_live = lax.dynamic_index_in_dim(live_flags, my_replica, 0, keepdims=False) > 0
     teach = teacher[0].astype(jnp.float32)
@@ -54,12 +53,11 @@
     teach_top_s, teach_sum_s = local_stats(teach)
     live_row = jnp.broadcast_to(live_value, teach_top_s.shape)
     teach_all = lax.all_gather(jnp.stack([teach_top_s, teach_sum_s, live_row]), "section")
-    teach_all, hid_own, hid_sib = lax.optimization_barrier((teach_all, hid_own, hid_sib))
+    teach_all, hid_w = lax.optimization_barrier((teach_all, hid_w))
     teach_top, teach_total = merged(teach_all[:, 0], teach_all[:, 1])
     live_count = jnp.sum(teach_all[:, 2, 0])
 
-    part = jnp.einsum("mtw,mrw->mtr", hid_own, own_rows, preferred_element_type=jnp.float32)
-    part = part + jnp.einsum("mtw,mrw->mtr", hid_sib, sib_rows, preferred_element_type=jnp.float32)
+    part = jnp.einsum("mtw,mrw->mtr", hid_w, rows, preferred_element_type=jnp.float32)
     logits = lax.psum_scatter(part, "z", scatter_dimension=0, tiled=True)[0]
 
     stud_top_s, stud_sum_s = local_stats(logits)
@@ -73,26 +71,22 @@
     logit_grad = (block_rows * live_count * (student - teach_prob)).astype(jnp.bfloat16)
     grads = lax.all_gather(logit_grad[None], "z", axis=0, tiled=True)
 
-    ghid = jnp.concatenate(
-        [
-            jnp.einsum("mtr,mrw->mtw", grads, own_rows, preferred_element_type=jnp.float32),
-            jnp.einsum("mtr,mrw->mtw", grads, sib_rows, preferred_element_type=jnp.float32),
-        ],
-        axis=2,
-    )
+    contrib_sib = jnp.einsum(
+        "mtr,mtw->mrw", grads, hid_w[:, :, col_width:], preferred_element_type=jnp.float32
+    ).astype(jnp.bfloat16)
+    contrib_got = lax.ppermute(contrib_sib, "core", swap)
+    contrib_own = jnp.einsum(
+        "mtr,mtw->mrw", grads, hid_w[:, :, :col_width], preferred_element_type=jnp.float32
+    ).astype(jnp.bfloat16)
+
+    ghid = jnp.einsum("mtr,mrw->mtw", grads, rows, preferred_element_type=jnp.float32)
+    ghid, contrib_got = lax.optimization_barrier((ghid, contrib_got))
     ghid = lax.psum_scatter(ghid, "section", scatter_dimension=1, tiled=True).astype(jnp.bfloat16)
     ghid = lax.all_to_all(ghid[:, :, None], "z", split_axis=0, concat_axis=2, tiled=True)
     ghid = ghid.reshape(tok_local, n_z, n_core, col_width)
     ghid = jnp.where(odd, ghid[:, :, ::-1, :], ghid)
     grad_hidden = ghid.reshape(1, tok_local, model_width)
 
-    contrib_own = jnp.einsum(
-        "mtr,mtw->mrw", grads, hid_own, preferred_element_type=jnp.float32
-    ).astype(jnp.bfloat16)
-    contrib_sib = jnp.einsum(
-        "mtr,mtw->mrw", grads, hid_sib, preferred_element_type=jnp.float32
-    ).astype(jnp.bfloat16)
-    contrib_got = lax.ppermute(contrib_sib, "core", swap)
     block_range = jnp.arange(blocks, dtype=jnp.int32)[None, :]
     selector = jnp.where(
         (live_flags[:, None] > 0) & (block_ids[:, None] == block_range), 1.0, 0.0

time: 348 us -> 348 us (level)
  local copies, waits for them, and re-layouts: 23.8 us -> 20.3 us
    reduce_scatter x1, waiting for transfers between devices: 76 us -> 80.9 us  [local(): lax.psum_scatter(ghid, 'section', scatter_dimension=1, tiled=True)]
    select_n x1 -> x2, other arithmetic: 0.01 us -> 4.65 us  [local(): own_rows = jnp.take(table, own_ids, axis=0)]
    concatenate x1 -> x0, other arithmetic: 4.47 us -> none  [local(): jnp.concatenate([jnp.einsum('mtr,mrw->mtw', grads, own_rows, preferred_el...]
    all_gather x1, waiting for transfers between devices: 9.14 us -> 4.81 us  [local(): lax.all_gather(pieces, 'section', axis=1, tiled=True)]
    dot_general x6 -> x4, matrix products: 22.5 us -> 25.4 us  [the longest x1 9.04 us: local(): jnp.einsum('mtw,mrw->mtr', hid_w, rows, preferred_element_type=jnp.float32)]
where the time goes in v4:
time: 348 us; the launch traced here: 347 us
  waiting for transfers between devices  179 us (51%)
  blocking collectives  67.1 us (19%)
  matrix products  36.6 us (11%)
  other arithmetic  22 us (6%)
  local copies, waits for them, and re-layouts  20.3 us (6%)
  between operations  15.2 us (4%)
  starting transfers between devices  7.31 us (2%)
    reduce_scatter x1, waiting for transfers between devices, local(): lax.psum_scatter(ghid, 'section', scatter_dimension=1, tiled=True)  80.9 us
    reduce_scatter x1, waiting for transfers between devices, local(): logits = lax.psum_scatter(part, 'z', scatter_dimension=0, tiled=True)[0]  53.9 us
    all_gather x1, waiting for transfers between devices, local(): grads = lax.all_gather(logit_grad[None], 'z', axis=0, tiled=True)  38.3 us
    all_gather x1, blocking collectives, local(): lax.all_gather(jnp.stack([teach_top_s, teach_sum_s, live_row]), 'section')  23.8 us
    all_gather x1, blocking collectives, local(): stud_all = lax.all_gather(jnp.stack([stud_top_s, stud_sum_s]), 'section')  23 us
    all_to_all x1, blocking collectives, local(): lax.all_to_all(pieces, 'z', split_axis=2, concat_axis=0, tiled=True)  20.2 us
    dot_general x1, matrix products, local(): jnp.einsum('mtw,mrw->mtr', hid_w, rows, preferred_element_type=jnp.float32)  9.04 us
    dot_general x1, matrix products, local(): jnp.einsum('mtr,mrw->mtw', grads, rows, preferred_element_type=jnp.float32)  7.78 us
  transfers between devices with their start and end apart: 7, of which 5 were waited for; matrix products, arithmetic and copies ran while one was open for 14% of the time, Pallas kernels for 0%

profile of v4, /device:TPU:2, one launch (start us, length us, event | category | flops | bytes accessed | tf_op | source)
XLA Modules:
  0.0 347.0 jit_solution(6837242374498389123)
XLA Ops:
  8.6 1.4 rev.6
  10.4 20.2 %all_to_all.33 = bf16[1,16,8,1024]{3,1,0,2:T(8,128)(2,1)} all-to-all(bf16[1,16,8,1024]{3,1,0,2:T(8,128)(2,1)S(1)} %reshape.125), channel_id=1, replica_groups=mesh['section'=16,'z'=8,'core'=2] {'z'}, dimensions={2} | all-to-all | bytes 524288 | tf_op jit(solution)/shard_map/all_to_all | solution.py:33
  31.3 1.3 reduce.17
  32.9 5.0 %gather_fusion.1 = bf16[8,512,512]{2,1,0:T(8,128)(2,1)} fusion(bf16[8,512,512]{2,1,0:T(8,128)(2,1)} %bitcast.83, s32[1024]{0:T(1024)S(1)} %pad_clamp_fusion), kind=kCustom, calls=%fused_computation.1.clone | custom fusion | bytes 8388640 | tf_op jit(solution)/shard_map/jit(_take)/gather | solution.py:37
  37.9 4.8 %broadcast_select_fusion = bf16[8,512,512]{2,1,0:T(8,128)(2,1)} fusion(bf16[8,512,512]{2,1,0:T(8,128)(2,1)} %gather_fusion.1, pred[8]{0:T(512)(128)(4,1)S(1)} %compare_and_fusion), kind=kLoop, calls=%fused_computation.10 | loop fusion | flops 2097152 | bytes 8388616 | tf_op jit(solution)/shard_map/jit(_take)/select_n | solution.py:37
  42.8 5.0 %gather_fusion = bf16[8,512,512]{2,1,0:T(8,128)(2,1)} fusion(bf16[8,512,512]{2,1,0:T(8,128)(2,1)} %bitcast.84, s32[1024]{0:T(1024)S(1)} %pad_clamp_fusion.1), kind=kCustom, calls=%fused_computation.clone | custom fusion | bytes 8388640 | tf_op jit(solution)/shard_map/jit(_take)/gather | solution.py:36
  50.5 23.8 %all-gather.3 = f32[16,3,256]{2,1,0:T(4,128)S(1)} all-gather(f32[1,3,256]{2,1,0:T(4,128)S(1)} %maximum_bitcast_fusion), channel_id=2, replica_groups=mesh['section'=16,'z'=8,'core'=2] {'section'}, dimensions={0}, use_global_device_ids=true | all-gather | bytes 52224 | tf_op jit(solution)/shard_map/all_gather | solution.py:55
  74.4 4.7 %broadcast_select_fusion.1 = bf16[8,512,512]{2,1,0:T(8,128)(2,1)} fusion(bf16[8,512,512]{2,1,0:T(8,128)(2,1)} %gather_fusion, pred[8]{0:T(512)(128)(4,1)S(1)} %compare_and_fusion.1), kind=kLoop, calls=%fused_computation.11 | loop fusion | flops 2097152 | bytes 8388616 | tf_op jit(solution)/shard_map/jit(_take)/select_n | solution.py:36
  79.0 4.8 %all-gather.10.cloned.1.call-done = bf16[8,1,256,1,1024]{4,2,0,3,1:T(8,128)(2,1)} async-done(((bf16[8,1,16,1,1024]{4,2,0,3,1:T(8,128)(2,1)}), bf16[8,1,256,1,1024]{4,2,0,3,1:T(8,128)(2,1)}) %all-gather.10.cloned.1.call-update) | async-done | bytes 4194320 | tf_op jit(solution)/shard_map/all_gather | solution.py:34
  83.8 9.0 %fusion.1 = f32[8,256,512]{2,1,0:T(8,128)} fusion(bf16[8,256,1024]{2,1,0:T(8,128)(2,1)} %bitcast.86, bf16[8,512,512]{2,1,0:T(8,128)(2,1)} %collective-permute-done, bf16[8,512,512]{2,1,0:T(8,128)(2,1)} %broadcast_select_fusion.1), kind=kOutput, calls=%fused_computation.5 | convolution fusion | flops 2164260864 | bytes 16777216 | tf_op jit(solution)/shard_map/mtw,mrw->mtr/dot_general | solution.py:60
  94.3 53.9 %reduce-scatter.3.cloned.1.call-done = f32[1,256,512]{2,1,0:T(8,128)} async-done(((f32[8,256,512]{2,1,0:T(8,128)}), f32[1,256,512]{2,1,0:T(8,128)}) %reduce-scatter.3.cloned.1.call-update) | async-done | bytes 524304 | tf_op jit(solution)/shard_map/reduce_scatter | solution.py:61
  151.7 23.0 %all-gather.4 = f32[16,2,256]{2,1,0:T(2,128)S(1)} all-gather(f32[1,2,256]{2,1,0:T(2,128)S(1)} %maximum_bitcast_fusion.1), channel_id=4, replica_groups=mesh['section'=16,'z'=8,'core'=2] {'section'}, dimensions={0}, use_global_device_ids=true | all-gather | bytes 34816 | tf_op jit(solution)/shard_map/all_gather | solution.py:64
  174.8 2.6 fusion.20
  177.5 38.3 %all-gather.8.cloned.1.call-done = bf16[8,256,512]{2,1,0:T(8,128)(2,1)} async-done(((bf16[1,256,512]{2,1,0:T(8,128)(2,1)}), bf16[8,256,512]{2,1,0:T(8,128)(2,1)}) %all-gather.8.cloned.1.call-update) | async-done | bytes 2097168 | tf_op jit(solution)/shard_map/all_gather | solution.py:72
  215.7 5.7 %convolution_convert_fusion.1 = bf16[8,512,512]{2,1,0:T(8,128)(2,1)} fusion(bf16[8,256,512]{2,1,0:T(8,128)(2,1)} %all-gather.8.cloned.1.call-done, bf16[8,256,1024]{2,1,0:T(8,128)(2,1)} %bitcast.87), kind=kOutput, calls=%fused_computation.13 | convolution fusion | flops 1075838976 | bytes 8388608 | tf_op jit(solution)/shard_map/mtr,mtw->mrw/dot_general | solution.py:74
  221.4 7.8 %fusion = f32[8,256,1024]{2,1,0:T(8,128)} fusion(bf16[8,256,512]{2,1,0:T(8,128)(2,1)S(1)} %copy-done, bf16[8,512,512]{2,1,0:T(8,128)(2,1)} %collective-permute-done, bf16[8,512,512]{2,1,0:T(8,128)(2,1)S(1)} %copy-done.1), kind=kOutput, calls=%fused_computation.4 | convolution fusion | flops 2164260864 | bytes 18874368 | tf_op jit(solution)/shard_map/mtr,mrw->mtw/dot_general | solution.py:82
  229.6 2.9 convolution_convert_fusion
  232.5 4.8 %fusion.4 = f32[8,512,512]{2,0,1:T(8,128)} fusion(bf16[8,512,512]{2,1,0:T(8,128)(2,1)S(1)} %convolution_convert_fusion, bf16[8,2,8]{2,0,1:T(8,128)(2,1)S(1)} %select_convert_fusion, s32[]{:T(128)S(6)} %select_n.134), kind=kOutput, calls=%fused_computation.8 | convolution fusion | flops 33554432 | bytes 12584964 | tf_op jit(solution)/shard_map/mb,mrw->brw/dot_general | solution.py:97
  237.3 80.9 %reduce-scatter.5.cloned.1.call-done = f32[8,16,1024]{2,1,0:T(8,128)} async-done(((f32[8,256,1024]{2,1,0:T(8,128)}), f32[8,16,1024]{2,1,0:T(8,128)}) %reduce-scatter.5.cloned.1.call-update) | async-done | bytes 524304 | tf_op jit(solution)/shard_map/reduce_scatter | solution.py:84
  318.1 1.8 convert_bitcast_fusion.1
  319.9 7.1 %all-to-all-start.1 = ((bf16[8,16,1,1024]{3,1,2,0:T(8,128)(2,1)}), bf16[8,16,1,1024]{3,1,2,0:T(8,128)(2,1)S(1)}, u32[]{:S(2)}, u32[]{:S(2)}) async-start(bf16[8,16,1,1024]{3,1,2,0:T(8,128)(2,1)} %convert_bitcast_fusion.1), calls=%async_computation.3 | async-start | bytes 524288 | tf_op jit(solution)/shard_map/all_to_all | solution.py:85
  327.1 6.4 %add_convert_fusion = bf16[8,512,512]{2,0,1:T(8,128)(2,1)S(1)} fusion(f32[8,512,512]{2,0,1:T(8,128)} %fusion.4, bf16[8,512,512]{2,1,0:T(8,128)(2,1)} %collective-permute-done.1, bf16[8,2,8]{2,0,1:T(8,128)(2,1)S(1)} %select_convert_fusion, s32[]{:T(128)S(6)} %select_n.135), kind=kOutput, calls=%fused_computation.3 | convolution fusion | flops 37748736 | bytes 16779268 | tf_op jit(solution)/shard_map/mb,mrw->brw/dot_general | solution.py:98
  333.5 3.5 copy.44
  337.9 1.4 rev.7
  (62 shorter events, 11.8 us)
Async XLA Ops:
  7.2 76.6 %all-gather.10.cloned.1.call-start = ((), (), s32[]{:S(2)}) async-start(), calls=%async_computation.7 | async-start | bytes 4456448 | tf_op jit(solution)/shard_map/all_gather | solution.py:34
  30.7 117.5 %reduce-scatter.3.cloned.1.call-start = ((), (), s32[]{:S(2)}) async-start(), calls=%async_computation.4 | async-start | bytes 4718592 | tf_op jit(solution)/shard_map/reduce_scatter | solution.py:61
  42.7 41.1 %collective-permute-start = (bf16[8,512,512]{2,1,0:T(8,128)(2,1)}, bf16[8,512,512]{2,1,0:T(8,128)(2,1)}, u32[]{:S(2)}, u32[]{:S(2)}) collective-permute-start(bf16[8,512,512]{2,1,0:T(8,128)(2,1)} %broadcast_select_fusion), channel_id=1, source_target_pairs={{0,1},{1,0},{2,3},{3,2},{4,5},{5,4},{6,7},{7,6},{8,9},{9,8},{10,11... | collective-permute-start | bytes 12582920 | tf_op jit(solution)/shard_map/ppermute | solution.py:37
  42.8 5.0 %copy-start.2 = (bf16[1,256,512]{2,1,0:T(8,128)(2,1)S(1)}, bf16[1,256,512]{2,1,0:T(8,128)(2,1)}, u32[]{:S(2)}) copy-start(bf16[1,256,512]{2,1,0:T(8,128)(2,1)} %param.11) | copy-start | bytes 786436
  42.8 5.1 %copy-start.3 = (s32[16,1]{0,1:T(1,128)S(1)}, s32[16,1]{0,1:T(1,128)}, u32[]{:S(2)}) copy-start(s32[16,1]{0,1:T(1,128)} %param.10) | copy-start | bytes 196
  92.9 122.9 %all-gather.8.cloned.1.call-start = ((), (), s32[]{:S(2)}) async-start(), calls=%async_computation.5 | async-start | bytes 2359296 | tf_op jit(solution)/shard_map/all_gather | solution.py:72
  177.4 140.7 %reduce-scatter.5.cloned.1.call-start = ((), (), s32[]{:S(2)}) async-start(), calls=%async_computation.6 | async-start | bytes 8912896 | tf_op jit(solution)/shard_map/reduce_scatter | solution.py:84
  215.7 5.7 %copy-start = (bf16[8,256,512]{2,1,0:T(8,128)(2,1)S(1)}, bf16[8,256,512]{2,1,0:T(8,128)(2,1)}, u32[]{:S(2)}) copy-start(bf16[8,256,512]{2,1,0:T(8,128)(2,1)} %all-gather.8.cloned.1.call-done) | copy-start | bytes 6291460
  215.7 5.7 %copy-start.1 = (bf16[8,512,512]{2,1,0:T(8,128)(2,1)S(1)}, bf16[8,512,512]{2,1,0:T(8,128)(2,1)}, u32[]{:S(2)}) copy-start(bf16[8,512,512]{2,1,0:T(8,128)(2,1)} %broadcast_select_fusion.1) | copy-start | bytes 12582916
  221.4 7.8 %collective-permute-start.1 = (bf16[8,512,512]{2,1,0:T(8,128)(2,1)}, bf16[8,512,512]{2,1,0:T(8,128)(2,1)}, u32[]{:S(2)}, u32[]{:S(2)}) collective-permute-start(bf16[8,512,512]{2,1,0:T(8,128)(2,1)} %convolution_convert_fusion.1), channel_id=1, source_target_pairs={{0,1},{1,0},{2,3},{3,2},{4,5},{5,4},{6,7},{7,6},{8,9},{9,8},{10,11... | collective-permute-start | bytes 12582920 | tf_op jit(solution)/shard_map/ppermute | solution.py:77
  319.9 17.8 %all-to-all-start.1 = ((bf16[8,16,1,1024]{3,1,2,0:T(8,128)(2,1)}), bf16[8,16,1,1024]{3,1,2,0:T(8,128)(2,1)S(1)}, u32[]{:S(2)}, u32[]{:S(2)}) async-start(bf16[8,16,1,1024]{3,1,2,0:T(8,128)(2,1)} %convert_bitcast_fusion.1), calls=%async_computation.3 | async-start | bytes 524288 | tf_op jit(solution)/shard_map/all_to_all | solution.py:85
Sparse Core Ops, SparseCore 0:
  30.8 52.9 all-gather.9
  93.0 55.0 reduce-scatter.2
  177.5 38.1 all-gather.7
  229.4 88.7 reduce-scatter.4

commit v5 on v4

--- a/solution.py
+++ b/solution.py
@@ -81,7 +81,13 @@
 
     ghid = jnp.einsum("mtr,mrw->mtw", grads, rows, preferred_element_type=jnp.float32)
     ghid, contrib_got = lax.optimization_barrier((ghid, contrib_got))
-    ghid = lax.psum_scatter(ghid, "section", scatter_dimension=1, tiled=True).astype(jnp.bfloat16)
+    half = n_z // 2
+    n_section = lax.axis_size("section")
+    summed_a = lax.psum_scatter(ghid[:half], "section", scatter_dimension=1, tiled=True)
+    spread = ghid[half:].reshape(n_z - half, n_section, tok_local, -1)
+    spread = lax.all_to_all(spread, "section", split_axis=1, concat_axis=1, tiled=True)
+    summed_b = jnp.sum(spread, axis=1)
+    ghid = jnp.concatenate([summed_a, summed_b], axis=0).astype(jnp.bfloat16)
     ghid = lax.all_to_all(ghid[:, :, None], "z", split_axis=0, concat_axis=2, tiled=True)
     ghid = ghid.reshape(tok_local, n_z, n_core, col_width)
     ghid = jnp.where(odd, ghid[:, :, ::-1, :], ghid)

time: 348 us -> 386 us (1.11)
  waiting for transfers between devices: 179 us -> 202 us
  local copies, waits for them, and re-layouts: 20.3 us -> 29.5 us
  starting transfers between devices: 7.31 us -> 14.6 us
  matrix products: 36.6 us -> 31 us
    all_to_all x0 -> x1, waiting for transfers between devices: none -> 58.3 us  [local(): lax.all_to_all(spread, 'section', split_axis=1, concat_axis=1, tiled=True)]
    reduce_scatter x1, waiting for transfers between devices: 80.9 us -> 43.9 us  [local(): lax.psum_scatter(ghid[:half], 'section', scatter_dimension=1, tiled=True)]
    all_to_all x0 -> x1, starting transfers between devices: none -> 7.27 us  [local(): lax.all_to_all(spread, 'section', split_axis=1, concat_axis=1, tiled=True)]
    reshape x0 -> x1, local copies, waits for them, and re-layouts: none -> 4.73 us  [local(): spread = ghid[half:].reshape(n_z - half, n_section, tok_local, -1)]
    slice x0 -> x1, local copies, waits for them, and re-layouts: none -> 4.2 us  [local(): ghid[:half]]
  transfers between devices with their start and end apart: 7 -> 8, of which waited for: 5 -> 7; matrix products, arithmetic and copies ran while one was open for 14% -> 14% of each run, Pallas kernels for 0% -> 0%
where the time goes in v5:
time: 386 us; the launch traced here: 385 us
  waiting for transfers between devices  202 us (52%)
  blocking collectives  67.1 us (17%)
  matrix products  31 us (8%)
  local copies, waits for them, and re-layouts  29.5 us (8%)
  other arithmetic  25 us (6%)
  between operations  15.3 us (4%)
  starting transfers between devices  14.6 us (4%)
    all_to_all x1, waiting for transfers between devices, local(): lax.all_to_all(spread, 'section', split_axis=1, concat_axis=1, tiled=True)  58.3 us
    reduce_scatter x1, waiting for transfers between devices, local(): logits = lax.psum_scatter(part, 'z', scatter_dimension=0, tiled=True)[0]  53.8 us
    reduce_scatter x1, waiting for transfers between devices, local(): lax.psum_scatter(ghid[:half], 'section', scatter_dimension=1, tiled=True)  43.9 us
    all_gather x1, waiting for transfers between devices, local(): grads = lax.all_gather(logit_grad[None], 'z', axis=0, tiled=True)  38.3 us
    all_gather x1, blocking collectives, local(): lax.all_gather(jnp.stack([teach_top_s, teach_sum_s, live_row]), 'section')  23.9 us
    all_gather x1, blocking collectives, local(): stud_all = lax.all_gather(jnp.stack([stud_top_s, stud_sum_s]), 'section')  23 us
    all_to_all x1, blocking collectives, local(): lax.all_to_all(pieces, 'z', split_axis=2, concat_axis=0, tiled=True)  20.2 us
    dot_general x1, matrix products, local(): jnp.einsum('mtw,mrw->mtr', hid_w, rows, preferred_element_type=jnp.float32)  9.04 us
  transfers between devices with their start and end apart: 8, of which 7 were waited for; matrix products, arithmetic and copies ran while one was open for 14% of the time, Pallas kernels for 0%

profile of v5, /device:TPU:2, one launch (start us, length us, event | category | flops | bytes accessed | tf_op | source)
XLA Modules:
  0.0 384.7 jit_solution(15345734471772228024)
XLA Ops:
  10.4 20.2 %all_to_all.38 = bf16[1,16,8,1024]{3,1,0,2:T(8,128)(2,1)} all-to-all(bf16[1,16,8,1024]{3,1,0,2:T(8,128)(2,1)S(1)} %reshape.159), channel_id=1, replica_groups=mesh['section'=16,'z'=8,'core'=2] {'z'}, dimensions={2} | all-to-all | bytes 524288 | tf_op jit(solution)/shard_map/all_to_all | solution.py:33
  32.9 5.0 %gather_fusion.1 = bf16[8,512,512]{2,1,0:T(8,128)(2,1)} fusion(bf16[8,512,512]{2,1,0:T(8,128)(2,1)} %bitcast.87, s32[1024]{0:T(1024)S(1)} %pad_clamp_fusion), kind=kCustom, calls=%fused_computation.1.clone | custom fusion | bytes 8388640 | tf_op jit(solution)/shard_map/jit(_take)/gather | solution.py:37
  37.9 4.8 %broadcast_select_fusion = bf16[8,512,512]{2,1,0:T(8,128)(2,1)} fusion(bf16[8,512,512]{2,1,0:T(8,128)(2,1)} %gather_fusion.1, pred[8]{0:T(512)(128)(4,1)S(1)} %compare_and_fusion), kind=kLoop, calls=%fused_computation.10 | loop fusion | flops 2097152 | bytes 8388616 | tf_op jit(solution)/shard_map/jit(_take)/select_n | solution.py:37
  42.8 5.0 %gather_fusion = bf16[8,512,512]{2,1,0:T(8,128)(2,1)} fusion(bf16[8,512,512]{2,1,0:T(8,128)(2,1)} %bitcast.88, s32[1024]{0:T(1024)S(1)} %pad_clamp_fusion.1), kind=kCustom, calls=%fused_computation.clone | custom fusion | bytes 8388640 | tf_op jit(solution)/shard_map/jit(_take)/gather | solution.py:36
  50.9 23.9 %all-gather.3 = f32[16,3,256]{2,1,0:T(4,128)S(1)} all-gather(f32[1,3,256]{2,1,0:T(4,128)S(1)} %maximum_bitcast_fusion.1), channel_id=2, replica_groups=mesh['section'=16,'z'=8,'core'=2] {'section'}, dimensions={0}, use_global_device_ids=true | all-gather | bytes 52224 | tf_op jit(solution)/shard_map/all_gather | solution.py:55
  74.7 4.7 %broadcast_select_fusion.1 = bf16[8,512,512]{2,1,0:T(8,128)(2,1)} fusion(bf16[8,512,512]{2,1,0:T(8,128)(2,1)} %gather_fusion, pred[8]{0:T(512)(128)(4,1)S(1)} %compare_and_fusion.1), kind=kLoop, calls=%fused_computation.11 | loop fusion | flops 2097152 | bytes 8388616 | tf_op jit(solution)/shard_map/jit(_take)/select_n | solution.py:36
  79.4 4.4 %all-gather.10.cloned.1.call-done = bf16[8,1,256,1,1024]{4,2,0,3,1:T(8,128)(2,1)} async-done(((bf16[8,1,16,1,1024]{4,2,0,3,1:T(8,128)(2,1)}), bf16[8,1,256,1,1024]{4,2,0,3,1:T(8,128)(2,1)}) %all-gather.10.cloned.1.call-update) | async-done | bytes 4194320 | tf_op jit(solution)/shard_map/all_gather | solution.py:34
  83.8 9.0 %fusion.1 = f32[8,256,512]{2,1,0:T(8,128)} fusion(bf16[8,256,1024]{2,1,0:T(8,128)(2,1)} %bitcast.91, bf16[8,512,512]{2,1,0:T(8,128)(2,1)} %collective-permute-done, bf16[8,512,512]{2,1,0:T(8,128)(2,1)} %broadcast_select_fusion.1), kind=kOutput, calls=%fused_computation.5 | convolution fusion | flops 2164260864 | bytes 16777216 | tf_op jit(solution)/shard_map/mtw,mrw->mtr/dot_general | solution.py:60
  94.3 53.8 %reduce-scatter.3.cloned.1.call-done = f32[1,256,512]{2,1,0:T(8,128)} async-done(((f32[8,256,512]{2,1,0:T(8,128)}), f32[1,256,512]{2,1,0:T(8,128)}) %reduce-scatter.3.cloned.1.call-update) | async-done | bytes 524304 | tf_op jit(solution)/shard_map/reduce_scatter | solution.py:61
  151.9 23.0 %all-gather.4 = f32[16,2,256]{2,1,0:T(2,128)S(1)} all-gather(f32[1,2,256]{2,1,0:T(2,128)S(1)} %maximum_bitcast_fusion.2), channel_id=4, replica_groups=mesh['section'=16,'z'=8,'core'=2] {'section'}, dimensions={0}, use_global_device_ids=true | all-gather | bytes 34816 | tf_op jit(solution)/shard_map/all_gather | solution.py:64
  177.7 38.3 %all-gather.8.cloned.1.call-done = bf16[8,256,512]{2,1,0:T(8,128)(2,1)} async-done(((bf16[1,256,512]{2,1,0:T(8,128)(2,1)}), bf16[8,256,512]{2,1,0:T(8,128)(2,1)}) %all-gather.8.cloned.1.call-update) | async-done | bytes 2097168 | tf_op jit(solution)/shard_map/all_gather | solution.py:72
  216.0 3.7 convolution_convert_fusion.1
  220.1 4.2 %fusion = f32[8,256,1024]{2,1,0:T(8,128)S(1)} fusion(bf16[8,256,512]{2,1,0:T(8,128)(2,1)S(1)} %copy-done, bf16[8,512,512]{2,1,0:T(8,128)(2,1)} %collective-permute-done, bf16[8,512,512]{2,1,0:T(8,128)(2,1)S(1)} %copy-done.1), kind=kOutput, calls=%fused_computation.4 | convolution fusion | flops 2164260864 | bytes 18874368 | tf_op jit(solution)/shard_map/mtr,mrw->mtw/dot_general | solution.py:82
  224.3 2.8 collective-permute-done.1
  227.1 4.2 %fusion.35 = (f32[4,256,1024]{2,1,0:T(8,128)}, f32[4,256,1024]{2,1,0:T(8,128)}) fusion(f32[8,256,1024]{2,1,0:T(8,128)S(1)} %fusion), kind=kLoop, calls=%fused_computation.74 | loop fusion | bytes 16777216 | tf_op jit(solution)/shard_map/slice | solution.py:86
  231.3 4.7 %copy.35 = f32[4,16,16,1024]{3,2,0,1:T(8,128)} copy(f32[4,16,16,1024]{3,2,1,0:T(8,128)} %bitcast.89) | data formatting | bytes 8388608 | tf_op jit(solution)/shard_map/reshape | solution.py:87
  236.0 7.3 %all-to-all-start.1 = ((f32[4,16,16,1024]{3,2,0,1:T(8,128)}), f32[4,16,16,1024]{3,2,0,1:T(8,128)}, u32[]{:S(2)}, u32[]{:S(2)}) async-start(f32[4,16,16,1024]{3,2,0,1:T(8,128)} %copy.35), calls=%async_computation.3 | async-start | bytes 8388608 | tf_op jit(solution)/shard_map/all_to_all | solution.py:88
  243.7 2.9 convolution_convert_fusion
  246.6 4.8 %fusion.4 = f32[8,512,512]{2,0,1:T(8,128)} fusion(bf16[8,512,512]{2,1,0:T(8,128)(2,1)S(1)} %convolution_convert_fusion, bf16[8,2,8]{2,0,1:T(8,128)(2,1)S(1)} %select_convert_fusion, s32[]{:T(128)S(6)} %select_n.134), kind=kOutput, calls=%fused_computation.8 | convolution fusion | flops 33554432 | bytes 12584964 | tf_op jit(solution)/shard_map/mb,mrw->brw/dot_general | solution.py:103
  251.4 58.3 %all-to-all-done.1 = f32[4,16,16,1024]{3,2,0,1:T(8,128)} async-done(((f32[4,16,16,1024]{3,2,0,1:T(8,128)}), f32[4,16,16,1024]{3,2,0,1:T(8,128)}, u32[]{:S(2)}, u32[]{:S(2)}) %all-to-all-start.1) | async-done | bytes 4194336 | tf_op jit(solution)/shard_map/all_to_all | solution.py:88
  312.3 43.9 %reduce-scatter.5.cloned.1.call-done = f32[4,16,1024]{2,1,0:T(8,128)} async-done(((f32[4,256,1024]{2,1,0:T(8,128)}), f32[4,16,1024]{2,1,0:T(8,128)}) %reduce-scatter.5.cloned.1.call-update) | async-done | bytes 262160 | tf_op jit(solution)/shard_map/reduce_scatter | solution.py:86
  357.9 7.0 %all-to-all-start.2 = ((bf16[8,16,1,1024]{3,1,2,0:T(8,128)(2,1)}), bf16[8,16,1,1024]{3,1,2,0:T(8,128)(2,1)S(1)}, u32[]{:S(2)}, u32[]{:S(2)}) async-start(bf16[8,16,1,1024]{3,1,2,0:T(8,128)(2,1)} %maximum_bitcast_fusion), calls=%async_computation.4 | async-start | bytes 524288 | tf_op jit(solution)/shard_map/all_to_all | solution.py:91
  364.9 6.4 %add_convert_fusion = bf16[8,512,512]{2,0,1:T(8,128)(2,1)S(1)} fusion(f32[8,512,512]{2,0,1:T(8,128)} %fusion.4, bf16[8,512,512]{2,1,0:T(8,128)(2,1)} %collective-permute-done.1, bf16[8,2,8]{2,0,1:T(8,128)(2,1)S(1)} %select_convert_fusion, s32[]{:T(128)S(6)} %select_n.135), kind=kOutput, calls=%fused_computation.3 | convolution fusion | flops 37748736 | bytes 16779268 | tf_op jit(solution)/shard_map/mb,mrw->brw/dot_general | solution.py:104
  371.4 3.5 copy.45
  (68 shorter events, 23.5 us)
Async XLA Ops:
  7.2 76.6 %all-gather.10.cloned.1.call-start = ((), (), s32[]{:S(2)}) async-start(), calls=%async_computation.8 | async-start | bytes 4456448 | tf_op jit(solution)/shard_map/all_gather | solution.py:34
  30.7 117.4 %reduce-scatter.3.cloned.1.call-start = ((), (), s32[]{:S(2)}) async-start(), calls=%async_computation.5 | async-start | bytes 4718592 | tf_op jit(solution)/shard_map/reduce_scatter | solution.py:61
  42.7 41.1 %collective-permute-start = (bf16[8,512,512]{2,1,0:T(8,128)(2,1)}, bf16[8,512,512]{2,1,0:T(8,128)(2,1)}, u32[]{:S(2)}, u32[]{:S(2)}) collective-permute-start(bf16[8,512,512]{2,1,0:T(8,128)(2,1)} %broadcast_select_fusion), channel_id=1, source_target_pairs={{0,1},{1,0},{2,3},{3,2},{4,5},{5,4},{6,7},{7,6},{8,9},{9,8},{10,11... | collective-permute-start | bytes 12582920 | tf_op jit(solution)/shard_map/ppermute | solution.py:37
  42.8 5.0 %copy-start.3 = (s32[16,1]{0,1:T(1,128)S(1)}, s32[16,1]{0,1:T(1,128)}, u32[]{:S(2)}) copy-start(s32[16,1]{0,1:T(1,128)} %param.10) | copy-start | bytes 196
  42.8 6.4 %copy-start.2 = (bf16[1,256,512]{2,1,0:T(8,128)(2,1)S(1)}, bf16[1,256,512]{2,1,0:T(8,128)(2,1)}, u32[]{:S(2)}) copy-start(bf16[1,256,512]{2,1,0:T(8,128)(2,1)} %param.11) | copy-start | bytes 786436
  92.9 123.1 %all-gather.8.cloned.1.call-start = ((), (), s32[]{:S(2)}) async-start(), calls=%async_computation.6 | async-start | bytes 2359296 | tf_op jit(solution)/shard_map/all_gather | solution.py:72
  177.7 178.5 %reduce-scatter.5.cloned.1.call-start = ((), (), s32[]{:S(2)}) async-start(), calls=%async_computation.7 | async-start | bytes 4456448 | tf_op jit(solution)/shard_map/reduce_scatter | solution.py:86
  216.0 3.8 copy-start
  216.0 4.1 %copy-start.1 = (bf16[8,512,512]{2,1,0:T(8,128)(2,1)S(1)}, bf16[8,512,512]{2,1,0:T(8,128)(2,1)}, u32[]{:S(2)}) copy-start(bf16[8,512,512]{2,1,0:T(8,128)(2,1)} %broadcast_select_fusion.1) | copy-start | bytes 12582916
  219.7 7.4 %collective-permute-start.1 = (bf16[8,512,512]{2,1,0:T(8,128)(2,1)S(1)}, bf16[8,512,512]{2,1,0:T(8,128)(2,1)}, u32[]{:S(2)}, u32[]{:S(2)}) collective-permute-start(bf16[8,512,512]{2,1,0:T(8,128)(2,1)S(1)} %convolution_convert_fusion.1), channel_id=1, source_target_pairs={{0,1},{1,0},{2,3},{3,2},{4,5},{5,4},{6,7},{7,6},{8,9},{9,8},{10,11... | collective-permute-start | bytes 12582920 | tf_op jit(solution)/shard_map/ppermute | solution.py:77
  236.0 73.7 %all-to-all-start.1 = ((f32[4,16,16,1024]{3,2,0,1:T(8,128)}), f32[4,16,16,1024]{3,2,0,1:T(8,128)}, u32[]{:S(2)}, u32[]{:S(2)}) async-start(f32[4,16,16,1024]{3,2,0,1:T(8,128)} %copy.35), calls=%async_computation.3 | async-start | bytes 8388608 | tf_op jit(solution)/shard_map/all_to_all | solution.py:88
  357.9 17.5 %all-to-all-start.2 = ((bf16[8,16,1,1024]{3,1,2,0:T(8,128)(2,1)}), bf16[8,16,1,1024]{3,1,2,0:T(8,128)(2,1)S(1)}, u32[]{:S(2)}, u32[]{:S(2)}) async-start(bf16[8,16,1,1024]{3,1,2,0:T(8,128)(2,1)} %maximum_bitcast_fusion), calls=%async_computation.4 | async-start | bytes 524288 | tf_op jit(solution)/shard_map/all_to_all | solution.py:91
Sparse Core Ops, SparseCore 0:
  30.8 52.9 all-gather.9
  93.0 55.0 reduce-scatter.2
  177.8 38.1 all-gather.7
  231.4 124.7 reduce-scatter.4

commit v6 on v4

--- a/solution.py
+++ b/solution.py
@@ -30,11 +30,13 @@
     pieces = hidden[0].reshape(tok_local, n_z, n_core, col_width)
     pieces = jnp.where(odd, pieces[:, :, ::-1, :], pieces)
     pieces = pieces.reshape(1, tok_local, n_z, n_core * col_width)
+
+    own_rows = jnp.take(table, own_ids, axis=0)
+    for_sib = jnp.take(table, sib_ids, axis=0)
+    pieces, own_rows, for_sib = lax.optimization_barrier((pieces, own_rows, for_sib))
+    sib_rows = lax.ppermute(for_sib, "core", swap)
     pieces = lax.all_to_all(pieces, "z", split_axis=2, concat_axis=0, tiled=True)
     hid_w = lax.all_gather(pieces, "section", axis=1, tiled=True).reshape(n_z, -1, n_core * col_width)
-
-    own_rows = jnp.take(table, own_ids, axis=0)
-    sib_rows = lax.ppermute(jnp.take(table, sib_ids, axis=0), "core", swap)
     rows = jnp.concatenate([own_rows, sib_rows], axis=2)
 
     own_live = lax.dynamic_index_in_dim(live_flags, my_replica, 0, keepdims=False) > 0
@@ -79,14 +81,6 @@
         "mtr,mtw->mrw", grads, hid_w[:, :, :col_width], preferred_element_type=jnp.float32
     ).astype(jnp.bfloat16)
 
-    ghid = jnp.einsum("mtr,mrw->mtw", grads, rows, preferred_element_type=jnp.float32)
-    ghid, contrib_got = lax.optimization_barrier((ghid, contrib_got))
-    ghid = lax.psum_scatter(ghid, "section", scatter_dimension=1, tiled=True).astype(jnp.bfloat16)
-    ghid = lax.all_to_all(ghid[:, :, None], "z", split_axis=0, concat_axis=2, tiled=True)
-    ghid = ghid.reshape(tok_local, n_z, n_core, col_width)
-    ghid = jnp.where(odd, ghid[:, :, ::-1, :], ghid)
-    grad_hidden = ghid.reshape(1, tok_local, model_width)
-
     block_range = jnp.arange(blocks, dtype=jnp.int32)[None, :]
     selector = jnp.where(
         (live_flags[:, None] > 0) & (block_ids[:, None] == block_range), 1.0, 0.0
@@ -99,6 +93,14 @@
         "mb,mrw->brw", sel_sib, contrib_got, preferred_element_type=jnp.float32
     )
     grad_head = grad_head.astype(jnp.bfloat16).reshape(blocks * block_rows, col_width)
+    ghid = jnp.einsum("mtr,mrw->mtw", grads, rows, preferred_element_type=jnp.float32)
+    ghid, grad_head = lax.optimization_barrier((ghid, grad_head))
+    ghid = lax.psum_scatter(ghid, "section", scatter_dimension=1, tiled=True).astype(jnp.bfloat16)
+    ghid = lax.all_to_all(ghid[:, :, None], "z", split_axis=0, concat_axis=2, tiled=True)
+    ghid = ghid.reshape(tok_local, n_z, n_core, col_width)
+    ghid = jnp.where(odd, ghid[:, :, ::-1, :], ghid)
+    grad_hidden = ghid.reshape(1, tok_local, model_width)
+
     return (grad_hidden, grad_head)
 
 

time: 348 us -> 386 us (1.11)
  waiting for transfers between devices: 179 us -> 198 us
  blocking collectives: 67.1 us -> 84.4 us
  local copies, waits for them, and re-layouts: 20.3 us -> 29.5 us
  starting transfers between devices: 7.31 us -> 0.26 us
    all_to_all x0 -> x1, blocking collectives: none -> 17.5 us  [local(): lax.all_to_all(ghid[:, :, None], 'z', split_axis=0, concat_axis=2, tiled=...]
    all_gather x1, waiting for transfers between devices: 4.81 us -> 16.9 us  [local(): lax.all_gather(pieces, 'section', axis=1, tiled=True)]
    reduce_scatter x1, waiting for transfers between devices: 80.9 us -> 88.8 us  [local(): lax.psum_scatter(ghid, 'section', scatter_dimension=1, tiled=True)]
    all_to_all x1 -> x0, starting transfers between devices: 7.14 us -> none  [local(): lax.all_to_all(ghid[:, :, None], 'z', split_axis=0, concat_axis=2, tiled=...]
    concatenate x0 -> x1, local copies, waits for them, and re-layouts: none -> 4.82 us  [local(): rows = jnp.concatenate([own_rows, sib_rows], axis=2)]
    unnamed x9 -> x10, local copies, waits for them, and re-layouts: 0.53 us -> 5.03 us
  transfers between devices with their start and end apart: 7 -> 6, of which waited for: 5 -> 4; matrix products, arithmetic and copies ran while one was open for 14% -> 8% of each run, Pallas kernels for 0% -> 0%
where the time goes in v6:
time: 386 us; the launch traced here: 385 us
  waiting for transfers between devices  198 us (51%)
  blocking collectives  84.4 us (22%)
  matrix products  37.8 us (10%)
  local copies, waits for them, and re-layouts  29.5 us (8%)
  other arithmetic  19.8 us (5%)
  between operations  15.3 us (4%)
    reduce_scatter x1, waiting for transfers between devices, local(): lax.psum_scatter(ghid, 'section', scatter_dimension=1, tiled=True)  88.8 us
    reduce_scatter x1, waiting for transfers between devices, local(): logits = lax.psum_scatter(part, 'z', scatter_dimension=0, tiled=True)[0]  53.8 us
    all_gather x1, waiting for transfers between devices, local(): grads = lax.all_gather(logit_grad[None], 'z', axis=0, tiled=True)  38.3 us
    all_gather x1, blocking collectives, local(): lax.all_gather(jnp.stack([teach_top_s, teach_sum_s, live_row]), 'section')  23.6 us
    all_gather x1, blocking collectives, local(): stud_all = lax.all_gather(jnp.stack([stud_top_s, stud_sum_s]), 'section')  23 us
    all_to_all x1, blocking collectives, local(): lax.all_to_all(pieces, 'z', split_axis=2, concat_axis=0, tiled=True)  20.2 us
    all_to_all x1, blocking collectives, local(): lax.all_to_all(ghid[:, :, None], 'z', split_axis=0, concat_axis=2, tiled=...  17.5 us
    all_gather x1, waiting for transfers between devices, local(): lax.all_gather(pieces, 'section', axis=1, tiled=True)  16.9 us
  transfers between devices with their start and end apart: 6, of which 4 were waited for; matrix products, arithmetic and copies ran while one was open for 8% of the time, Pallas kernels for 0%

profile of v6, /device:TPU:2, one launch (start us, length us, event | category | flops | bytes accessed | tf_op | source)
XLA Modules:
  0.0 384.9 jit_solution(652400217219865132)
XLA Ops:
  10.7 1.4 rev.6
  12.6 5.0 %gather_fusion = bf16[8,512,512]{2,1,0:T(8,128)(2,1)} fusion(bf16[8,512,512]{2,1,0:T(8,128)(2,1)} %bitcast.85, s32[1024]{0:T(1024)S(1)} %pad_clamp_fusion.1), kind=kCustom, calls=%fused_computation.clone | custom fusion | bytes 8388640 | tf_op jit(solution)/shard_map/jit(_take)/gather | solution.py:34
  17.6 4.9 %gather_fusion.1 = bf16[8,512,512]{2,1,0:T(8,128)(2,1)} fusion(bf16[8,512,512]{2,1,0:T(8,128)(2,1)} %bitcast.86, s32[1024]{0:T(1024)S(1)} %pad_clamp_fusion), kind=kCustom, calls=%fused_computation.1.clone | custom fusion | bytes 8388640 | tf_op jit(solution)/shard_map/jit(_take)/gather | solution.py:35
  22.6 4.8 %broadcast_select_fusion.1 = bf16[8,512,512]{2,1,0:T(8,128)(2,1)} fusion(bf16[8,512,512]{2,1,0:T(8,128)(2,1)} %gather_fusion, pred[8]{0:T(512)(128)(4,1)S(1)} %get-tuple-element.25), kind=kLoop, calls=%fused_computation.8 | loop fusion | flops 2097152 | bytes 8388616 | tf_op jit(solution)/shard_map/jit(_take)/select_n | solution.py:34
  27.4 2.4 broadcast_select_fusion
  29.8 20.2 %all_to_all.33 = bf16[1,16,8,1024]{3,1,0,2:T(8,128)(2,1)} all-to-all(bf16[1,16,8,1024]{3,1,0,2:T(8,128)(2,1)S(1)} %reshape.125), channel_id=1, replica_groups=mesh['section'=16,'z'=8,'core'=2] {'z'}, dimensions={2} | all-to-all | bytes 524288 | tf_op jit(solution)/shard_map/all_to_all | solution.py:38
  53.5 23.6 %all-gather.3 = f32[16,3,256]{2,1,0:T(4,128)S(1)} all-gather(f32[1,3,256]{2,1,0:T(4,128)S(1)} %maximum_bitcast_fusion), channel_id=2, replica_groups=mesh['section'=16,'z'=8,'core'=2] {'section'}, dimensions={0}, use_global_device_ids=true | all-gather | bytes 52224 | tf_op jit(solution)/shard_map/all_gather | solution.py:57
  77.1 4.5 %constant_dynamic-update-slice_fusion.1 = bf16[8,512,1024]{2,1,0:T(8,128)(2,1)} fusion(bf16[8,512,512]{2,1,0:T(8,128)(2,1)} %broadcast_select_fusion.1), kind=kLoop, calls=%fused_computation.48 | loop fusion | bytes 8388608
  81.6 4.8 %constant_dynamic-update-slice_fusion = bf16[8,512,1024]{2,1,0:T(8,128)(2,1)} fusion(bf16[8,512,1024]{2,1,0:T(8,128)(2,1)} %constant_dynamic-update-slice_fusion.1, bf16[8,512,512]{2,1,0:T(8,128)(2,1)} %collective-permute-done), kind=kLoop, calls=%fused_computation.47 | loop fusion | bytes 8388608 | tf_op jit(solution)/shard_map/concatenate | solution.py:40
  86.5 16.9 %all-gather.10.cloned.1.call-done = bf16[8,1,256,1,1024]{4,2,0,3,1:T(8,128)(2,1)} async-done(((bf16[8,1,16,1,1024]{4,2,0,3,1:T(8,128)(2,1)}), bf16[8,1,256,1,1024]{4,2,0,3,1:T(8,128)(2,1)}) %all-gather.10.cloned.1.call-update) | async-done | bytes 4194320 | tf_op jit(solution)/shard_map/all_gather | solution.py:39
  103.3 9.0 %fusion.32 = f32[8,256,512]{2,1,0:T(8,128)} fusion(bf16[8,256,1024]{2,1,0:T(8,128)(2,1)} %bitcast.87, bf16[8,512,1024]{2,1,0:T(8,128)(2,1)} %constant_dynamic-update-slice_fusion), kind=kOutput, calls=%fused_computation.70 | convolution fusion | flops 2147483648 | bytes 16777216 | tf_op jit(solution)/shard_map/mtw,mrw->mtr/dot_general | solution.py:62
  113.8 53.8 %reduce-scatter.3.cloned.1.call-done = f32[1,256,512]{2,1,0:T(8,128)} async-done(((f32[8,256,512]{2,1,0:T(8,128)}), f32[1,256,512]{2,1,0:T(8,128)}) %reduce-scatter.3.cloned.1.call-update) | async-done | bytes 524304 | tf_op jit(solution)/shard_map/reduce_scatter | solution.py:63
  171.4 23.0 %all-gather.4 = f32[16,2,256]{2,1,0:T(2,128)S(1)} all-gather(f32[1,2,256]{2,1,0:T(2,128)S(1)} %maximum_bitcast_fusion.1), channel_id=4, replica_groups=mesh['section'=16,'z'=8,'core'=2] {'section'}, dimensions={0}, use_global_device_ids=true | all-gather | bytes 34816 | tf_op jit(solution)/shard_map/all_gather | solution.py:66
  194.5 2.8 fusion.18
  197.3 38.3 %all-gather.8.cloned.1.call-done = bf16[8,256,512]{2,1,0:T(8,128)(2,1)} async-done(((bf16[1,256,512]{2,1,0:T(8,128)(2,1)}), bf16[8,256,512]{2,1,0:T(8,128)(2,1)}) %all-gather.8.cloned.1.call-update) | async-done | bytes 2097168 | tf_op jit(solution)/shard_map/all_gather | solution.py:74
  235.6 5.7 %convolution_convert_fusion = bf16[8,512,512]{2,1,0:T(8,128)(2,1)} fusion(bf16[8,256,512]{2,1,0:T(8,128)(2,1)} %all-gather.8.cloned.1.call-done, bf16[8,256,1024]{2,1,0:T(8,128)(2,1)} %bitcast.88), kind=kOutput, calls=%fused_computation.9 | convolution fusion | flops 1075838976 | bytes 8388608 | tf_op jit(solution)/shard_map/mtr,mtw->mrw/dot_general | solution.py:76
  241.7 2.9 convolution_convert_fusion.1
  244.6 4.8 %fusion.2 = f32[8,512,512]{2,0,1:T(8,128)} fusion(bf16[8,512,512]{2,1,0:T(8,128)(2,1)S(1)} %convolution_convert_fusion.1, bf16[8,2,8]{2,0,1:T(8,128)(2,1)S(1)} %select_convert_fusion, s32[]{:T(128)S(6)} %select_n.133), kind=kOutput, calls=%fused_computation.5 | convolution fusion | flops 33554432 | bytes 12584964 | tf_op jit(solution)/shard_map/mb,mrw->brw/dot_general | solution.py:91
  249.4 9.0 %fusion.33 = f32[8,256,1024]{2,1,0:T(8,128)} fusion(bf16[8,256,512]{2,1,0:T(8,128)(2,1)S(1)} %copy-done, bf16[8,512,1024]{2,1,0:T(8,128)(2,1)} %constant_dynamic-update-slice_fusion), kind=kOutput, calls=%fused_computation.71 | convolution fusion | flops 2147483648 | bytes 18874368 | tf_op jit(solution)/shard_map/mtr,mrw->mtw/dot_general | solution.py:96
  258.3 6.4 %add_convert_fusion = bf16[8,512,512]{2,0,1:T(8,128)(2,1)S(1)} fusion(f32[8,512,512]{2,0,1:T(8,128)} %fusion.2, bf16[8,512,512]{2,1,0:T(8,128)(2,1)} %collective-permute-done.1, bf16[8,2,8]{2,0,1:T(8,128)(2,1)S(1)} %select_convert_fusion, s32[]{:T(128)S(6)} %select_n.134), kind=kOutput, calls=%fused_computation.2 | convolution fusion | flops 37748736 | bytes 16779268 | tf_op jit(solution)/shard_map/mb,mrw->brw/dot_general | solution.py:92
  264.7 3.5 copy.38
  268.2 88.8 %reduce-scatter.5.cloned.1.call-done = f32[8,16,1024]{2,1,0:T(8,128)} async-done(((f32[8,256,1024]{2,1,0:T(8,128)}), f32[8,16,1024]{2,1,0:T(8,128)}) %reduce-scatter.5.cloned.1.call-update) | async-done | bytes 524304 | tf_op jit(solution)/shard_map/reduce_scatter | solution.py:98
  358.0 17.5 %all_to_all.34 = bf16[8,16,1,1024]{3,1,2,0:T(8,128)(2,1)S(1)} all-to-all(bf16[8,16,1,1024]{3,1,2,0:T(8,128)(2,1)S(1)} %convert_bitcast_fusion.1), channel_id=1, replica_groups=mesh['section'=16,'z'=8,'core'=2] {'z'}, dimensions={0} | all-to-all | bytes 524288 | tf_op jit(solution)/shard_map/all_to_all | solution.py:99
  375.8 1.4 rev.7
  (61 shorter events, 14.2 us)
Async XLA Ops:
  7.2 96.2 %all-gather.10.cloned.1.call-start = ((), (), s32[]{:S(2)}) async-start(), calls=%async_computation.7 | async-start | bytes 4456448 | tf_op jit(solution)/shard_map/all_gather | solution.py:39
  22.6 4.8 %copy-start.1 = (bf16[8,512,512]{2,1,0:T(8,128)(2,1)S(1)}, bf16[8,512,512]{2,1,0:T(8,128)(2,1)}, u32[]{:S(2)}) copy-start(bf16[8,512,512]{2,1,0:T(8,128)(2,1)} %gather_fusion.1) | copy-start | bytes 12582916
  27.4 22.9 %copy-start.3 = (s32[16,1]{0,1:T(1,128)S(1)}, s32[16,1]{0,1:T(1,128)}, u32[]{:S(2)}) copy-start(s32[16,1]{0,1:T(1,128)} %param.10) | copy-start | bytes 196
  27.4 24.3 %copy-start.2 = (bf16[1,256,512]{2,1,0:T(8,128)(2,1)S(1)}, bf16[1,256,512]{2,1,0:T(8,128)(2,1)}, u32[]{:S(2)}) copy-start(bf16[1,256,512]{2,1,0:T(8,128)(2,1)} %param.11) | copy-start | bytes 786436
  50.1 117.5 %reduce-scatter.3.cloned.1.call-start = ((), (), s32[]{:S(2)}) async-start(), calls=%async_computation.4 | async-start | bytes 4718592 | tf_op jit(solution)/shard_map/reduce_scatter | solution.py:63
  50.1 31.5 %collective-permute-start = (bf16[8,512,512]{2,1,0:T(8,128)(2,1)}, bf16[8,512,512]{2,1,0:T(8,128)(2,1)}, u32[]{:S(2)}, u32[]{:S(2)}) collective-permute-start(bf16[8,512,512]{2,1,0:T(8,128)(2,1)} %broadcast_select_fusion), channel_id=1, source_target_pairs={{0,1},{1,0},{2,3},{3,2},{4,5},{5,4},{6,7},{7,6},{8,9},{9,8},{10,11... | collective-permute-start | bytes 12582920 | tf_op jit(solution)/shard_map/ppermute | solution.py:37
  112.4 123.2 %all-gather.8.cloned.1.call-start = ((), (), s32[]{:S(2)}) async-start(), calls=%async_computation.5 | async-start | bytes 2359296 | tf_op jit(solution)/shard_map/all_gather | solution.py:74
  197.3 159.7 %reduce-scatter.5.cloned.1.call-start = ((), (), s32[]{:S(2)}) async-start(), calls=%async_computation.6 | async-start | bytes 8912896 | tf_op jit(solution)/shard_map/reduce_scatter | solution.py:98
  235.6 6.1 %copy-start = (bf16[8,256,512]{2,1,0:T(8,128)(2,1)S(1)}, bf16[8,256,512]{2,1,0:T(8,128)(2,1)}, u32[]{:S(2)}) copy-start(bf16[8,256,512]{2,1,0:T(8,128)(2,1)} %all-gather.8.cloned.1.call-done) | copy-start | bytes 6291460
  241.3 17.0 %collective-permute-start.1 = (bf16[8,512,512]{2,1,0:T(8,128)(2,1)}, bf16[8,512,512]{2,1,0:T(8,128)(2,1)}, u32[]{:S(2)}, u32[]{:S(2)}) collective-permute-start(bf16[8,512,512]{2,1,0:T(8,128)(2,1)} %convolution_convert_fusion), channel_id=1, source_target_pairs={{0,1},{1,0},{2,3},{3,2},{4,5},{5,4},{6,7},{7,6},{8,9},{9,8},{10,11... | collective-permute-start | bytes 12582920 | tf_op jit(solution)/shard_map/ppermute | solution.py:79
Sparse Core Ops, SparseCore 0:
  50.2 53.0 all-gather.9
  112.5 55.0 reduce-scatter.2
  197.4 38.1 all-gather.7
  268.3 88.5 reduce-scatter.4

commit v7 on v4

--- a/solution.py
+++ b/solution.py
@@ -29,9 +29,14 @@
 
     pieces = hidden[0].reshape(tok_local, n_z, n_core, col_width)
     pieces = jnp.where(odd, pieces[:, :, ::-1, :], pieces)
-    pieces = pieces.reshape(1, tok_local, n_z, n_core * col_width)
-    pieces = lax.all_to_all(pieces, "z", split_axis=2, concat_axis=0, tiled=True)
-    hid_w = lax.all_gather(pieces, "section", axis=1, tiled=True).reshape(n_z, -1, n_core * col_width)
+    pieces = pieces.transpose(1, 0, 2, 3).reshape(n_z, tok_local, n_core * col_width)
+    arrived = [lax.dynamic_index_in_dim(pieces, z_at, 0, keepdims=False)]
+    for k in range(1, n_z):
+        sent = lax.dynamic_index_in_dim(pieces, (z_at + k) % n_z, 0, keepdims=False)
+        arrived.append(lax.ppermute(sent, "z", [(j, (j + k) % n_z) for j in range(n_z)]))
+    order = (z_at - jnp.arange(n_z, dtype=jnp.int32)) % n_z
+    pieces = jnp.take(jnp.stack(arrived), order, axis=0)
+    hid_w = lax.all_gather(pieces, "section", axis=1, tiled=True)
 
     own_rows = jnp.take(table, own_ids, axis=0)
     sib_rows = lax.ppermute(jnp.take(table, sib_ids, axis=0), "core", swap)

time: 348 us -> 352 us (1.011)
  blocking collectives: 67.1 us -> 46.8 us
  starting transfers between devices: 7.31 us -> 25.9 us
  waiting for transfers between devices: 179 us -> 184 us
    all_to_all x1 -> x0, blocking collectives: 20.2 us -> none  [local(): lax.all_to_all(pieces, 'z', split_axis=2, concat_axis=0, tiled=True)]
    ppermute x0 -> x7, starting transfers between devices: none -> 18.5 us  [local(): lax.ppermute(sent, 'z', [(j, (j + k) % n_z) for j in range(n_z)])]
  transfers between devices with their start and end apart: 7 -> 14, of which waited for: 5 -> 7; matrix products, arithmetic and copies ran while one was open for 14% -> 14% of each run, Pallas kernels for 0% -> 0%
where the time goes in v7:
time: 352 us; the launch traced here: 351 us
  waiting for transfers between devices  184 us (52%)
  blocking collectives  46.8 us (13%)
  matrix products  36.6 us (10%)
  starting transfers between devices  25.9 us (7%)
  other arithmetic  22 us (6%)
  local copies, waits for them, and re-layouts  20.9 us (6%)
  between operations  15.4 us (4%)
    reduce_scatter x1, waiting for transfers between devices, local(): lax.psum_scatter(ghid, 'section', scatter_dimension=1, tiled=True)  80.9 us
    reduce_scatter x1, waiting for transfers between devices, local(): logits = lax.psum_scatter(part, 'z', scatter_dimension=0, tiled=True)[0]  53.6 us
    all_gather x1, waiting for transfers between devices, local(): grads = lax.all_gather(logit_grad[None], 'z', axis=0, tiled=True)  38.3 us
    all_gather x1, blocking collectives, local(): lax.all_gather(jnp.stack([teach_top_s, teach_sum_s, live_row]), 'section')  23.8 us
    all_gather x1, blocking collectives, local(): stud_all = lax.all_gather(jnp.stack([stud_top_s, stud_sum_s]), 'section')  23 us
    ppermute x7, starting transfers between devices, local(): lax.ppermute(sent, 'z', [(j, (j + k) % n_z) for j in range(n_z)])  18.5 us
    dot_general x1, matrix products, local(): jnp.einsum('mtw,mrw->mtr', hid_w, rows, preferred_element_type=jnp.float32)  9.04 us
    dot_general x1, matrix products, local(): jnp.einsum('mtr,mrw->mtw', grads, rows, preferred_element_type=jnp.float32)  7.78 us
  transfers between devices with their start and end apart: 14, of which 7 were waited for; matrix products, arithmetic and copies ran while one was open for 14% of the time, Pallas kernels for 0%

profile of v7, /device:TPU:2, one launch (start us, length us, event | category | flops | bytes accessed | tf_op | source)
XLA Modules:
  0.0 351.3 jit_solution(5605085319823577655)
XLA Ops:
  10.6 2.0 collective-permute-start
  12.6 3.3 collective-permute-start.1
  15.9 4.0 %collective-permute-start.2 = (bf16[16,1024]{1,0:T(8,128)(2,1)S(1)}, bf16[16,1024]{1,0:T(8,128)(2,1)S(1)}, u32[]{:S(2)}, u32[]{:S(2)}) collective-permute-start(bf16[16,1024]{1,0:T(8,128)(2,1)S(1)} %get-tuple-element.17), channel_id=1, source_target_pairs={{0,6},{2,8},{4,10},{6,12},{8,14},{10,0},{12,2},{14,4},{1,7},{3,9},... | collective-permute-start | bytes 98312 | tf_op jit(solution)/shard_map/ppermute | solution.py:36
  20.4 4.9 %collective-permute-start.4 = (bf16[16,1024]{1,0:T(8,128)(2,1)S(1)}, bf16[16,1024]{1,0:T(8,128)(2,1)S(1)}, u32[]{:S(2)}, u32[]{:S(2)}) collective-permute-start(bf16[16,1024]{1,0:T(8,128)(2,1)S(1)} %get-tuple-element.15), channel_id=1, source_target_pairs={{0,10},{2,12},{4,14},{6,0},{8,2},{10,4},{12,6},{14,8},{1,11},{3,13... | collective-permute-start | bytes 98312 | tf_op jit(solution)/shard_map/ppermute | solution.py:36
  25.4 2.7 collective-permute-start.5
  35.1 5.0 %gather_fusion.2 = bf16[8,512,512]{2,1,0:T(8,128)(2,1)} fusion(bf16[8,512,512]{2,1,0:T(8,128)(2,1)} %bitcast.109, s32[1024]{0:T(1024)S(1)} %pad_clamp_fusion), kind=kCustom, calls=%fused_computation.1.clone | custom fusion | bytes 8388640 | tf_op jit(solution)/shard_map/jit(_take)/gather | solution.py:42
  40.1 4.7 %broadcast_select_fusion = bf16[8,512,512]{2,1,0:T(8,128)(2,1)} fusion(bf16[8,512,512]{2,1,0:T(8,128)(2,1)} %gather_fusion.2, pred[8]{0:T(512)(128)(4,1)S(1)} %compare_and_fusion), kind=kLoop, calls=%fused_computation.11 | loop fusion | flops 2097152 | bytes 8388616 | tf_op jit(solution)/shard_map/jit(_take)/select_n | solution.py:42
  44.8 5.0 %gather_fusion.1 = bf16[8,512,512]{2,1,0:T(8,128)(2,1)} fusion(bf16[8,512,512]{2,1,0:T(8,128)(2,1)} %bitcast.110, s32[1024]{0:T(1024)S(1)} %pad_clamp_fusion.1), kind=kCustom, calls=%fused_computation.clone | custom fusion | bytes 8388640 | tf_op jit(solution)/shard_map/jit(_take)/gather | solution.py:41
  52.5 23.8 %all-gather.2 = f32[16,3,256]{2,1,0:T(4,128)S(1)} all-gather(f32[1,3,256]{2,1,0:T(4,128)S(1)} %maximum_bitcast_fusion), channel_id=2, replica_groups=mesh['section'=16,'z'=8,'core'=2] {'section'}, dimensions={0}, use_global_device_ids=true | all-gather | bytes 52224 | tf_op jit(solution)/shard_map/all_gather | solution.py:60
  76.3 4.7 %broadcast_select_fusion.1 = bf16[8,512,512]{2,1,0:T(8,128)(2,1)} fusion(bf16[8,512,512]{2,1,0:T(8,128)(2,1)} %gather_fusion.1, pred[8]{0:T(512)(128)(4,1)S(1)} %compare_and_fusion.1), kind=kLoop, calls=%fused_computation.12 | loop fusion | flops 2097152 | bytes 8388616 | tf_op jit(solution)/shard_map/jit(_take)/select_n | solution.py:41
  80.9 7.3 %all-gather.7.cloned.1.call-done = bf16[8,256,1024]{2,1,0:T(8,128)(2,1)} async-done(((bf16[8,16,1024]{2,1,0:T(8,128)(2,1)}), bf16[8,256,1024]{2,1,0:T(8,128)(2,1)}) %all-gather.7.cloned.1.call-update) | async-done | bytes 4194320 | tf_op jit(solution)/shard_map/all_gather | solution.py:39
  88.3 9.0 %fusion.1 = f32[8,256,512]{2,1,0:T(8,128)} fusion(bf16[8,256,1024]{2,1,0:T(8,128)(2,1)} %all-gather.7.cloned.1.call-done, bf16[8,512,512]{2,1,0:T(8,128)(2,1)} %collective-permute-done.7, bf16[8,512,512]{2,1,0:T(8,128)(2,1)} %broadcast_select_fusion.1), kind=kOutput, calls=%fused_computation.6 | convolution fusion | flops 2164260864 | bytes 16777216 | tf_op jit(solution)/shard_map/mtw,mrw->mtr/dot_general | solution.py:65
  98.9 53.6 %reduce-scatter.3.cloned.1.call-done = f32[1,256,512]{2,1,0:T(8,128)} async-done(((f32[8,256,512]{2,1,0:T(8,128)}), f32[1,256,512]{2,1,0:T(8,128)}) %reduce-scatter.3.cloned.1.call-update) | async-done | bytes 524304 | tf_op jit(solution)/shard_map/reduce_scatter | solution.py:66
  156.1 23.0 %all-gather.3 = f32[16,2,256]{2,1,0:T(2,128)S(1)} all-gather(f32[1,2,256]{2,1,0:T(2,128)S(1)} %maximum_bitcast_fusion.1), channel_id=3, replica_groups=mesh['section'=16,'z'=8,'core'=2] {'section'}, dimensions={0}, use_global_device_ids=true | all-gather | bytes 34816 | tf_op jit(solution)/shard_map/all_gather | solution.py:69
  179.2 2.6 fusion.20
  181.8 38.3 %all-gather.9.cloned.1.call-done = bf16[8,256,512]{2,1,0:T(8,128)(2,1)} async-done(((bf16[1,256,512]{2,1,0:T(8,128)(2,1)}), bf16[8,256,512]{2,1,0:T(8,128)(2,1)}) %all-gather.9.cloned.1.call-update) | async-done | bytes 2097168 | tf_op jit(solution)/shard_map/all_gather | solution.py:77
  220.1 5.7 %convolution_convert_fusion.1 = bf16[8,512,512]{2,1,0:T(8,128)(2,1)} fusion(bf16[8,256,512]{2,1,0:T(8,128)(2,1)} %all-gather.9.cloned.1.call-done, bf16[8,256,1024]{2,1,0:T(8,128)(2,1)} %all-gather.7.cloned.1.call-done), kind=kOutput, calls=%fused_computation.14 | convolution fusion | flops 1075838976 | bytes 8388608 | tf_op jit(solution)/shard_map/mtr,mtw->mrw/dot_general | solution.py:79
  225.8 7.8 %fusion = f32[8,256,1024]{2,1,0:T(8,128)} fusion(bf16[8,256,512]{2,1,0:T(8,128)(2,1)S(1)} %copy-done, bf16[8,512,512]{2,1,0:T(8,128)(2,1)} %collective-permute-done.7, bf16[8,512,512]{2,1,0:T(8,128)(2,1)S(1)} %copy-done.1), kind=kOutput, calls=%fused_computation.5 | convolution fusion | flops 2164260864 | bytes 18874368 | tf_op jit(solution)/shard_map/mtr,mrw->mtw/dot_general | solution.py:87
  234.0 2.9 convolution_convert_fusion
  236.9 4.8 %fusion.4 = f32[8,512,512]{2,0,1:T(8,128)} fusion(bf16[8,512,512]{2,1,0:T(8,128)(2,1)S(1)} %convolution_convert_fusion, bf16[8,2,8]{2,0,1:T(8,128)(2,1)S(1)} %select_convert_fusion, s32[]{:T(128)S(6)} %select_n.246), kind=kOutput, calls=%fused_computation.9 | convolution fusion | flops 33554432 | bytes 12584964 | tf_op jit(solution)/shard_map/mb,mrw->brw/dot_general | solution.py:102
  241.6 80.9 %reduce-scatter.5.cloned.1.call-done = f32[8,16,1024]{2,1,0:T(8,128)} async-done(((f32[8,256,1024]{2,1,0:T(8,128)}), f32[8,16,1024]{2,1,0:T(8,128)}) %reduce-scatter.5.cloned.1.call-update) | async-done | bytes 524304 | tf_op jit(solution)/shard_map/reduce_scatter | solution.py:89
  324.3 7.0 %all-to-all-start = ((bf16[8,16,1,1024]{3,1,2,0:T(8,128)(2,1)}), bf16[8,16,1,1024]{3,1,2,0:T(8,128)(2,1)S(1)}, u32[]{:S(2)}, u32[]{:S(2)}) async-start(bf16[8,16,1,1024]{3,1,2,0:T(8,128)(2,1)} %convert_bitcast_fusion.1), calls=%async_computation.2 | async-start | bytes 524288 | tf_op jit(solution)/shard_map/all_to_all | solution.py:90
  331.4 6.4 %add_convert_fusion = bf16[8,512,512]{2,0,1:T(8,128)(2,1)S(1)} fusion(f32[8,512,512]{2,0,1:T(8,128)} %fusion.4, bf16[8,512,512]{2,1,0:T(8,128)(2,1)} %collective-permute-done.8, bf16[8,2,8]{2,0,1:T(8,128)(2,1)S(1)} %select_convert_fusion, s32[]{:T(128)S(6)} %select_n.247), kind=kOutput, calls=%fused_computation.4 | convolution fusion | flops 37748736 | bytes 16779268 | tf_op jit(solution)/shard_map/mb,mrw->brw/dot_general | solution.py:103
  337.8 3.5 copy.44
  (90 shorter events, 23.1 us)
Async XLA Ops:
  7.2 26.9 %copy-start.3 = (s32[16,1]{0,1:T(1,128)S(1)}, s32[16,1]{0,1:T(1,128)}, u32[]{:S(2)}) copy-start(s32[16,1]{0,1:T(1,128)} %param.9) | copy-start | bytes 196
  7.2 81.1 %all-gather.7.cloned.1.call-start = ((), (), s32[]{:S(2)}) async-start(), calls=%async_computation.3 | async-start | bytes 4456448 | tf_op jit(solution)/shard_map/all_gather | solution.py:39
  10.6 14.8 %collective-permute-start = (bf16[16,1024]{1,0:T(8,128)(2,1)S(1)}, bf16[16,1024]{1,0:T(8,128)(2,1)S(1)}, u32[]{:S(2)}, u32[]{:S(2)}) collective-permute-start(bf16[16,1024]{1,0:T(8,128)(2,1)S(1)} %get-tuple-element.19), channel_id=1, source_target_pairs={{0,2},{2,4},{4,6},{6,8},{8,10},{10,12},{12,14},{14,0},{1,3},{3,5},... | collective-permute-start | bytes 98312 | tf_op jit(solution)/shard_map/ppermute | solution.py:36
  12.6 15.6 %collective-permute-start.1 = (bf16[16,1024]{1,0:T(8,128)(2,1)S(1)}, bf16[16,1024]{1,0:T(8,128)(2,1)S(1)}, u32[]{:S(2)}, u32[]{:S(2)}) collective-permute-start(bf16[16,1024]{1,0:T(8,128)(2,1)S(1)} %get-tuple-element.18), channel_id=1, source_target_pairs={{0,4},{2,6},{4,8},{6,10},{8,12},{10,14},{12,0},{14,2},{1,5},{3,7},... | collective-permute-start | bytes 98312 | tf_op jit(solution)/shard_map/ppermute | solution.py:36
  15.9 13.3 %collective-permute-start.2 = (bf16[16,1024]{1,0:T(8,128)(2,1)S(1)}, bf16[16,1024]{1,0:T(8,128)(2,1)S(1)}, u32[]{:S(2)}, u32[]{:S(2)}) collective-permute-start(bf16[16,1024]{1,0:T(8,128)(2,1)S(1)} %get-tuple-element.17), channel_id=1, source_target_pairs={{0,6},{2,8},{4,10},{6,12},{8,14},{10,0},{12,2},{14,4},{1,7},{3,9},... | collective-permute-start | bytes 98312 | tf_op jit(solution)/shard_map/ppermute | solution.py:36
  19.9 9.3 %collective-permute-start.3 = (bf16[16,1024]{1,0:T(8,128)(2,1)S(1)}, bf16[16,1024]{1,0:T(8,128)(2,1)S(1)}, u32[]{:S(2)}, u32[]{:S(2)}) collective-permute-start(bf16[16,1024]{1,0:T(8,128)(2,1)S(1)} %get-tuple-element.16), channel_id=1, source_target_pairs={{0,8},{2,10},{4,12},{6,14},{8,0},{10,2},{12,4},{14,6},{1,9},{3,11}... | collective-permute-start | bytes 98312 | tf_op jit(solution)/shard_map/ppermute | solution.py:36
  20.4 8.8 %collective-permute-start.4 = (bf16[16,1024]{1,0:T(8,128)(2,1)S(1)}, bf16[16,1024]{1,0:T(8,128)(2,1)S(1)}, u32[]{:S(2)}, u32[]{:S(2)}) collective-permute-start(bf16[16,1024]{1,0:T(8,128)(2,1)S(1)} %get-tuple-element.15), channel_id=1, source_target_pairs={{0,10},{2,12},{4,14},{6,0},{8,2},{10,4},{12,6},{14,8},{1,11},{3,13... | collective-permute-start | bytes 98312 | tf_op jit(solution)/shard_map/ppermute | solution.py:36
  25.4 5.1 %collective-permute-start.5 = (bf16[16,1024]{1,0:T(8,128)(2,1)S(1)}, bf16[16,1024]{1,0:T(8,128)(2,1)S(1)}, u32[]{:S(2)}, u32[]{:S(2)}) collective-permute-start(bf16[16,1024]{1,0:T(8,128)(2,1)S(1)} %get-tuple-element.14), channel_id=1, source_target_pairs={{0,12},{2,14},{4,0},{6,2},{8,4},{10,6},{12,8},{14,10},{1,13},{3,15... | collective-permute-start | bytes 98312 | tf_op jit(solution)/shard_map/ppermute | solution.py:36
  28.2 3.9 %collective-permute-start.6 = (bf16[16,1024]{1,0:T(8,128)(2,1)S(1)}, bf16[16,1024]{1,0:T(8,128)(2,1)S(1)}, u32[]{:S(2)}, u32[]{:S(2)}) collective-permute-start(bf16[16,1024]{1,0:T(8,128)(2,1)S(1)} %get-tuple-element.13), channel_id=1, source_target_pairs={{0,14},{2,0},{4,2},{6,4},{8,6},{10,8},{12,10},{14,12},{1,15},{3,1}... | collective-permute-start | bytes 98312 | tf_op jit(solution)/shard_map/ppermute | solution.py:36
  33.5 119.0 %reduce-scatter.3.cloned.1.call-start = ((), (), s32[]{:S(2)}) async-start(), calls=%async_computation.4 | async-start | bytes 4718592 | tf_op jit(solution)/shard_map/reduce_scatter | solution.py:66
  44.8 43.5 %collective-permute-start.7 = (bf16[8,512,512]{2,1,0:T(8,128)(2,1)}, bf16[8,512,512]{2,1,0:T(8,128)(2,1)}, u32[]{:S(2)}, u32[]{:S(2)}) collective-permute-start(bf16[8,512,512]{2,1,0:T(8,128)(2,1)} %broadcast_select_fusion), channel_id=1, source_target_pairs={{0,1},{1,0},{2,3},{3,2},{4,5},{5,4},{6,7},{7,6},{8,9},{9,8},{10,11... | collective-permute-start | bytes 12582920 | tf_op jit(solution)/shard_map/ppermute | solution.py:42
  44.8 5.0 %copy-start.2 = (bf16[1,256,512]{2,1,0:T(8,128)(2,1)S(1)}, bf16[1,256,512]{2,1,0:T(8,128)(2,1)}, u32[]{:S(2)}) copy-start(bf16[1,256,512]{2,1,0:T(8,128)(2,1)} %param.11) | copy-start | bytes 786436
  44.8 5.1 %copy-start.4 = (s32[16,1]{0,1:T(1,128)S(1)}, s32[16,1]{0,1:T(1,128)}, u32[]{:S(2)}) copy-start(s32[16,1]{0,1:T(1,128)} %param.10) | copy-start | bytes 196
  97.3 122.8 %all-gather.9.cloned.1.call-start = ((), (), s32[]{:S(2)}) async-start(), calls=%async_computation.5 | async-start | bytes 2359296 | tf_op jit(solution)/shard_map/all_gather | solution.py:77
  181.8 140.8 %reduce-scatter.5.cloned.1.call-start = ((), (), s32[]{:S(2)}) async-start(), calls=%async_computation.6 | async-start | bytes 8912896 | tf_op jit(solution)/shard_map/reduce_scatter | solution.py:89
  220.1 5.7 %copy-start = (bf16[8,256,512]{2,1,0:T(8,128)(2,1)S(1)}, bf16[8,256,512]{2,1,0:T(8,128)(2,1)}, u32[]{:S(2)}) copy-start(bf16[8,256,512]{2,1,0:T(8,128)(2,1)} %all-gather.9.cloned.1.call-done) | copy-start | bytes 6291460
  220.1 5.7 %copy-start.1 = (bf16[8,512,512]{2,1,0:T(8,128)(2,1)S(1)}, bf16[8,512,512]{2,1,0:T(8,128)(2,1)}, u32[]{:S(2)}) copy-start(bf16[8,512,512]{2,1,0:T(8,128)(2,1)} %broadcast_select_fusion.1) | copy-start | bytes 12582916
  225.8 7.8 %collective-permute-start.8 = (bf16[8,512,512]{2,1,0:T(8,128)(2,1)}, bf16[8,512,512]{2,1,0:T(8,128)(2,1)}, u32[]{:S(2)}, u32[]{:S(2)}) collective-permute-start(bf16[8,512,512]{2,1,0:T(8,128)(2,1)} %convolution_convert_fusion.1), channel_id=1, source_target_pairs={{0,1},{1,0},{2,3},{3,2},{4,5},{5,4},{6,7},{7,6},{8,9},{9,8},{10,11... | collective-permute-start | bytes 12582920 | tf_op jit(solution)/shard_map/ppermute | solution.py:82
  324.3 17.7 %all-to-all-start = ((bf16[8,16,1,1024]{3,1,2,0:T(8,128)(2,1)}), bf16[8,16,1,1024]{3,1,2,0:T(8,128)(2,1)S(1)}, u32[]{:S(2)}, u32[]{:S(2)}) async-start(bf16[8,16,1,1024]{3,1,2,0:T(8,128)(2,1)} %convert_bitcast_fusion.1), calls=%async_computation.2 | async-start | bytes 524288 | tf_op jit(solution)/shard_map/all_to_all | solution.py:90
Sparse Core Ops, SparseCore 0:
  33.6 54.5 all-gather.6
  97.5 55.0 reduce-scatter.2
  181.9 38.1 all-gather.8
  233.7 88.7 reduce-scatter.4

commit v8 on v4

--- a/solution.py
+++ b/solution.py
@@ -71,6 +71,8 @@
     logit_grad = (block_rows * live_count * (student - teach_prob)).astype(jnp.bfloat16)
     grads = lax.all_gather(logit_grad[None], "z", axis=0, tiled=True)
 
+    ghid = jnp.einsum("mtr,mrw->mtw", grads, rows, preferred_element_type=jnp.float32)
+    ghid, grads = lax.optimization_barrier((ghid, grads))
     contrib_sib = jnp.einsum(
         "mtr,mtw->mrw", grads, hid_w[:, :, col_width:], preferred_element_type=jnp.float32
     ).astype(jnp.bfloat16)
@@ -79,8 +81,6 @@
         "mtr,mtw->mrw", grads, hid_w[:, :, :col_width], preferred_element_type=jnp.float32
     ).astype(jnp.bfloat16)
 
-    ghid = jnp.einsum("mtr,mrw->mtw", grads, rows, preferred_element_type=jnp.float32)
-    ghid, contrib_got = lax.optimization_barrier((ghid, contrib_got))
     ghid = lax.psum_scatter(ghid, "section", scatter_dimension=1, tiled=True).astype(jnp.bfloat16)
     ghid = lax.all_to_all(ghid[:, :, None], "z", split_axis=0, concat_axis=2, tiled=True)
     ghid = ghid.reshape(tok_local, n_z, n_core, col_width)
@@ -94,10 +94,10 @@
     sel_by = selector.reshape(n_z, n_core, blocks)
     sel_own = lax.dynamic_index_in_dim(sel_by, core_at, 1, keepdims=False)
     sel_sib = lax.dynamic_index_in_dim(sel_by, 1 - core_at, 1, keepdims=False)
-    grad_head = jnp.einsum("mb,mrw->brw", sel_own, contrib_own, preferred_element_type=jnp.float32)
-    grad_head = grad_head + jnp.einsum(
-        "mb,mrw->brw", sel_sib, contrib_got, preferred_element_type=jnp.float32
-    )
+    n_own = contrib_own.shape[0]
+    grad_head = jnp.dot(
+        sel_own.T, contrib_own.reshape(n_own, -1), preferred_element_type=jnp.float32
+    ) + jnp.dot(sel_sib.T, contrib_got.reshape(n_own, -1), preferred_element_type=jnp.float32)
     grad_head = grad_head.astype(jnp.bfloat16).reshape(blocks * block_rows, col_width)
     return (grad_hidden, grad_head)
 

time: 348 us -> 347 us (level)
  waiting for transfers between devices: 179 us -> 162 us
  local copies, waits for them, and re-layouts: 20.3 us -> 33.5 us
    reduce_scatter x1, waiting for transfers between devices: 80.9 us -> 66 us  [local(): lax.psum_scatter(ghid, 'section', scatter_dimension=1, tiled=True)]
    unnamed x9, local copies, waits for them, and re-layouts: 0.53 us -> 11.1 us
    reshape x0 -> x1, local copies, waits for them, and re-layouts: none -> 6.09 us  [local(): grad_head.astype(jnp.bfloat16).reshape(blocks * block_rows, col_width)]
  transfers between devices with their start and end apart: 7 -> 7, of which waited for: 5 -> 4; matrix products, arithmetic and copies ran while one was open for 14% -> 17% of each run, Pallas kernels for 0% -> 0%
where the time goes in v8:
time: 347 us; the launch traced here: 346 us
  waiting for transfers between devices  162 us (47%)
  blocking collectives  67.1 us (19%)
  matrix products  37.2 us (11%)
  local copies, waits for them, and re-layouts  33.5 us (10%)
  other arithmetic  22.8 us (7%)
  between operations  15.3 us (4%)
  starting transfers between devices  7.23 us (2%)
    reduce_scatter x1, waiting for transfers between devices, local(): lax.psum_scatter(ghid, 'section', scatter_dimension=1, tiled=True)  66 us
    reduce_scatter x1, waiting for transfers between devices, local(): logits = lax.psum_scatter(part, 'z', scatter_dimension=0, tiled=True)[0]  53.9 us
    all_gather x1, waiting for transfers between devices, local(): grads = lax.all_gather(logit_grad[None], 'z', axis=0, tiled=True)  38.3 us
    all_gather x1, blocking collectives, local(): lax.all_gather(jnp.stack([teach_top_s, teach_sum_s, live_row]), 'section')  23.8 us
    all_gather x1, blocking collectives, local(): stud_all = lax.all_gather(jnp.stack([stud_top_s, stud_sum_s]), 'section')  23 us
    all_to_all x1, blocking collectives, local(): lax.all_to_all(pieces, 'z', split_axis=2, concat_axis=0, tiled=True)  20.2 us
    unnamed x9, local copies, waits for them, and re-layouts  11.1 us
    dot_general x1, matrix products, local(): jnp.einsum('mtr,mrw->mtw', grads, rows, preferred_element_type=jnp.float32)  9.6 us
  transfers between devices with their start and end apart: 7, of which 4 were waited for; matrix products, arithmetic and copies ran while one was open for 17% of the time, Pallas kernels for 0%

profile of v8, /device:TPU:2, one launch (start us, length us, event | category | flops | bytes accessed | tf_op | source)
XLA Modules:
  0.0 345.6 jit_solution(9871075012595317456)
XLA Ops:
  10.4 20.2 %all_to_all.33 = bf16[1,16,8,1024]{3,1,0,2:T(8,128)(2,1)} all-to-all(bf16[1,16,8,1024]{3,1,0,2:T(8,128)(2,1)S(1)} %reshape.131), channel_id=1, replica_groups=mesh['section'=16,'z'=8,'core'=2] {'z'}, dimensions={2} | all-to-all | bytes 524288 | tf_op jit(solution)/shard_map/all_to_all | solution.py:33
  32.9 5.0 %gather_fusion.1 = bf16[8,512,512]{2,1,0:T(8,128)(2,1)} fusion(bf16[8,512,512]{2,1,0:T(8,128)(2,1)} %bitcast.87, s32[1024]{0:T(1024)S(1)} %pad_clamp_fusion), kind=kCustom, calls=%fused_computation.1.clone | custom fusion | bytes 8388640 | tf_op jit(solution)/shard_map/jit(_take)/gather | solution.py:37
  37.9 4.8 %broadcast_select_fusion = bf16[8,512,512]{2,1,0:T(8,128)(2,1)} fusion(bf16[8,512,512]{2,1,0:T(8,128)(2,1)} %gather_fusion.1, pred[8]{0:T(512)(128)(4,1)S(1)} %compare_and_fusion), kind=kLoop, calls=%fused_computation.8 | loop fusion | flops 2097152 | bytes 8388616 | tf_op jit(solution)/shard_map/jit(_take)/select_n | solution.py:37
  42.8 5.0 %gather_fusion = bf16[8,512,512]{2,1,0:T(8,128)(2,1)} fusion(bf16[8,512,512]{2,1,0:T(8,128)(2,1)} %bitcast.88, s32[1024]{0:T(1024)S(1)} %pad_clamp_fusion.1), kind=kCustom, calls=%fused_computation.clone | custom fusion | bytes 8388640 | tf_op jit(solution)/shard_map/jit(_take)/gather | solution.py:36
  51.0 23.8 %all-gather.3 = f32[16,3,256]{2,1,0:T(4,128)S(1)} all-gather(f32[1,3,256]{2,1,0:T(4,128)S(1)} %maximum_bitcast_fusion), channel_id=2, replica_groups=mesh['section'=16,'z'=8,'core'=2] {'section'}, dimensions={0}, use_global_device_ids=true | all-gather | bytes 52224 | tf_op jit(solution)/shard_map/all_gather | solution.py:55
  74.9 4.7 %broadcast_select_fusion.1 = bf16[8,512,512]{2,1,0:T(8,128)(2,1)} fusion(bf16[8,512,512]{2,1,0:T(8,128)(2,1)} %gather_fusion, pred[8]{0:T(512)(128)(4,1)S(1)} %compare_and_fusion.1), kind=kLoop, calls=%fused_computation.9 | loop fusion | flops 2097152 | bytes 8388616 | tf_op jit(solution)/shard_map/jit(_take)/select_n | solution.py:36
  79.5 4.3 %all-gather.10.cloned.1.call-done = bf16[8,1,256,1,1024]{4,2,0,3,1:T(8,128)(2,1)} async-done(((bf16[8,1,16,1,1024]{4,2,0,3,1:T(8,128)(2,1)}), bf16[8,1,256,1,1024]{4,2,0,3,1:T(8,128)(2,1)}) %all-gather.10.cloned.1.call-update) | async-done | bytes 4194320 | tf_op jit(solution)/shard_map/all_gather | solution.py:34
  83.8 9.0 %fusion.2 = f32[8,256,512]{2,1,0:T(8,128)} fusion(bf16[8,256,1024]{2,1,0:T(8,128)(2,1)} %bitcast.89, bf16[8,512,512]{2,1,0:T(8,128)(2,1)} %collective-permute-done, bf16[8,512,512]{2,1,0:T(8,128)(2,1)} %broadcast_select_fusion.1), kind=kOutput, calls=%fused_computation.6 | convolution fusion | flops 2164260864 | bytes 16777216 | tf_op jit(solution)/shard_map/mtw,mrw->mtr/dot_general | solution.py:60
  94.3 53.9 %reduce-scatter.3.cloned.1.call-done = f32[1,256,512]{2,1,0:T(8,128)} async-done(((f32[8,256,512]{2,1,0:T(8,128)}), f32[1,256,512]{2,1,0:T(8,128)}) %reduce-scatter.3.cloned.1.call-update) | async-done | bytes 524304 | tf_op jit(solution)/shard_map/reduce_scatter | solution.py:61
  152.0 23.0 %all-gather.4 = f32[16,2,256]{2,1,0:T(2,128)S(1)} all-gather(f32[1,2,256]{2,1,0:T(2,128)S(1)} %maximum_bitcast_fusion.1), channel_id=4, replica_groups=mesh['section'=16,'z'=8,'core'=2] {'section'}, dimensions={0}, use_global_device_ids=true | all-gather | bytes 34816 | tf_op jit(solution)/shard_map/all_gather | solution.py:64
  175.1 2.8 fusion.15
  177.9 38.3 %all-gather.8.cloned.1.call-done = bf16[8,256,512]{2,1,0:T(8,128)(2,1)} async-done(((bf16[1,256,512]{2,1,0:T(8,128)(2,1)}), bf16[8,256,512]{2,1,0:T(8,128)(2,1)}) %all-gather.8.cloned.1.call-update) | async-done | bytes 2097168 | tf_op jit(solution)/shard_map/all_gather | solution.py:72
  216.2 9.6 %fusion.1 = f32[8,256,1024]{2,1,0:T(8,128)} fusion(bf16[8,256,512]{2,1,0:T(8,128)(2,1)} %all-gather.8.cloned.1.call-done, bf16[8,512,512]{2,1,0:T(8,128)(2,1)} %collective-permute-done, bf16[8,512,512]{2,1,0:T(8,128)(2,1)} %broadcast_select_fusion.1), kind=kOutput, calls=%fused_computation.5 | convolution fusion | flops 2164260864 | bytes 18874368 | tf_op jit(solution)/shard_map/mtr,mrw->mtw/dot_general | solution.py:74
  225.8 1.6 copy-done
  227.4 4.9 %convolution_convert_fusion = bf16[8,512,512]{2,1,0:T(8,128)(2,1)} fusion(bf16[8,256,512]{2,1,0:T(8,128)(2,1)S(1)} %copy-done, bf16[8,256,1024]{2,1,0:T(8,128)(2,1)} %bitcast.90), kind=kOutput, calls=%fused_computation.10 | convolution fusion | flops 1075838976 | bytes 8388608 | tf_op jit(solution)/shard_map/mtr,mtw->mrw/dot_general | solution.py:76
  232.6 2.9 convert_bitcast_fusion
  235.5 2.4 copy.40
  237.9 4.0 %fusion.23 = f32[8,262144]{1,0:T(8,128)} fusion(bf16[8,262144]{1,0:T(8,128)(2,1)S(1)} %bitcast.86, bf16[8,2,8]{2,0,1:T(8,128)(2,1)S(1)} %select_convert_fusion, s32[]{:T(128)S(6)} %select_n.134), kind=kOutput, calls=%fused_computation.53 | convolution fusion | flops 33554432 | bytes 12584964 | tf_op jit(solution)/shard_map/dot_general | solution.py:98
  242.0 6.7 %copy.41 = bf16[1,8,512,512]{3,1,2,0:T(8,128)(2,1)} copy(bf16[1,8,512,512]{3,2,1,0:T(8,128)(2,1)} %bitcast.32) | data formatting | bytes 8388608
  248.6 66.0 %reduce-scatter.5.cloned.1.call-done = f32[8,16,1024]{2,1,0:T(8,128)} async-done(((f32[8,256,1024]{2,1,0:T(8,128)}), f32[8,16,1024]{2,1,0:T(8,128)}) %reduce-scatter.5.cloned.1.call-update) | async-done | bytes 524304 | tf_op jit(solution)/shard_map/reduce_scatter | solution.py:84
  314.6 1.8 convert_bitcast_fusion.2
  316.4 7.1 %all-to-all-start.1 = ((bf16[8,16,1,1024]{3,1,2,0:T(8,128)(2,1)}), bf16[8,16,1,1024]{3,1,2,0:T(8,128)(2,1)S(1)}, u32[]{:S(2)}, u32[]{:S(2)}) async-start(bf16[8,16,1,1024]{3,1,2,0:T(8,128)(2,1)} %convert_bitcast_fusion.2), calls=%async_computation.3 | async-start | bytes 524288 | tf_op jit(solution)/shard_map/all_to_all | solution.py:85
  323.5 6.8 %fusion = bf16[8,262144]{1,0:T(8,128)(2,1)} fusion(f32[8,262144]{1,0:T(8,128)} %fusion.23, bf16[8,262144]{1,0:T(8,128)(2,1)} %bitcast.85, bf16[8,2,8]{2,0,1:T(8,128)(2,1)S(1)} %select_convert_fusion, s32[]{:T(128)S(6)} %select_n.135), kind=kOutput, calls=%fused_computation.3 | convolution fusion | flops 37748736 | bytes 16779268 | tf_op jit(solution)/shard_map/dot_general | solution.py:100
  330.2 6.1 %reshape.138 = bf16[4096,512]{1,0:T(8,128)(2,1)} reshape(bf16[8,262144]{1,0:T(8,128)(2,1)} %fusion) | data formatting | bytes 8388608 | tf_op jit(solution)/shard_map/reshape | solution.py:101
  (62 shorter events, 15.9 us)
Async XLA Ops:
  7.2 76.6 %all-gather.10.cloned.1.call-start = ((), (), s32[]{:S(2)}) async-start(), calls=%async_computation.7 | async-start | bytes 4456448 | tf_op jit(solution)/shard_map/all_gather | solution.py:34
  30.7 117.5 %reduce-scatter.3.cloned.1.call-start = ((), (), s32[]{:S(2)}) async-start(), calls=%async_computation.4 | async-start | bytes 4718592 | tf_op jit(solution)/shard_map/reduce_scatter | solution.py:61
  42.7 41.1 %collective-permute-start = (bf16[8,512,512]{2,1,0:T(8,128)(2,1)}, bf16[8,512,512]{2,1,0:T(8,128)(2,1)}, u32[]{:S(2)}, u32[]{:S(2)}) collective-permute-start(bf16[8,512,512]{2,1,0:T(8,128)(2,1)} %broadcast_select_fusion), channel_id=1, source_target_pairs={{0,1},{1,0},{2,3},{3,2},{4,5},{5,4},{6,7},{7,6},{8,9},{9,8},{10,11... | collective-permute-start | bytes 12582920 | tf_op jit(solution)/shard_map/ppermute | solution.py:37
  42.8 5.0 %copy-start.2 = (s32[16,1]{0,1:T(1,128)S(1)}, s32[16,1]{0,1:T(1,128)}, u32[]{:S(2)}) copy-start(s32[16,1]{0,1:T(1,128)} %param.10) | copy-start | bytes 196
  42.8 6.4 %copy-start.1 = (bf16[1,256,512]{2,1,0:T(8,128)(2,1)S(1)}, bf16[1,256,512]{2,1,0:T(8,128)(2,1)}, u32[]{:S(2)}) copy-start(bf16[1,256,512]{2,1,0:T(8,128)(2,1)} %param.11) | copy-start | bytes 786436
  92.9 123.3 %all-gather.8.cloned.1.call-start = ((), (), s32[]{:S(2)}) async-start(), calls=%async_computation.5 | async-start | bytes 2359296 | tf_op jit(solution)/shard_map/all_gather | solution.py:72
  177.8 136.8 %reduce-scatter.5.cloned.1.call-start = ((), (), s32[]{:S(2)}) async-start(), calls=%async_computation.6 | async-start | bytes 8912896 | tf_op jit(solution)/shard_map/reduce_scatter | solution.py:84
  225.8 1.6 copy-start
  232.3 9.7 %collective-permute-start.1 = (bf16[8,512,512]{2,1,0:T(8,128)(2,1)}, bf16[8,512,512]{2,1,0:T(8,128)(2,1)}, u32[]{:S(2)}, u32[]{:S(2)}) collective-permute-start(bf16[8,512,512]{2,1,0:T(8,128)(2,1)} %convolution_convert_fusion), channel_id=1, source_target_pairs={{0,1},{1,0},{2,3},{3,2},{4,5},{5,4},{6,7},{7,6},{8,9},{9,8},{10,11... | collective-permute-start | bytes 12582920 | tf_op jit(solution)/shard_map/ppermute | solution.py:79
  316.4 19.9 %all-to-all-start.1 = ((bf16[8,16,1,1024]{3,1,2,0:T(8,128)(2,1)}), bf16[8,16,1,1024]{3,1,2,0:T(8,128)(2,1)S(1)}, u32[]{:S(2)}, u32[]{:S(2)}) async-start(bf16[8,16,1,1024]{3,1,2,0:T(8,128)(2,1)} %convert_bitcast_fusion.2), calls=%async_computation.3 | async-start | bytes 524288 | tf_op jit(solution)/shard_map/all_to_all | solution.py:85
Sparse Core Ops, SparseCore 0:
  30.8 52.9 all-gather.9
  93.0 55.0 reduce-scatter.2
  178.0 38.1 all-gather.7
  225.9 88.6 reduce-scatter.4

commit v9 on v8

--- a/solution.py
+++ b/solution.py
@@ -81,12 +81,6 @@
         "mtr,mtw->mrw", grads, hid_w[:, :, :col_width], preferred_element_type=jnp.float32
     ).astype(jnp.bfloat16)
 
-    ghid = lax.psum_scatter(ghid, "section", scatter_dimension=1, tiled=True).astype(jnp.bfloat16)
-    ghid = lax.all_to_all(ghid[:, :, None], "z", split_axis=0, concat_axis=2, tiled=True)
-    ghid = ghid.reshape(tok_local, n_z, n_core, col_width)
-    ghid = jnp.where(odd, ghid[:, :, ::-1, :], ghid)
-    grad_hidden = ghid.reshape(1, tok_local, model_width)
-
     block_range = jnp.arange(blocks, dtype=jnp.int32)[None, :]
     selector = jnp.where(
         (live_flags[:, None] > 0) & (block_ids[:, None] == block_range), 1.0, 0.0
@@ -98,7 +92,16 @@
     grad_head = jnp.dot(
         sel_own.T, contrib_own.reshape(n_own, -1), preferred_element_type=jnp.float32
     ) + jnp.dot(sel_sib.T, contrib_got.reshape(n_own, -1), preferred_element_type=jnp.float32)
-    grad_head = grad_head.astype(jnp.bfloat16).reshape(blocks * block_rows, col_width)
+    grad_head = grad_head.astype(jnp.bfloat16)
+    ghid = lax.psum_scatter(ghid, "section", scatter_dimension=1, tiled=True)
+    ghid, grad_head = lax.optimization_barrier((ghid, grad_head))
+    grad_head = grad_head.reshape(blocks * block_rows, col_width)
+    ghid = ghid.astype(jnp.bfloat16)
+    ghid = lax.all_to_all(ghid[:, :, None], "z", split_axis=0, concat_axis=2, tiled=True)
+    ghid = ghid.reshape(tok_local, n_z, n_core, col_width)
+    ghid = jnp.where(odd, ghid[:, :, ::-1, :], ghid)
+    grad_hidden = ghid.reshape(1, tok_local, model_width)
+
     return (grad_hidden, grad_head)
 
 

time: 347 us -> 344 us (level)
  matrix products: 37.2 us -> 31.2 us
  waiting for transfers between devices: 162 us -> 168 us
    all_to_all x1, waiting for transfers between devices: 0.01 us -> 4.58 us  [local(): lax.all_to_all(ghid[:, :, None], 'z', split_axis=0, concat_axis=2, tiled=...]
  transfers between devices with their start and end apart: 7 -> 7, of which waited for: 4 -> 6; matrix products, arithmetic and copies ran while one was open for 17% -> 15% of each run, Pallas kernels for 0% -> 0%
where the time goes in v9:
time: 344 us; the launch traced here: 343 us
  waiting for transfers between devices  168 us (49%)
  blocking collectives  67.1 us (20%)
  local copies, waits for them, and re-layouts  31.4 us (9%)
  matrix products  31.2 us (9%)
  other arithmetic  22.8 us (7%)
  between operations  15.3 us (4%)
  starting transfers between devices  7.25 us (2%)
    reduce_scatter x1, waiting for transfers between devices, local(): ghid = lax.psum_scatter(ghid, 'section', scatter_dimension=1, tiled=True)  66.9 us
    reduce_scatter x1, waiting for transfers between devices, local(): logits = lax.psum_scatter(part, 'z', scatter_dimension=0, tiled=True)[0]  53.9 us
    all_gather x1, waiting for transfers between devices, local(): grads = lax.all_gather(logit_grad[None], 'z', axis=0, tiled=True)  38.3 us
    all_gather x1, blocking collectives, local(): lax.all_gather(jnp.stack([teach_top_s, teach_sum_s, live_row]), 'section')  23.8 us
    all_gather x1, blocking collectives, local(): stud_all = lax.all_gather(jnp.stack([stud_top_s, stud_sum_s]), 'section')  23 us
    all_to_all x1, blocking collectives, local(): lax.all_to_all(pieces, 'z', split_axis=2, concat_axis=0, tiled=True)  20.2 us
    dot_general x1, matrix products, local(): jnp.einsum('mtr,mrw->mtw', grads, rows, preferred_element_type=jnp.float32)  9.6 us
    dot_general x1, matrix products, local(): jnp.einsum('mtw,mrw->mtr', hid_w, rows, preferred_element_type=jnp.float32)  9.04 us
  transfers between devices with their start and end apart: 7, of which 6 were waited for; matrix products, arithmetic and copies ran while one was open for 15% of the time, Pallas kernels for 0%

profile of v9, /device:TPU:2, one launch (start us, length us, event | category | flops | bytes accessed | tf_op | source)
XLA Modules:
  0.0 343.5 jit_solution(2921128620328112905)
XLA Ops:
  10.4 20.2 %all_to_all.33 = bf16[1,16,8,1024]{3,1,0,2:T(8,128)(2,1)} all-to-all(bf16[1,16,8,1024]{3,1,0,2:T(8,128)(2,1)S(1)} %reshape.131), channel_id=1, replica_groups=mesh['section'=16,'z'=8,'core'=2] {'z'}, dimensions={2} | all-to-all | bytes 524288 | tf_op jit(solution)/shard_map/all_to_all | solution.py:33
  32.9 5.0 %gather_fusion.1 = bf16[8,512,512]{2,1,0:T(8,128)(2,1)} fusion(bf16[8,512,512]{2,1,0:T(8,128)(2,1)} %bitcast.87, s32[1024]{0:T(1024)S(1)} %pad_clamp_fusion), kind=kCustom, calls=%fused_computation.1.clone | custom fusion | bytes 8388640 | tf_op jit(solution)/shard_map/jit(_take)/gather | solution.py:37
  37.9 4.8 %broadcast_select_fusion = bf16[8,512,512]{2,1,0:T(8,128)(2,1)} fusion(bf16[8,512,512]{2,1,0:T(8,128)(2,1)} %gather_fusion.1, pred[8]{0:T(512)(128)(4,1)S(1)} %compare_and_fusion), kind=kLoop, calls=%fused_computation.8 | loop fusion | flops 2097152 | bytes 8388616 | tf_op jit(solution)/shard_map/jit(_take)/select_n | solution.py:37
  42.8 5.0 %gather_fusion = bf16[8,512,512]{2,1,0:T(8,128)(2,1)} fusion(bf16[8,512,512]{2,1,0:T(8,128)(2,1)} %bitcast.88, s32[1024]{0:T(1024)S(1)} %pad_clamp_fusion.1), kind=kCustom, calls=%fused_computation.clone | custom fusion | bytes 8388640 | tf_op jit(solution)/shard_map/jit(_take)/gather | solution.py:36
  51.0 23.8 %all-gather.3 = f32[16,3,256]{2,1,0:T(4,128)S(1)} all-gather(f32[1,3,256]{2,1,0:T(4,128)S(1)} %maximum_bitcast_fusion), channel_id=2, replica_groups=mesh['section'=16,'z'=8,'core'=2] {'section'}, dimensions={0}, use_global_device_ids=true | all-gather | bytes 52224 | tf_op jit(solution)/shard_map/all_gather | solution.py:55
  74.9 4.7 %broadcast_select_fusion.1 = bf16[8,512,512]{2,1,0:T(8,128)(2,1)} fusion(bf16[8,512,512]{2,1,0:T(8,128)(2,1)} %gather_fusion, pred[8]{0:T(512)(128)(4,1)S(1)} %compare_and_fusion.1), kind=kLoop, calls=%fused_computation.9 | loop fusion | flops 2097152 | bytes 8388616 | tf_op jit(solution)/shard_map/jit(_take)/select_n | solution.py:36
  79.5 4.3 %all-gather.10.cloned.1.call-done = bf16[8,1,256,1,1024]{4,2,0,3,1:T(8,128)(2,1)} async-done(((bf16[8,1,16,1,1024]{4,2,0,3,1:T(8,128)(2,1)}), bf16[8,1,256,1,1024]{4,2,0,3,1:T(8,128)(2,1)}) %all-gather.10.cloned.1.call-update) | async-done | bytes 4194320 | tf_op jit(solution)/shard_map/all_gather | solution.py:34
  83.8 9.0 %fusion.2 = f32[8,256,512]{2,1,0:T(8,128)} fusion(bf16[8,256,1024]{2,1,0:T(8,128)(2,1)} %bitcast.89, bf16[8,512,512]{2,1,0:T(8,128)(2,1)} %collective-permute-done, bf16[8,512,512]{2,1,0:T(8,128)(2,1)} %broadcast_select_fusion.1), kind=kOutput, calls=%fused_computation.6 | convolution fusion | flops 2164260864 | bytes 16777216 | tf_op jit(solution)/shard_map/mtw,mrw->mtr/dot_general | solution.py:60
  94.3 53.9 %reduce-scatter.3.cloned.1.call-done = f32[1,256,512]{2,1,0:T(8,128)} async-done(((f32[8,256,512]{2,1,0:T(8,128)}), f32[1,256,512]{2,1,0:T(8,128)}) %reduce-scatter.3.cloned.1.call-update) | async-done | bytes 524304 | tf_op jit(solution)/shard_map/reduce_scatter | solution.py:61
  152.0 23.0 %all-gather.4 = f32[16,2,256]{2,1,0:T(2,128)S(1)} all-gather(f32[1,2,256]{2,1,0:T(2,128)S(1)} %maximum_bitcast_fusion.1), channel_id=4, replica_groups=mesh['section'=16,'z'=8,'core'=2] {'section'}, dimensions={0}, use_global_device_ids=true | all-gather | bytes 34816 | tf_op jit(solution)/shard_map/all_gather | solution.py:64
  175.1 2.8 fusion.15
  177.9 38.3 %all-gather.8.cloned.1.call-done = bf16[8,256,512]{2,1,0:T(8,128)(2,1)} async-done(((bf16[1,256,512]{2,1,0:T(8,128)(2,1)}), bf16[8,256,512]{2,1,0:T(8,128)(2,1)}) %all-gather.8.cloned.1.call-update) | async-done | bytes 2097168 | tf_op jit(solution)/shard_map/all_gather | solution.py:72
  216.2 9.6 %fusion.1 = f32[8,256,1024]{2,1,0:T(8,128)} fusion(bf16[8,256,512]{2,1,0:T(8,128)(2,1)} %all-gather.8.cloned.1.call-done, bf16[8,512,512]{2,1,0:T(8,128)(2,1)} %collective-permute-done, bf16[8,512,512]{2,1,0:T(8,128)(2,1)} %broadcast_select_fusion.1), kind=kOutput, calls=%fused_computation.5 | convolution fusion | flops 2164260864 | bytes 18874368 | tf_op jit(solution)/shard_map/mtr,mrw->mtw/dot_general | solution.py:74
  225.8 1.6 copy-done
  227.4 4.9 %convolution_convert_fusion = bf16[8,512,512]{2,1,0:T(8,128)(2,1)} fusion(bf16[8,256,512]{2,1,0:T(8,128)(2,1)S(1)} %copy-done, bf16[8,256,1024]{2,1,0:T(8,128)(2,1)} %bitcast.90), kind=kOutput, calls=%fused_computation.10 | convolution fusion | flops 1075838976 | bytes 8388608 | tf_op jit(solution)/shard_map/mtr,mtw->mrw/dot_general | solution.py:76
  232.6 2.9 convert_bitcast_fusion
  235.5 2.4 copy.40
  239.8 4.5 %copy.41 = bf16[1,8,512,512]{3,1,2,0:T(8,128)(2,1)S(1)} copy(bf16[1,8,512,512]{3,2,1,0:T(8,128)(2,1)} %bitcast.30) | data formatting | bytes 8388608
  244.3 3.5 %fusion = bf16[8,262144]{1,0:T(8,128)(2,1)} fusion(f32[8,262144]{1,0:T(8,128)S(1)} %fusion.23, bf16[8,262144]{1,0:T(8,128)(2,1)S(1)} %bitcast.85, bf16[8,2,8]{2,0,1:T(8,128)(2,1)S(1)} %select_convert_fusion, s32[]{:T(128)S(6)} %select_n.135), kind=kOutput, calls=%fused_computation.3 | convolution fusion | flops 37748736 | bytes 16779268 | tf_op jit(solution)/shard_map/dot_general | solution.py:94
  247.8 66.9 %reduce-scatter.5.cloned.1.call-done = f32[8,16,1024]{2,1,0:T(8,128)} async-done(((f32[8,256,1024]{2,1,0:T(8,128)}), f32[8,16,1024]{2,1,0:T(8,128)}) %reduce-scatter.5.cloned.1.call-update) | async-done | bytes 524304 | tf_op jit(solution)/shard_map/reduce_scatter | solution.py:96
  314.6 1.8 convert_bitcast_fusion.2
  316.4 7.1 %all-to-all-start.1 = ((bf16[8,16,1,1024]{3,1,2,0:T(8,128)(2,1)}), bf16[8,16,1,1024]{3,1,2,0:T(8,128)(2,1)S(1)}, u32[]{:S(2)}, u32[]{:S(2)}) async-start(bf16[8,16,1,1024]{3,1,2,0:T(8,128)(2,1)} %convert_bitcast_fusion.2), calls=%async_computation.3 | async-start | bytes 524288 | tf_op jit(solution)/shard_map/all_to_all | solution.py:100
  323.5 6.1 %reshape.138 = bf16[4096,512]{1,0:T(8,128)(2,1)} reshape(bf16[8,262144]{1,0:T(8,128)(2,1)} %fusion) | data formatting | bytes 8388608 | tf_op jit(solution)/shard_map/reshape | solution.py:98
  329.6 4.6 %all-to-all-done.1 = bf16[8,16,1,1024]{3,1,2,0:T(8,128)(2,1)S(1)} async-done(((bf16[8,16,1,1024]{3,1,2,0:T(8,128)(2,1)}), bf16[8,16,1,1024]{3,1,2,0:T(8,128)(2,1)S(1)}, u32[]{:S(2)}, u32[]{:S(2)}) %all-to-all-start.1) | async-done | bytes 262176 | tf_op jit(solution)/shard_map/all_to_all | solution.py:100
  (62 shorter events, 17.7 us)
Async XLA Ops:
  7.2 76.6 %all-gather.10.cloned.1.call-start = ((), (), s32[]{:S(2)}) async-start(), calls=%async_computation.7 | async-start | bytes 4456448 | tf_op jit(solution)/shard_map/all_gather | solution.py:34
  30.7 117.5 %reduce-scatter.3.cloned.1.call-start = ((), (), s32[]{:S(2)}) async-start(), calls=%async_computation.4 | async-start | bytes 4718592 | tf_op jit(solution)/shard_map/reduce_scatter | solution.py:61
  42.7 41.1 %collective-permute-start = (bf16[8,512,512]{2,1,0:T(8,128)(2,1)}, bf16[8,512,512]{2,1,0:T(8,128)(2,1)}, u32[]{:S(2)}, u32[]{:S(2)}) collective-permute-start(bf16[8,512,512]{2,1,0:T(8,128)(2,1)} %broadcast_select_fusion), channel_id=1, source_target_pairs={{0,1},{1,0},{2,3},{3,2},{4,5},{5,4},{6,7},{7,6},{8,9},{9,8},{10,11... | collective-permute-start | bytes 12582920 | tf_op jit(solution)/shard_map/ppermute | solution.py:37
  42.8 5.0 %copy-start.2 = (s32[16,1]{0,1:T(1,128)S(1)}, s32[16,1]{0,1:T(1,128)}, u32[]{:S(2)}) copy-start(s32[16,1]{0,1:T(1,128)} %param.10) | copy-start | bytes 196
  42.8 6.4 %copy-start.1 = (bf16[1,256,512]{2,1,0:T(8,128)(2,1)S(1)}, bf16[1,256,512]{2,1,0:T(8,128)(2,1)}, u32[]{:S(2)}) copy-start(bf16[1,256,512]{2,1,0:T(8,128)(2,1)} %param.11) | copy-start | bytes 786436
  92.9 123.3 %all-gather.8.cloned.1.call-start = ((), (), s32[]{:S(2)}) async-start(), calls=%async_computation.5 | async-start | bytes 2359296 | tf_op jit(solution)/shard_map/all_gather | solution.py:72
  177.8 136.8 %reduce-scatter.5.cloned.1.call-start = ((), (), s32[]{:S(2)}) async-start(), calls=%async_computation.6 | async-start | bytes 8912896 | tf_op jit(solution)/shard_map/reduce_scatter | solution.py:96
  225.8 1.6 copy-start
  232.3 7.5 %collective-permute-start.1 = (bf16[8,512,512]{2,1,0:T(8,128)(2,1)}, bf16[8,512,512]{2,1,0:T(8,128)(2,1)}, u32[]{:S(2)}, u32[]{:S(2)}) collective-permute-start(bf16[8,512,512]{2,1,0:T(8,128)(2,1)} %convolution_convert_fusion), channel_id=1, source_target_pairs={{0,1},{1,0},{2,3},{3,2},{4,5},{5,4},{6,7},{7,6},{8,9},{9,8},{10,11... | collective-permute-start | bytes 12582920 | tf_op jit(solution)/shard_map/ppermute | solution.py:79
  316.4 17.8 %all-to-all-start.1 = ((bf16[8,16,1,1024]{3,1,2,0:T(8,128)(2,1)}), bf16[8,16,1,1024]{3,1,2,0:T(8,128)(2,1)S(1)}, u32[]{:S(2)}, u32[]{:S(2)}) async-start(bf16[8,16,1,1024]{3,1,2,0:T(8,128)(2,1)} %convert_bitcast_fusion.2), calls=%async_computation.3 | async-start | bytes 524288 | tf_op jit(solution)/shard_map/all_to_all | solution.py:100
Sparse Core Ops, SparseCore 0:
  30.8 52.9 all-gather.9
  93.0 55.0 reduce-scatter.2
  178.0 38.1 all-gather.7
  225.9 88.6 reduce-scatter.4

commit v10 on v9

--- a/solution.py
+++ b/solution.py
@@ -27,15 +27,14 @@
     own_ids = lax.dynamic_index_in_dim(ids_by, core_at, 1, keepdims=False)
     sib_ids = lax.dynamic_index_in_dim(ids_by, 1 - core_at, 1, keepdims=False)
 
-    pieces = hidden[0].reshape(tok_local, n_z, n_core, col_width)
-    pieces = jnp.where(odd, pieces[:, :, ::-1, :], pieces)
-    pieces = pieces.reshape(1, tok_local, n_z, n_core * col_width)
+    pieces = hidden.reshape(1, tok_local, n_z, n_core * col_width)
     pieces = lax.all_to_all(pieces, "z", split_axis=2, concat_axis=0, tiled=True)
     hid_w = lax.all_gather(pieces, "section", axis=1, tiled=True).reshape(n_z, -1, n_core * col_width)
 
     own_rows = jnp.take(table, own_ids, axis=0)
     sib_rows = lax.ppermute(jnp.take(table, sib_ids, axis=0), "core", swap)
-    rows = jnp.concatenate([own_rows, sib_rows], axis=2)
+    rows = jnp.stack([own_rows, sib_rows], axis=2)
+    rows = jnp.where(odd, rows[:, :, ::-1], rows).reshape(n_z, block_rows, n_core * col_width)
 
     own_live = lax.dynamic_index_in_dim(live_flags, my_replica, 0, keepdims=False) > 0
     teach = teacher[0].astype(jnp.float32)
@@ -74,11 +73,11 @@
     ghid = jnp.einsum("mtr,mrw->mtw", grads, rows, preferred_element_type=jnp.float32)
     ghid, grads = lax.optimization_barrier((ghid, grads))
     contrib_sib = jnp.einsum(
-        "mtr,mtw->mrw", grads, hid_w[:, :, col_width:], preferred_element_type=jnp.float32
+        "mtr,mtw->mrw", grads, lax.dynamic_slice_in_dim(hid_w, (1 - core_at) * col_width, col_width, 2), preferred_element_type=jnp.float32
     ).astype(jnp.bfloat16)
     contrib_got = lax.ppermute(contrib_sib, "core", swap)
     contrib_own = jnp.einsum(
-        "mtr,mtw->mrw", grads, hid_w[:, :, :col_width], preferred_element_type=jnp.float32
+        "mtr,mtw->mrw", grads, lax.dynamic_slice_in_dim(hid_w, core_at * col_width, col_width, 2), preferred_element_type=jnp.float32
     ).astype(jnp.bfloat16)
 
     block_range = jnp.arange(blocks, dtype=jnp.int32)[None, :]
@@ -98,8 +97,6 @@
     grad_head = grad_head.reshape(blocks * block_rows, col_width)
     ghid = ghid.astype(jnp.bfloat16)
     ghid = lax.all_to_all(ghid[:, :, None], "z", split_axis=0, concat_axis=2, tiled=True)
-    ghid = ghid.reshape(tok_local, n_z, n_core, col_width)
-    ghid = jnp.where(odd, ghid[:, :, ::-1, :], ghid)
     grad_hidden = ghid.reshape(1, tok_local, model_width)
 
     return (grad_hidden, grad_head)

time: 344 us -> 355 us (1.032)
  other arithmetic: 22.8 us -> 38.6 us
  waiting for transfers between devices: 168 us -> 159 us
  local copies, waits for them, and re-layouts: 31.4 us -> 35.5 us
    unnamed x3 -> x4, other arithmetic: 1.4 us -> 13.1 us
    another operation x0 -> x2, other arithmetic: none -> 9 us  [local(): rows = jnp.stack([own_rows, sib_rows], axis=2)]
    reshape x2, local copies, waits for them, and re-layouts: 0.35 us -> 8.74 us  [the longest x1 7.77 us: local(): jnp.where(odd, rows[:, :, ::-1], rows)]
    reduce_scatter x1, waiting for transfers between devices: 53.9 us -> 48.3 us  [local(): logits = lax.psum_scatter(part, 'z', scatter_dimension=0, tiled=True)[0]]
    select_n x2 -> x1, other arithmetic: 4.66 us -> 0.01 us  [local(): own_rows = jnp.take(table, own_ids, axis=0)]
    all_gather x1, waiting for transfers between devices: 4.27 us -> 0.01 us  [local(): lax.all_gather(pieces, 'section', axis=1, tiled=True)]
  transfers between devices with their start and end apart: 7 -> 7, of which waited for: 6 -> 5; matrix products, arithmetic and copies ran while one was open for 15% -> 21% of each run, Pallas kernels for 0% -> 0%
where the time goes in v10:
time: 355 us; the launch traced here: 354 us
  waiting for transfers between devices  159 us (45%)
  blocking collectives  67.1 us (19%)
  other arithmetic  38.6 us (11%)
  local copies, waits for them, and re-layouts  35.5 us (10%)
  matrix products  31.1 us (9%)
  between operations  15.3 us (4%)
  starting transfers between devices  7.62 us (2%)
    reduce_scatter x1, waiting for transfers between devices, local(): ghid = lax.psum_scatter(ghid, 'section', scatter_dimension=1, tiled=True)  67 us
    reduce_scatter x1, waiting for transfers between devices, local(): logits = lax.psum_scatter(part, 'z', scatter_dimension=0, tiled=True)[0]  48.3 us
    all_gather x1, waiting for transfers between devices, local(): grads = lax.all_gather(logit_grad[None], 'z', axis=0, tiled=True)  38.1 us
    all_gather x1, blocking collectives, local(): lax.all_gather(jnp.stack([teach_top_s, teach_sum_s, live_row]), 'section')  23.8 us
    all_gather x1, blocking collectives, local(): stud_all = lax.all_gather(jnp.stack([stud_top_s, stud_sum_s]), 'section')  23 us
    all_to_all x1, blocking collectives, local(): lax.all_to_all(pieces, 'z', split_axis=2, concat_axis=0, tiled=True)  20.2 us
    unnamed x4, other arithmetic  13.1 us
    dot_general x1, matrix products, local(): jnp.einsum('mtr,mrw->mtw', grads, rows, preferred_element_type=jnp.float32)  9.58 us
  transfers between devices with their start and end apart: 7, of which 5 were waited for; matrix products, arithmetic and copies ran while one was open for 21% of the time, Pallas kernels for 0%

profile of v10, /device:TPU:2, one launch (start us, length us, event | category | flops | bytes accessed | tf_op | source)
XLA Modules:
  0.0 353.8 jit_solution(12060285375931341920)
XLA Ops:
  8.2 20.2 %all_to_all.33 = bf16[1,16,8,1024]{3,1,0,2:T(8,128)(2,1)} all-to-all(bf16[1,16,8,1024]{3,1,0,2:T(8,128)(2,1)S(1)} %bitcast.103), channel_id=1, replica_groups=mesh['section'=16,'z'=8,'core'=2] {'z'}, dimensions={2} | all-to-all | bytes 524288 | tf_op jit(solution)/shard_map/all_to_all | solution.py:31
  30.7 5.0 %gather_fusion.1 = bf16[8,512,512]{2,1,0:T(8,128)(2,1)} fusion(bf16[8,512,512]{2,1,0:T(8,128)(2,1)} %bitcast.96, s32[1024]{0:T(1024)S(1)} %pad_clamp_fusion), kind=kCustom, calls=%fused_computation.1.clone | custom fusion | bytes 8388640 | tf_op jit(solution)/shard_map/jit(_take)/gather | solution.py:35
  35.7 4.8 %broadcast_select_fusion = bf16[8,512,512]{2,1,0:T(8,128)(2,1)} fusion(bf16[8,512,512]{2,1,0:T(8,128)(2,1)} %gather_fusion.1, pred[8]{0:T(512)(128)(4,1)S(1)} %compare_and_fusion), kind=kLoop, calls=%fused_computation.9 | loop fusion | flops 2097152 | bytes 8388616 | tf_op jit(solution)/shard_map/jit(_take)/select_n | solution.py:35
  40.5 5.0 %gather_fusion = bf16[8,512,512]{2,1,0:T(8,128)(2,1)} fusion(bf16[8,512,512]{2,1,0:T(8,128)(2,1)} %bitcast.97, s32[1024]{0:T(1024)S(1)} %pad_clamp_fusion.1), kind=kCustom, calls=%fused_computation.clone | custom fusion | bytes 8388640 | tf_op jit(solution)/shard_map/jit(_take)/gather | solution.py:34
  48.8 23.8 %all-gather.3 = f32[16,3,256]{2,1,0:T(4,128)S(1)} all-gather(f32[1,3,256]{2,1,0:T(4,128)S(1)} %maximum_bitcast_fusion), channel_id=2, replica_groups=mesh['section'=16,'z'=8,'core'=2] {'section'}, dimensions={0}, use_global_device_ids=true | all-gather | bytes 52224 | tf_op jit(solution)/shard_map/all_gather | solution.py:54
  72.7 2.7 select_bitcast_fusion
  75.4 6.3 %pad_maximum_fusion = bf16[8,512,2,512]{3,1,0,2:T(8,128)(2,1)} fusion(bf16[8,512,1,512]{3,1,0,2:T(8,128)(2,1)} %bitcast.10, bf16[8,512,1,512]{3,1,0,2:T(8,128)(2,1)S(1)} %select_bitcast_fusion), kind=kLoop, calls=%fused_computation.6 | loop fusion | flops 4194304 | bytes 16777216 | tf_op jit(solution)/shard_map/stack | solution.py:36
  81.7 11.7 %fusion.1 = bf16[2,8,64,8,512]{4,3,2,1,0:T(8,128)(2,1)} fusion(bf16[8,512,2,512]{3,1,0,2:T(8,128)(2,1)} %pad_maximum_fusion, pred[]{:T(512)S(6)} %eq.17), kind=kLoop, calls=%fused_computation.5 | loop fusion | flops 4194304 | bytes 16777216
  93.4 7.8 %copy.39 = bf16[2,8,64,8,512]{4,3,0,2,1:T(8,128)(2,1)} copy(bf16[2,8,64,8,512]{4,3,2,1,0:T(8,128)(2,1)} %fusion.1) | data formatting | bytes 16777216 | tf_op jit(solution)/shard_map/reshape | solution.py:37
  101.2 9.1 %fusion.31 = f32[8,256,512]{2,1,0:T(8,128)} fusion(bf16[8,256,1024]{2,1,0:T(8,128)(2,1)} %bitcast.98, bf16[8,512,1024]{2,1,0:T(8,128)(2,1)} %bitcast.92), kind=kOutput, calls=%fused_computation.70 | convolution fusion | flops 2147483648 | bytes 16777216 | tf_op jit(solution)/shard_map/mtw,mrw->mtr/dot_general | solution.py:59
  111.7 48.3 %reduce-scatter.3.cloned.1.call-done = f32[1,256,512]{2,1,0:T(8,128)} async-done(((f32[8,256,512]{2,1,0:T(8,128)}), f32[1,256,512]{2,1,0:T(8,128)}) %reduce-scatter.3.cloned.1.call-update) | async-done | bytes 524304 | tf_op jit(solution)/shard_map/reduce_scatter | solution.py:60
  163.8 23.0 %all-gather.4 = f32[16,2,256]{2,1,0:T(2,128)S(1)} all-gather(f32[1,2,256]{2,1,0:T(2,128)S(1)} %maximum_bitcast_fusion.1), channel_id=4, replica_groups=mesh['section'=16,'z'=8,'core'=2] {'section'}, dimensions={0}, use_global_device_ids=true | all-gather | bytes 34816 | tf_op jit(solution)/shard_map/all_gather | solution.py:63
  186.9 2.8 fusion.14
  189.9 38.1 %all-gather.8.cloned.1.call-done = bf16[8,256,512]{2,1,0:T(8,128)(2,1)} async-done(((bf16[1,256,512]{2,1,0:T(8,128)(2,1)}), bf16[8,256,512]{2,1,0:T(8,128)(2,1)}) %all-gather.8.cloned.1.call-update) | async-done | bytes 2097168 | tf_op jit(solution)/shard_map/all_gather | solution.py:71
  228.0 9.6 %fusion.32 = f32[8,256,1024]{2,1,0:T(8,128)} fusion(bf16[8,256,512]{2,1,0:T(8,128)(2,1)} %all-gather.8.cloned.1.call-done, bf16[8,512,1024]{2,1,0:T(8,128)(2,1)} %bitcast.93), kind=kOutput, calls=%fused_computation.71 | convolution fusion | flops 2147483648 | bytes 18874368 | tf_op jit(solution)/shard_map/mtr,mrw->mtw/dot_general | solution.py:73
  239.2 4.9 %convolution_convert_fusion = bf16[8,512,512]{2,1,0:T(8,128)(2,1)} fusion(bf16[8,256,512]{2,1,0:T(8,128)(2,1)S(1)} %copy-done, bf16[8,256,1024]{2,1,0:T(8,128)(2,1)} %bitcast.99, s32[]{:T(128)S(6)} %select_n.146), kind=kOutput, calls=%fused_computation.10 | convolution fusion | flops 1075838976 | bytes 8388612 | tf_op jit(solution)/shard_map/mtr,mtw->mrw/dot_general | solution.py:75
  244.5 2.9 convert_bitcast_fusion
  247.4 2.4 copy.40
  251.6 4.5 %copy.41 = bf16[1,8,512,512]{3,1,2,0:T(8,128)(2,1)S(1)} copy(bf16[1,8,512,512]{3,2,1,0:T(8,128)(2,1)} %bitcast.35) | data formatting | bytes 8388608
  256.1 3.4 fusion
  259.5 67.0 %reduce-scatter.5.cloned.1.call-done = f32[8,16,1024]{2,1,0:T(8,128)} async-done(((f32[8,256,1024]{2,1,0:T(8,128)}), f32[8,16,1024]{2,1,0:T(8,128)}) %reduce-scatter.5.cloned.1.call-update) | async-done | bytes 524304 | tf_op jit(solution)/shard_map/reduce_scatter | solution.py:95
  328.3 7.3 %all-to-all-start.1 = ((bf16[8,16,1,1024]{3,1,2,0:T(8,128)(2,1)}), bf16[8,16,1,1024]{3,1,2,0:T(8,128)(2,1)S(1)}, u32[]{:S(2)}, u32[]{:S(2)}) async-start(bf16[8,16,1,1024]{3,1,2,0:T(8,128)(2,1)} %convert_bitcast_fusion.2), calls=%async_computation.3 | async-start | bytes 524288 | tf_op jit(solution)/shard_map/all_to_all | solution.py:99
  335.6 6.1 %reshape.138 = bf16[4096,512]{1,0:T(8,128)(2,1)} reshape(bf16[8,262144]{1,0:T(8,128)(2,1)} %fusion) | data formatting | bytes 8388608 | tf_op jit(solution)/shard_map/reshape | solution.py:97
  341.7 4.6 %all-to-all-done.1 = bf16[8,16,1,1024]{3,1,2,0:T(8,128)(2,1)S(1)} async-done(((bf16[8,16,1,1024]{3,1,2,0:T(8,128)(2,1)}), bf16[8,16,1,1024]{3,1,2,0:T(8,128)(2,1)S(1)}, u32[]{:S(2)}, u32[]{:S(2)}) %all-to-all-start.1) | async-done | bytes 262176 | tf_op jit(solution)/shard_map/all_to_all | solution.py:99
  (58 shorter events, 17.2 us)
Async XLA Ops:
  7.2 94.0 %all-gather.10.cloned.1.call-start = ((), (), s32[]{:S(2)}) async-start(), calls=%async_computation.7 | async-start | bytes 4456448 | tf_op jit(solution)/shard_map/all_gather | solution.py:32
  28.5 131.6 %reduce-scatter.3.cloned.1.call-start = ((), (), s32[]{:S(2)}) async-start(), calls=%async_computation.4 | async-start | bytes 4718592 | tf_op jit(solution)/shard_map/reduce_scatter | solution.py:60
  40.5 34.9 %collective-permute-start = (bf16[8,512,512]{2,1,0:T(8,128)(2,1)}, bf16[8,512,512]{2,1,0:T(8,128)(2,1)}, u32[]{:S(2)}, u32[]{:S(2)}) collective-permute-start(bf16[8,512,512]{2,1,0:T(8,128)(2,1)} %broadcast_select_fusion), channel_id=1, source_target_pairs={{0,1},{1,0},{2,3},{3,2},{4,5},{5,4},{6,7},{7,6},{8,9},{9,8},{10,11... | collective-permute-start | bytes 12582920 | tf_op jit(solution)/shard_map/ppermute | solution.py:35
  40.5 5.0 %copy-start.2 = (s32[16,1]{0,1:T(1,128)S(1)}, s32[16,1]{0,1:T(1,128)}, u32[]{:S(2)}) copy-start(s32[16,1]{0,1:T(1,128)} %param.10) | copy-start | bytes 196
  40.5 6.5 %copy-start.1 = (bf16[1,256,512]{2,1,0:T(8,128)(2,1)S(1)}, bf16[1,256,512]{2,1,0:T(8,128)(2,1)}, u32[]{:S(2)}) copy-start(bf16[1,256,512]{2,1,0:T(8,128)(2,1)} %param.11) | copy-start | bytes 786436
  110.3 117.7 %all-gather.8.cloned.1.call-start = ((), (), s32[]{:S(2)}) async-start(), calls=%async_computation.5 | async-start | bytes 2359296 | tf_op jit(solution)/shard_map/all_gather | solution.py:71
  189.7 136.9 %reduce-scatter.5.cloned.1.call-start = ((), (), s32[]{:S(2)}) async-start(), calls=%async_computation.6 | async-start | bytes 8912896 | tf_op jit(solution)/shard_map/reduce_scatter | solution.py:95
  237.6 1.6 copy-start
  244.1 7.5 %collective-permute-start.1 = (bf16[8,512,512]{2,1,0:T(8,128)(2,1)}, bf16[8,512,512]{2,1,0:T(8,128)(2,1)}, u32[]{:S(2)}, u32[]{:S(2)}) collective-permute-start(bf16[8,512,512]{2,1,0:T(8,128)(2,1)} %convolution_convert_fusion), channel_id=1, source_target_pairs={{0,1},{1,0},{2,3},{3,2},{4,5},{5,4},{6,7},{7,6},{8,9},{9,8},{10,11... | collective-permute-start | bytes 12582920 | tf_op jit(solution)/shard_map/ppermute | solution.py:78
  328.3 18.0 %all-to-all-start.1 = ((bf16[8,16,1,1024]{3,1,2,0:T(8,128)(2,1)}), bf16[8,16,1,1024]{3,1,2,0:T(8,128)(2,1)S(1)}, u32[]{:S(2)}, u32[]{:S(2)}) async-start(bf16[8,16,1,1024]{3,1,2,0:T(8,128)(2,1)} %convert_bitcast_fusion.2), calls=%async_computation.3 | async-start | bytes 524288 | tf_op jit(solution)/shard_map/all_to_all | solution.py:99
Sparse Core Ops, SparseCore 0:
  28.6 52.9 all-gather.9
  110.4 49.5 reduce-scatter.2
  189.8 38.1 all-gather.7
  237.7 88.7 reduce-scatter.4

commit v11 on v9

--- a/solution.py
+++ b/solution.py
@@ -12,7 +12,6 @@
     n_z = lax.axis_size("z")
     n_core = lax.axis_size("core")
     my_replica = z_at * n_core + core_at
-    odd = core_at == 1
     tok_local = hidden.shape[1]
     model_width = hidden.shape[2]
     block_rows = teacher.shape[2]
@@ -27,8 +26,8 @@
     own_ids = lax.dynamic_index_in_dim(ids_by, core_at, 1, keepdims=False)
     sib_ids = lax.dynamic_index_in_dim(ids_by, 1 - core_at, 1, keepdims=False)
 
-    pieces = hidden[0].reshape(tok_local, n_z, n_core, col_width)
-    pieces = jnp.where(odd, pieces[:, :, ::-1, :], pieces)
+    pair_swap = jnp.arange(n_z * n_core, dtype=jnp.int32) ^ core_at
+    pieces = jnp.take(hidden[0].reshape(tok_local, n_z * n_core, col_width), pair_swap, axis=1)
     pieces = pieces.reshape(1, tok_local, n_z, n_core * col_width)
     pieces = lax.all_to_all(pieces, "z", split_axis=2, concat_axis=0, tiled=True)
     hid_w = lax.all_gather(pieces, "section", axis=1, tiled=True).reshape(n_z, -1, n_core * col_width)
@@ -98,8 +97,7 @@
     grad_head = grad_head.reshape(blocks * block_rows, col_width)
     ghid = ghid.astype(jnp.bfloat16)
     ghid = lax.all_to_all(ghid[:, :, None], "z", split_axis=0, concat_axis=2, tiled=True)
-    ghid = ghid.reshape(tok_local, n_z, n_core, col_width)
-    ghid = jnp.where(odd, ghid[:, :, ::-1, :], ghid)
+    ghid = jnp.take(ghid.reshape(tok_local, n_z * n_core, col_width), pair_swap, axis=1)
     grad_hidden = ghid.reshape(1, tok_local, model_width)
 
     return (grad_hidden, grad_head)

time: 344 us -> 342 us (level)
    unnamed x9 -> x12, local copies, waits for them, and re-layouts: 9.03 us -> 10.1 us
where the time goes in v11:
time: 342 us
  waiting for transfers between devices  169 us (49%)
  blocking collectives  67.1 us (20%)
  matrix products  31.2 us (9%)
  local copies, waits for them, and re-layouts  29.9 us (9%)
  other arithmetic  22 us (6%)
  between operations  15.4 us (5%)
  starting transfers between devices  7.17 us (2%)
    reduce_scatter x1, waiting for transfers between devices, local(): ghid = lax.psum_scatter(ghid, 'section', scatter_dimension=1, tiled=True)  66.6 us
    reduce_scatter x1, waiting for transfers between devices, local(): logits = lax.psum_scatter(part, 'z', scatter_dimension=0, tiled=True)[0]  53.8 us
    all_gather x1, waiting for transfers between devices, local(): grads = lax.all_gather(logit_grad[None], 'z', axis=0, tiled=True)  38.3 us
    all_gather x1, blocking collectives, local(): lax.all_gather(jnp.stack([teach_top_s, teach_sum_s, live_row]), 'section')  23.9 us
    all_gather x1, blocking collectives, local(): stud_all = lax.all_gather(jnp.stack([stud_top_s, stud_sum_s]), 'section')  23 us
    all_to_all x1, blocking collectives, local(): lax.all_to_all(pieces, 'z', split_axis=2, concat_axis=0, tiled=True)  20.2 us
    unnamed x12, local copies, waits for them, and re-layouts  10.1 us
    dot_general x1, matrix products, local(): jnp.einsum('mtr,mrw->mtw', grads, rows, preferred_element_type=jnp.float32)  9.6 us
  transfers between devices with their start and end apart: 7, of which 6 were waited for; matrix products, arithmetic and copies ran while one was open for 15% of the time, Pallas kernels for 0%

profile of v11, /device:TPU:2, one launch (start us, length us, event | category | flops | bytes accessed | tf_op | source)
XLA Modules:
  0.0 341.6 jit_solution(4679736815765024859)
XLA Ops:
  9.5 20.2 %all_to_all.33 = bf16[1,16,8,1024]{3,1,0,2:T(8,128)(2,1)} all-to-all(bf16[1,16,8,1024]{3,1,0,2:T(8,128)(2,1)S(1)} %copy.37), channel_id=1, replica_groups=mesh['section'=16,'z'=8,'core'=2] {'z'}, dimensions={2} | all-to-all | bytes 524288 | tf_op jit(solution)/shard_map/all_to_all | solution.py:32
  31.4 5.0 %gather_fusion.2 = bf16[8,512,512]{2,1,0:T(8,128)(2,1)} fusion(bf16[8,512,512]{2,1,0:T(8,128)(2,1)} %bitcast.89, s32[1024]{0:T(1024)S(1)} %pad_clamp_fusion), kind=kCustom, calls=%fused_computation.3.clone | custom fusion | bytes 8388640 | tf_op jit(solution)/shard_map/jit(_take)/gather | solution.py:36
  36.4 4.7 %broadcast_select_fusion = bf16[8,512,512]{2,1,0:T(8,128)(2,1)} fusion(bf16[8,512,512]{2,1,0:T(8,128)(2,1)} %gather_fusion.2, pred[8]{0:T(512)(128)(4,1)S(1)} %compare_and_fusion.1), kind=kLoop, calls=%fused_computation.10 | loop fusion | flops 2097152 | bytes 8388616 | tf_op jit(solution)/shard_map/jit(_take)/select_n | solution.py:36
  41.2 5.0 %gather_fusion.1 = bf16[8,512,512]{2,1,0:T(8,128)(2,1)} fusion(bf16[8,512,512]{2,1,0:T(8,128)(2,1)} %bitcast.90, s32[1024]{0:T(1024)S(1)} %pad_clamp_fusion.1), kind=kCustom, calls=%fused_computation.1.clone | custom fusion | bytes 8388640 | tf_op jit(solution)/shard_map/jit(_take)/gather | solution.py:35
  49.4 23.9 %all-gather.3 = f32[16,3,256]{2,1,0:T(4,128)S(1)} all-gather(f32[1,3,256]{2,1,0:T(4,128)S(1)} %maximum_bitcast_fusion), channel_id=2, replica_groups=mesh['section'=16,'z'=8,'core'=2] {'section'}, dimensions={0}, use_global_device_ids=true | all-gather | bytes 52224 | tf_op jit(solution)/shard_map/all_gather | solution.py:54
  73.3 4.7 %broadcast_select_fusion.1 = bf16[8,512,512]{2,1,0:T(8,128)(2,1)} fusion(bf16[8,512,512]{2,1,0:T(8,128)(2,1)} %gather_fusion.1, pred[8]{0:T(512)(128)(4,1)S(1)} %compare_and_fusion.2), kind=kLoop, calls=%fused_computation.11 | loop fusion | flops 2097152 | bytes 8388616 | tf_op jit(solution)/shard_map/jit(_take)/select_n | solution.py:35
  78.0 5.0 %all-gather.10.cloned.1.call-done = bf16[8,1,256,1,1024]{4,2,0,3,1:T(8,128)(2,1)} async-done(((bf16[8,1,16,1,1024]{4,2,0,3,1:T(8,128)(2,1)}), bf16[8,1,256,1,1024]{4,2,0,3,1:T(8,128)(2,1)}) %all-gather.10.cloned.1.call-update) | async-done | bytes 4194320 | tf_op jit(solution)/shard_map/all_gather | solution.py:33
  82.9 9.0 %fusion.2 = f32[8,256,512]{2,1,0:T(8,128)} fusion(bf16[8,256,1024]{2,1,0:T(8,128)(2,1)} %bitcast.91, bf16[8,512,512]{2,1,0:T(8,128)(2,1)} %collective-permute-done, bf16[8,512,512]{2,1,0:T(8,128)(2,1)} %broadcast_select_fusion.1), kind=kOutput, calls=%fused_computation.8 | convolution fusion | flops 2164260864 | bytes 16777216 | tf_op jit(solution)/shard_map/mtw,mrw->mtr/dot_general | solution.py:59
  93.4 53.8 %reduce-scatter.3.cloned.1.call-done = f32[1,256,512]{2,1,0:T(8,128)} async-done(((f32[8,256,512]{2,1,0:T(8,128)}), f32[1,256,512]{2,1,0:T(8,128)}) %reduce-scatter.3.cloned.1.call-update) | async-done | bytes 524304 | tf_op jit(solution)/shard_map/reduce_scatter | solution.py:60
  151.1 23.0 %all-gather.4 = f32[16,2,256]{2,1,0:T(2,128)S(1)} all-gather(f32[1,2,256]{2,1,0:T(2,128)S(1)} %maximum_bitcast_fusion.1), channel_id=4, replica_groups=mesh['section'=16,'z'=8,'core'=2] {'section'}, dimensions={0}, use_global_device_ids=true | all-gather | bytes 34816 | tf_op jit(solution)/shard_map/all_gather | solution.py:63
  174.2 2.8 fusion.15
  177.0 38.3 %all-gather.8.cloned.1.call-done = bf16[8,256,512]{2,1,0:T(8,128)(2,1)} async-done(((bf16[1,256,512]{2,1,0:T(8,128)(2,1)}), bf16[8,256,512]{2,1,0:T(8,128)(2,1)}) %all-gather.8.cloned.1.call-update) | async-done | bytes 2097168 | tf_op jit(solution)/shard_map/all_gather | solution.py:71
  215.3 9.6 %fusion.1 = f32[8,256,1024]{2,1,0:T(8,128)} fusion(bf16[8,256,512]{2,1,0:T(8,128)(2,1)} %all-gather.8.cloned.1.call-done, bf16[8,512,512]{2,1,0:T(8,128)(2,1)} %collective-permute-done, bf16[8,512,512]{2,1,0:T(8,128)(2,1)} %broadcast_select_fusion.1), kind=kOutput, calls=%fused_computation.7 | convolution fusion | flops 2164260864 | bytes 18874368 | tf_op jit(solution)/shard_map/mtr,mrw->mtw/dot_general | solution.py:73
  224.9 1.6 copy-done
  226.5 4.9 %convolution_convert_fusion = bf16[8,512,512]{2,1,0:T(8,128)(2,1)} fusion(bf16[8,256,512]{2,1,0:T(8,128)(2,1)S(1)} %copy-done, bf16[8,256,1024]{2,1,0:T(8,128)(2,1)} %bitcast.92), kind=kOutput, calls=%fused_computation.12 | convolution fusion | flops 1075838976 | bytes 8388608 | tf_op jit(solution)/shard_map/mtr,mtw->mrw/dot_general | solution.py:75
  231.8 2.9 convert_bitcast_fusion
  234.7 2.4 copy.54
  238.9 4.5 %copy.55 = bf16[1,8,512,512]{3,1,2,0:T(8,128)(2,1)S(1)} copy(bf16[1,8,512,512]{3,2,1,0:T(8,128)(2,1)} %bitcast.34) | data formatting | bytes 8388608
  243.5 3.5 %fusion = bf16[8,262144]{1,0:T(8,128)(2,1)} fusion(f32[8,262144]{1,0:T(8,128)S(1)} %fusion.23, bf16[8,262144]{1,0:T(8,128)(2,1)S(1)} %bitcast.87, bf16[8,2,8]{2,0,1:T(8,128)(2,1)S(1)} %select_convert_fusion, s32[]{:T(128)S(6)} %select_n.128), kind=kOutput, calls=%fused_computation.5 | convolution fusion | flops 37748736 | bytes 16779268 | tf_op jit(solution)/shard_map/dot_general | solution.py:93
  246.9 66.6 %reduce-scatter.5.cloned.1.call-done = f32[8,16,1024]{2,1,0:T(8,128)} async-done(((f32[8,256,1024]{2,1,0:T(8,128)}), f32[8,16,1024]{2,1,0:T(8,128)}) %reduce-scatter.5.cloned.1.call-update) | async-done | bytes 524304 | tf_op jit(solution)/shard_map/reduce_scatter | solution.py:95
  313.5 1.8 convert_bitcast_fusion.2
  315.3 7.0 %all-to-all-start.1 = ((bf16[8,16,1,1024]{3,1,2,0:T(8,128)(2,1)}), bf16[8,16,1,1024]{3,1,2,0:T(8,128)(2,1)S(1)}, u32[]{:S(2)}, u32[]{:S(2)}) async-start(bf16[8,16,1,1024]{3,1,2,0:T(8,128)(2,1)} %convert_bitcast_fusion.2), calls=%async_computation.3 | async-start | bytes 524288 | tf_op jit(solution)/shard_map/all_to_all | solution.py:99
  322.3 6.1 %reshape.143 = bf16[4096,512]{1,0:T(8,128)(2,1)} reshape(bf16[8,262144]{1,0:T(8,128)(2,1)} %fusion) | data formatting | bytes 8388608 | tf_op jit(solution)/shard_map/reshape | solution.py:97
  328.4 4.7 %all-to-all-done.1 = bf16[8,16,1,1024]{3,1,2,0:T(8,128)(2,1)S(1)} async-done(((bf16[8,16,1,1024]{3,1,2,0:T(8,128)(2,1)}), bf16[8,16,1,1024]{3,1,2,0:T(8,128)(2,1)S(1)}, u32[]{:S(2)}, u32[]{:S(2)}) %all-to-all-start.1) | async-done | bytes 262176 | tf_op jit(solution)/shard_map/all_to_all | solution.py:99
  (71 shorter events, 15.4 us)
Async XLA Ops:
  7.2 23.2 %copy-start.2 = (s32[16,1]{0,1:T(1,128)S(1)}, s32[16,1]{0,1:T(1,128)}, u32[]{:S(2)}) copy-start(s32[16,1]{0,1:T(1,128)} %param.11) | copy-start | bytes 196
  7.2 75.8 %all-gather.10.cloned.1.call-start = ((), (), s32[]{:S(2)}) async-start(), calls=%async_computation.7 | async-start | bytes 4456448 | tf_op jit(solution)/shard_map/all_gather | solution.py:33
  29.8 117.5 %reduce-scatter.3.cloned.1.call-start = ((), (), s32[]{:S(2)}) async-start(), calls=%async_computation.4 | async-start | bytes 4718592 | tf_op jit(solution)/shard_map/reduce_scatter | solution.py:60
  41.1 41.8 %collective-permute-start = (bf16[8,512,512]{2,1,0:T(8,128)(2,1)}, bf16[8,512,512]{2,1,0:T(8,128)(2,1)}, u32[]{:S(2)}, u32[]{:S(2)}) collective-permute-start(bf16[8,512,512]{2,1,0:T(8,128)(2,1)} %broadcast_select_fusion), channel_id=1, source_target_pairs={{0,1},{1,0},{2,3},{3,2},{4,5},{5,4},{6,7},{7,6},{8,9},{9,8},{10,11... | collective-permute-start | bytes 12582920 | tf_op jit(solution)/shard_map/ppermute | solution.py:36
  41.1 5.0 %copy-start.3 = (s32[16,1]{0,1:T(1,128)S(1)}, s32[16,1]{0,1:T(1,128)}, u32[]{:S(2)}) copy-start(s32[16,1]{0,1:T(1,128)} %param.12) | copy-start | bytes 196
  41.1 6.4 %copy-start.1 = (bf16[1,256,512]{2,1,0:T(8,128)(2,1)S(1)}, bf16[1,256,512]{2,1,0:T(8,128)(2,1)}, u32[]{:S(2)}) copy-start(bf16[1,256,512]{2,1,0:T(8,128)(2,1)} %param.13) | copy-start | bytes 786436
  92.0 123.3 %all-gather.8.cloned.1.call-start = ((), (), s32[]{:S(2)}) async-start(), calls=%async_computation.5 | async-start | bytes 2359296 | tf_op jit(solution)/shard_map/all_gather | solution.py:71
  177.0 136.5 %reduce-scatter.5.cloned.1.call-start = ((), (), s32[]{:S(2)}) async-start(), calls=%async_computation.6 | async-start | bytes 8912896 | tf_op jit(solution)/shard_map/reduce_scatter | solution.py:95
  224.9 1.6 copy-start
  231.4 7.5 %collective-permute-start.1 = (bf16[8,512,512]{2,1,0:T(8,128)(2,1)}, bf16[8,512,512]{2,1,0:T(8,128)(2,1)}, u32[]{:S(2)}, u32[]{:S(2)}) collective-permute-start(bf16[8,512,512]{2,1,0:T(8,128)(2,1)} %convolution_convert_fusion), channel_id=1, source_target_pairs={{0,1},{1,0},{2,3},{3,2},{4,5},{5,4},{6,7},{7,6},{8,9},{9,8},{10,11... | collective-permute-start | bytes 12582920 | tf_op jit(solution)/shard_map/ppermute | solution.py:78
  315.3 17.8 %all-to-all-start.1 = ((bf16[8,16,1,1024]{3,1,2,0:T(8,128)(2,1)}), bf16[8,16,1,1024]{3,1,2,0:T(8,128)(2,1)S(1)}, u32[]{:S(2)}, u32[]{:S(2)}) async-start(bf16[8,16,1,1024]{3,1,2,0:T(8,128)(2,1)} %convert_bitcast_fusion.2), calls=%async_computation.3 | async-start | bytes 524288 | tf_op jit(solution)/shard_map/all_to_all | solution.py:99
Sparse Core Ops, SparseCore 0:
  29.9 52.9 all-gather.9
  92.1 55.0 reduce-scatter.2
  177.1 38.1 all-gather.7
  225.1 88.3 reduce-scatter.4

commit v12 on v11

--- a/solution.py
+++ b/solution.py
@@ -30,10 +30,12 @@
     pieces = jnp.take(hidden[0].reshape(tok_local, n_z * n_core, col_width), pair_swap, axis=1)
     pieces = pieces.reshape(1, tok_local, n_z, n_core * col_width)
     pieces = lax.all_to_all(pieces, "z", split_axis=2, concat_axis=0, tiled=True)
-    hid_w = lax.all_gather(pieces, "section", axis=1, tiled=True).reshape(n_z, -1, n_core * col_width)
 
     own_rows = jnp.take(table, own_ids, axis=0)
-    sib_rows = lax.ppermute(jnp.take(table, sib_ids, axis=0), "core", swap)
+    for_sib = jnp.take(table, sib_ids, axis=0)
+    pieces, own_rows, for_sib = lax.optimization_barrier((pieces, own_rows, for_sib))
+    hid_w = lax.all_gather(pieces, "section", axis=1, tiled=True).reshape(n_z, -1, n_core * col_width)
+    sib_rows = lax.ppermute(for_sib, "core", swap)
     rows = jnp.concatenate([own_rows, sib_rows], axis=2)
 
     own_live = lax.dynamic_index_in_dim(live_flags, my_replica, 0, keepdims=False) > 0

time: 342 us -> 358 us (1.047)
  blocking collectives: 67.1 us -> 46.7 us
  waiting for transfers between devices: 169 us -> 187 us
  local copies, waits for them, and re-layouts: 29.9 us -> 40.3 us
  starting transfers between devices: 7.17 us -> 15.8 us
    all_to_all x1 -> x0, blocking collectives: 20.2 us -> none  [local(): lax.all_to_all(pieces, 'z', split_axis=2, concat_axis=0, tiled=True)]
    all_gather x1, waiting for transfers between devices: 4.96 us -> 22.8 us  [local(): lax.all_gather(pieces, 'section', axis=1, tiled=True)]
    all_to_all x0 -> x1, starting transfers between devices: none -> 8.47 us  [local(): lax.all_to_all(pieces, 'z', split_axis=2, concat_axis=0, tiled=True)]
    unnamed x12 -> x15, local copies, waits for them, and re-layouts: 10.1 us -> 15.3 us
    concatenate x0 -> x1, local copies, waits for them, and re-layouts: none -> 4.47 us  [local(): rows = jnp.concatenate([own_rows, sib_rows], axis=2)]
  transfers between devices with their start and end apart: 7 -> 8, of which waited for: 6 -> 6; matrix products, arithmetic and copies ran while one was open for 15% -> 16% of each run, Pallas kernels for 0% -> 0%
where the time goes in v12:
time: 358 us; the launch traced here: 357 us
  waiting for transfers between devices  187 us (52%)
  blocking collectives  46.7 us (13%)
  local copies, waits for them, and re-layouts  40.3 us (11%)
  matrix products  31.2 us (9%)
  other arithmetic  21.4 us (6%)
  starting transfers between devices  15.8 us (4%)
  between operations  15.3 us (4%)
    reduce_scatter x1, waiting for transfers between devices, local(): ghid = lax.psum_scatter(ghid, 'section', scatter_dimension=1, tiled=True)  66.7 us
    reduce_scatter x1, waiting for transfers between devices, local(): logits = lax.psum_scatter(part, 'z', scatter_dimension=0, tiled=True)[0]  53.8 us
    all_gather x1, waiting for transfers between devices, local(): grads = lax.all_gather(logit_grad[None], 'z', axis=0, tiled=True)  38.3 us
    all_gather x1, blocking collectives, local(): lax.all_gather(jnp.stack([teach_top_s, teach_sum_s, live_row]), 'section')  23.7 us
    all_gather x1, blocking collectives, local(): stud_all = lax.all_gather(jnp.stack([stud_top_s, stud_sum_s]), 'section')  23 us
    all_gather x1, waiting for transfers between devices, local(): lax.all_gather(pieces, 'section', axis=1, tiled=True)  22.8 us
    unnamed x15, local copies, waits for them, and re-layouts  15.3 us
    dot_general x1, matrix products, local(): jnp.einsum('mtr,mrw->mtw', grads, rows, preferred_element_type=jnp.float32)  9.59 us
  transfers between devices with their start and end apart: 8, of which 6 were waited for; matrix products, arithmetic and copies ran while one was open for 16% of the time, Pallas kernels for 0%

profile of v12, /device:TPU:2, one launch (start us, length us, event | category | flops | bytes accessed | tf_op | source)
XLA Modules:
  0.0 357.3 jit_solution(2563508676691068561)
XLA Ops:
  10.2 8.5 %all-to-all-start = ((bf16[1,16,8,1024]{3,1,0,2:T(8,128)(2,1)}), bf16[1,16,8,1024]{3,1,0,2:T(8,128)(2,1)S(1)}, u32[]{:S(2)}, u32[]{:S(2)}) async-start(bf16[1,16,8,1024]{3,1,0,2:T(8,128)(2,1)} %copy.37), calls=%async_computation | async-start | bytes 524288 | tf_op jit(solution)/shard_map/all_to_all | solution.py:32
  20.2 5.0 %gather_fusion.2 = bf16[8,512,512]{2,1,0:T(8,128)(2,1)} fusion(bf16[8,512,512]{2,1,0:T(8,128)(2,1)} %bitcast.93, s32[1024]{0:T(1024)S(1)} %pad_clamp_fusion), kind=kCustom, calls=%fused_computation.3.clone | custom fusion | bytes 8388640 | tf_op jit(solution)/shard_map/jit(_take)/gather | solution.py:35
  25.2 4.6 %broadcast_select_fusion = bf16[8,512,512]{2,1,0:T(8,128)(2,1)} fusion(bf16[8,512,512]{2,1,0:T(8,128)(2,1)} %gather_fusion.2, pred[8]{0:T(512)(128)(4,1)S(1)} %get-tuple-element.29), kind=kLoop, calls=%fused_computation.7 | loop fusion | flops 2097152 | bytes 8388616 | tf_op jit(solution)/shard_map/jit(_take)/select_n | solution.py:35
  29.8 5.0 %gather_fusion.1 = bf16[8,512,512]{2,1,0:T(8,128)(2,1)} fusion(bf16[8,512,512]{2,1,0:T(8,128)(2,1)} %bitcast.94, s32[1024]{0:T(1024)S(1)} %pad_clamp_fusion.1), kind=kCustom, calls=%fused_computation.1.clone | custom fusion | bytes 8388640 | tf_op jit(solution)/shard_map/jit(_take)/gather | solution.py:34
  34.8 4.7 %broadcast_select_fusion.1 = bf16[8,512,512]{2,1,0:T(8,128)(2,1)} fusion(bf16[8,512,512]{2,1,0:T(8,128)(2,1)} %gather_fusion.1, pred[8]{0:T(512)(128)(4,1)S(1)} %get-tuple-element.30), kind=kLoop, calls=%fused_computation.8 | loop fusion | flops 2097152 | bytes 8388616 | tf_op jit(solution)/shard_map/jit(_take)/select_n | solution.py:34
  43.4 23.7 %all-gather.2 = f32[16,3,256]{2,1,0:T(4,128)S(1)} all-gather(f32[1,3,256]{2,1,0:T(4,128)S(1)} %maximum_bitcast_fusion), channel_id=2, replica_groups=mesh['section'=16,'z'=8,'core'=2] {'section'}, dimensions={0}, use_global_device_ids=true | all-gather | bytes 52224 | tf_op jit(solution)/shard_map/all_gather | solution.py:56
  67.1 4.5 %constant_dynamic-update-slice_fusion.1 = bf16[8,512,1024]{2,1,0:T(8,128)(2,1)} fusion(bf16[8,512,512]{2,1,0:T(8,128)(2,1)} %broadcast_select_fusion.1), kind=kLoop, calls=%fused_computation.48 | loop fusion | bytes 8388608
  71.6 4.5 %constant_dynamic-update-slice_fusion = bf16[8,512,1024]{2,1,0:T(8,128)(2,1)} fusion(bf16[8,512,1024]{2,1,0:T(8,128)(2,1)} %constant_dynamic-update-slice_fusion.1, bf16[8,512,512]{2,1,0:T(8,128)(2,1)} %collective-permute-done), kind=kLoop, calls=%fused_computation.47 | loop fusion | bytes 8388608 | tf_op jit(solution)/shard_map/concatenate | solution.py:39
  76.1 22.8 %all-gather.7.cloned.1.call-done = bf16[8,256,1,1024]{3,1,0,2:T(8,128)(2,1)} async-done(((bf16[8,16,1,1024]{3,1,0,2:T(8,128)(2,1)}), bf16[8,256,1,1024]{3,1,0,2:T(8,128)(2,1)}) %all-gather.7.cloned.1.call-update) | async-done | bytes 4194320 | tf_op jit(solution)/shard_map/all_gather | solution.py:37
  98.9 9.1 %fusion.28 = f32[8,256,512]{2,1,0:T(8,128)} fusion(bf16[8,256,1024]{2,1,0:T(8,128)(2,1)} %bitcast.95, bf16[8,512,1024]{2,1,0:T(8,128)(2,1)} %constant_dynamic-update-slice_fusion), kind=kOutput, calls=%fused_computation.73 | convolution fusion | flops 2147483648 | bytes 16777216 | tf_op jit(solution)/shard_map/mtw,mrw->mtr/dot_general | solution.py:61
  109.4 53.8 %reduce-scatter.3.cloned.1.call-done = f32[1,256,512]{2,1,0:T(8,128)} async-done(((f32[8,256,512]{2,1,0:T(8,128)}), f32[1,256,512]{2,1,0:T(8,128)}) %reduce-scatter.3.cloned.1.call-update) | async-done | bytes 524304 | tf_op jit(solution)/shard_map/reduce_scatter | solution.py:62
  166.8 23.0 %all-gather.3 = f32[16,2,256]{2,1,0:T(2,128)S(1)} all-gather(f32[1,2,256]{2,1,0:T(2,128)S(1)} %maximum_bitcast_fusion.1), channel_id=3, replica_groups=mesh['section'=16,'z'=8,'core'=2] {'section'}, dimensions={0}, use_global_device_ids=true | all-gather | bytes 34816 | tf_op jit(solution)/shard_map/all_gather | solution.py:65
  189.9 2.7 fusion.13
  192.6 38.3 %all-gather.9.cloned.1.call-done = bf16[8,256,512]{2,1,0:T(8,128)(2,1)} async-done(((bf16[1,256,512]{2,1,0:T(8,128)(2,1)}), bf16[8,256,512]{2,1,0:T(8,128)(2,1)}) %all-gather.9.cloned.1.call-update) | async-done | bytes 2097168 | tf_op jit(solution)/shard_map/all_gather | solution.py:73
  230.9 9.6 %fusion.29 = f32[8,256,1024]{2,1,0:T(8,128)} fusion(bf16[8,256,512]{2,1,0:T(8,128)(2,1)} %all-gather.9.cloned.1.call-done, bf16[8,512,1024]{2,1,0:T(8,128)(2,1)} %constant_dynamic-update-slice_fusion), kind=kOutput, calls=%fused_computation.74 | convolution fusion | flops 2147483648 | bytes 18874368 | tf_op jit(solution)/shard_map/mtr,mrw->mtw/dot_general | solution.py:75
  242.1 4.9 %convolution_convert_fusion = bf16[8,512,512]{2,1,0:T(8,128)(2,1)} fusion(bf16[8,256,512]{2,1,0:T(8,128)(2,1)S(1)} %copy-done, bf16[8,256,1024]{2,1,0:T(8,128)(2,1)} %bitcast.96), kind=kOutput, calls=%fused_computation.9 | convolution fusion | flops 1075838976 | bytes 8388608 | tf_op jit(solution)/shard_map/mtr,mtw->mrw/dot_general | solution.py:77
  247.4 2.9 convert_bitcast_fusion
  250.3 2.4 copy.54
  254.5 4.5 %copy.55 = bf16[1,8,512,512]{3,1,2,0:T(8,128)(2,1)S(1)} copy(bf16[1,8,512,512]{3,2,1,0:T(8,128)(2,1)} %bitcast.36) | data formatting | bytes 8388608
  259.1 3.5 fusion
  262.5 66.7 %reduce-scatter.5.cloned.1.call-done = f32[8,16,1024]{2,1,0:T(8,128)} async-done(((f32[8,256,1024]{2,1,0:T(8,128)}), f32[8,16,1024]{2,1,0:T(8,128)}) %reduce-scatter.5.cloned.1.call-update) | async-done | bytes 524304 | tf_op jit(solution)/shard_map/reduce_scatter | solution.py:97
  331.0 7.1 %all-to-all-start.1 = ((bf16[8,16,1,1024]{3,1,2,0:T(8,128)(2,1)}), bf16[8,16,1,1024]{3,1,2,0:T(8,128)(2,1)S(1)}, u32[]{:S(2)}, u32[]{:S(2)}) async-start(bf16[8,16,1,1024]{3,1,2,0:T(8,128)(2,1)} %convert_bitcast_fusion.2), calls=%async_computation.3 | async-start | bytes 524288 | tf_op jit(solution)/shard_map/all_to_all | solution.py:101
  338.0 6.1 %reshape.143 = bf16[4096,512]{1,0:T(8,128)(2,1)} reshape(bf16[8,262144]{1,0:T(8,128)(2,1)} %fusion) | data formatting | bytes 8388608 | tf_op jit(solution)/shard_map/reshape | solution.py:99
  344.1 4.6 %all-to-all-done.1 = bf16[8,16,1,1024]{3,1,2,0:T(8,128)(2,1)S(1)} async-done(((bf16[8,16,1,1024]{3,1,2,0:T(8,128)(2,1)}), bf16[8,16,1,1024]{3,1,2,0:T(8,128)(2,1)S(1)}, u32[]{:S(2)}, u32[]{:S(2)}) %all-to-all-start.1) | async-done | bytes 262176 | tf_op jit(solution)/shard_map/all_to_all | solution.py:101
  (74 shorter events, 19.8 us)
Async XLA Ops:
  7.2 12.1 %copy-start.3 = (s32[16,1]{0,1:T(1,128)S(1)}, s32[16,1]{0,1:T(1,128)}, u32[]{:S(2)}) copy-start(s32[16,1]{0,1:T(1,128)} %param.11) | copy-start | bytes 196
  10.2 29.4 %all-to-all-start = ((bf16[1,16,8,1024]{3,1,0,2:T(8,128)(2,1)}), bf16[1,16,8,1024]{3,1,0,2:T(8,128)(2,1)S(1)}, u32[]{:S(2)}, u32[]{:S(2)}) async-start(bf16[1,16,8,1024]{3,1,0,2:T(8,128)(2,1)} %copy.37), calls=%async_computation | async-start | bytes 524288 | tf_op jit(solution)/shard_map/all_to_all | solution.py:32
  18.7 80.2 %all-gather.7.cloned.1.call-start = ((), (), s32[]{:S(2)}) async-start(), calls=%async_computation.4 | async-start | bytes 4456448 | tf_op jit(solution)/shard_map/all_gather | solution.py:37
  34.8 5.6 %copy-start.4 = (s32[16,1]{0,1:T(1,128)S(1)}, s32[16,1]{0,1:T(1,128)}, u32[]{:S(2)}) copy-start(s32[16,1]{0,1:T(1,128)} %param.12) | copy-start | bytes 196
  34.8 6.2 %copy-start.1 = (bf16[1,256,512]{2,1,0:T(8,128)(2,1)S(1)}, bf16[1,256,512]{2,1,0:T(8,128)(2,1)}, u32[]{:S(2)}) copy-start(bf16[1,256,512]{2,1,0:T(8,128)(2,1)} %param.13) | copy-start | bytes 786436
  39.6 0.7 copy-start.2
  40.3 122.8 %reduce-scatter.3.cloned.1.call-start = ((), (), s32[]{:S(2)}) async-start(), calls=%async_computation.5 | async-start | bytes 4718592 | tf_op jit(solution)/shard_map/reduce_scatter | solution.py:62
  40.3 31.3 %collective-permute-start = (bf16[8,512,512]{2,1,0:T(8,128)(2,1)}, bf16[8,512,512]{2,1,0:T(8,128)(2,1)}, u32[]{:S(2)}, u32[]{:S(2)}) collective-permute-start(bf16[8,512,512]{2,1,0:T(8,128)(2,1)} %broadcast_select_fusion), channel_id=1, source_target_pairs={{0,1},{1,0},{2,3},{3,2},{4,5},{5,4},{6,7},{7,6},{8,9},{9,8},{10,11... | collective-permute-start | bytes 12582920 | tf_op jit(solution)/shard_map/ppermute | solution.py:38
  108.0 123.0 %all-gather.9.cloned.1.call-start = ((), (), s32[]{:S(2)}) async-start(), calls=%async_computation.6 | async-start | bytes 2359296 | tf_op jit(solution)/shard_map/all_gather | solution.py:73
  192.6 136.6 %reduce-scatter.5.cloned.1.call-start = ((), (), s32[]{:S(2)}) async-start(), calls=%async_computation.7 | async-start | bytes 8912896 | tf_op jit(solution)/shard_map/reduce_scatter | solution.py:97
  240.5 1.6 copy-start
  247.0 7.5 %collective-permute-start.1 = (bf16[8,512,512]{2,1,0:T(8,128)(2,1)}, bf16[8,512,512]{2,1,0:T(8,128)(2,1)}, u32[]{:S(2)}, u32[]{:S(2)}) collective-permute-start(bf16[8,512,512]{2,1,0:T(8,128)(2,1)} %convolution_convert_fusion), channel_id=1, source_target_pairs={{0,1},{1,0},{2,3},{3,2},{4,5},{5,4},{6,7},{7,6},{8,9},{9,8},{10,11... | collective-permute-start | bytes 12582920 | tf_op jit(solution)/shard_map/ppermute | solution.py:80
  331.0 17.8 %all-to-all-start.1 = ((bf16[8,16,1,1024]{3,1,2,0:T(8,128)(2,1)}), bf16[8,16,1,1024]{3,1,2,0:T(8,128)(2,1)S(1)}, u32[]{:S(2)}, u32[]{:S(2)}) async-start(bf16[8,16,1,1024]{3,1,2,0:T(8,128)(2,1)} %convert_bitcast_fusion.2), calls=%async_computation.3 | async-start | bytes 524288 | tf_op jit(solution)/shard_map/all_to_all | solution.py:101
Sparse Core Ops, SparseCore 0:
  40.4 58.4 all-gather.6
  108.1 55.0 reduce-scatter.2
  192.7 38.1 all-gather.8
  240.7 88.4 reduce-scatter.4

commit v13 on v11

--- a/solution.py
+++ b/solution.py
@@ -70,7 +70,7 @@
     logit_grad = (block_rows * live_count * (student - teach_prob)).astype(jnp.bfloat16)
     grads = lax.all_gather(logit_grad[None], "z", axis=0, tiled=True)
 
-    ghid = jnp.einsum("mtr,mrw->mtw", grads, rows, preferred_element_type=jnp.float32)
+    ghid = jnp.einsum("mtr,mrw->tmw", grads, rows, preferred_element_type=jnp.float32)
     ghid, grads = lax.optimization_barrier((ghid, grads))
     contrib_sib = jnp.einsum(
         "mtr,mtw->mrw", grads, hid_w[:, :, col_width:], preferred_element_type=jnp.float32
@@ -92,11 +92,11 @@
         sel_own.T, contrib_own.reshape(n_own, -1), preferred_element_type=jnp.float32
     ) + jnp.dot(sel_sib.T, contrib_got.reshape(n_own, -1), preferred_element_type=jnp.float32)
     grad_head = grad_head.astype(jnp.bfloat16)
-    ghid = lax.psum_scatter(ghid, "section", scatter_dimension=1, tiled=True)
+    ghid = lax.psum_scatter(ghid, "section", scatter_dimension=0, tiled=True)
     ghid, grad_head = lax.optimization_barrier((ghid, grad_head))
     grad_head = grad_head.reshape(blocks * block_rows, col_width)
     ghid = ghid.astype(jnp.bfloat16)
-    ghid = lax.all_to_all(ghid[:, :, None], "z", split_axis=0, concat_axis=2, tiled=True)
+    ghid = lax.all_to_all(ghid, "z", split_axis=1, concat_axis=1, tiled=True)
     ghid = jnp.take(ghid.reshape(tok_local, n_z * n_core, col_width), pair_swap, axis=1)
     grad_hidden = ghid.reshape(1, tok_local, model_width)
 

time: 342 us -> 352 us (1.029)
  local copies, waits for them, and re-layouts: 29.9 us -> 39.7 us
    optimization_barrier x0 -> x1, local copies, waits for them, and re-layouts: none -> 8.97 us  [local(): ghid, grads = lax.optimization_barrier((ghid, grads))]
  transfers between devices with their start and end apart: 7 -> 7, of which waited for: 6 -> 6; matrix products, arithmetic and copies ran while one was open for 15% -> 14% of each run, Pallas kernels for 0% -> 0%
where the time goes in v13:
time: 352 us; the launch traced here: 351 us
  waiting for transfers between devices  169 us (48%)
  blocking collectives  67.2 us (19%)
  local copies, waits for them, and re-layouts  39.7 us (11%)
  matrix products  31.6 us (9%)
  other arithmetic  21 us (6%)
  between operations  15.3 us (4%)
  starting transfers between devices  7.23 us (2%)
    reduce_scatter x1, waiting for transfers between devices, local(): ghid = lax.psum_scatter(ghid, 'section', scatter_dimension=0, tiled=True)  67 us
    reduce_scatter x1, waiting for transfers between devices, local(): logits = lax.psum_scatter(part, 'z', scatter_dimension=0, tiled=True)[0]  53.9 us
    all_gather x1, waiting for transfers between devices, local(): grads = lax.all_gather(logit_grad[None], 'z', axis=0, tiled=True)  38.3 us
    all_gather x1, blocking collectives, local(): lax.all_gather(jnp.stack([teach_top_s, teach_sum_s, live_row]), 'section')  23.9 us
    all_gather x1, blocking collectives, local(): stud_all = lax.all_gather(jnp.stack([stud_top_s, stud_sum_s]), 'section')  23 us
    all_to_all x1, blocking collectives, local(): lax.all_to_all(pieces, 'z', split_axis=2, concat_axis=0, tiled=True)  20.2 us
    unnamed x12, local copies, waits for them, and re-layouts  10.1 us
    dot_general x1, matrix products, local(): jnp.einsum('mtr,mrw->tmw', grads, rows, preferred_element_type=jnp.float32)  9.96 us
  transfers between devices with their start and end apart: 7, of which 6 were waited for; matrix products, arithmetic and copies ran while one was open for 14% of the time, Pallas kernels for 0%

profile of v13, /device:TPU:2, one launch (start us, length us, event | category | flops | bytes accessed | tf_op | source)
XLA Modules:
  0.0 351.3 jit_solution(16461049000884046700)
XLA Ops:
  9.5 20.2 %all_to_all.23 = bf16[1,16,8,1024]{3,1,0,2:T(8,128)(2,1)} all-to-all(bf16[1,16,8,1024]{3,1,0,2:T(8,128)(2,1)S(1)} %copy.64), channel_id=1, replica_groups=mesh['section'=16,'z'=8,'core'=2] {'z'}, dimensions={2} | all-to-all | bytes 524288 | tf_op jit(solution)/shard_map/all_to_all | solution.py:32
  31.4 5.0 %gather_fusion.1 = bf16[8,512,512]{2,1,0:T(8,128)(2,1)} fusion(bf16[8,512,512]{2,1,0:T(8,128)(2,1)} %bitcast.80, s32[1024]{0:T(1024)S(1)} %pad_clamp_fusion.1), kind=kCustom, calls=%fused_computation.2.clone | custom fusion | bytes 8388640 | tf_op jit(solution)/shard_map/jit(_take)/gather | solution.py:36
  36.4 4.7 %broadcast_select_fusion = bf16[8,512,512]{2,1,0:T(8,128)(2,1)} fusion(bf16[8,512,512]{2,1,0:T(8,128)(2,1)} %gather_fusion.1, pred[8]{0:T(512)(128)(4,1)S(1)} %compare_and_fusion.1), kind=kLoop, calls=%fused_computation.10 | loop fusion | flops 2097152 | bytes 8388616 | tf_op jit(solution)/shard_map/jit(_take)/select_n | solution.py:36
  41.2 5.0 %gather_fusion = bf16[8,512,512]{2,1,0:T(8,128)(2,1)} fusion(bf16[8,512,512]{2,1,0:T(8,128)(2,1)} %bitcast.81, s32[1024]{0:T(1024)S(1)} %pad_clamp_fusion.2), kind=kCustom, calls=%fused_computation.clone | custom fusion | bytes 8388640 | tf_op jit(solution)/shard_map/jit(_take)/gather | solution.py:35
  49.2 23.9 %all-gather.3 = f32[16,3,256]{2,1,0:T(4,128)S(1)} all-gather(f32[1,3,256]{2,1,0:T(4,128)S(1)} %maximum_bitcast_fusion), channel_id=2, replica_groups=mesh['section'=16,'z'=8,'core'=2] {'section'}, dimensions={0}, use_global_device_ids=true | all-gather | bytes 52224 | tf_op jit(solution)/shard_map/all_gather | solution.py:54
  73.2 4.7 %broadcast_select_fusion.1 = bf16[8,512,512]{2,1,0:T(8,128)(2,1)} fusion(bf16[8,512,512]{2,1,0:T(8,128)(2,1)} %gather_fusion, pred[8]{0:T(512)(128)(4,1)S(1)} %compare_and_fusion.2), kind=kLoop, calls=%fused_computation.11 | loop fusion | flops 2097152 | bytes 8388616 | tf_op jit(solution)/shard_map/jit(_take)/select_n | solution.py:35
  77.9 5.0 %all-gather.10.cloned.1.call-done = bf16[8,1,256,1,1024]{4,2,0,3,1:T(8,128)(2,1)} async-done(((bf16[8,1,16,1,1024]{4,2,0,3,1:T(8,128)(2,1)}), bf16[8,1,256,1,1024]{4,2,0,3,1:T(8,128)(2,1)}) %all-gather.10.cloned.1.call-update) | async-done | bytes 4194320 | tf_op jit(solution)/shard_map/all_gather | solution.py:33
  82.9 9.0 %fusion.2 = f32[8,256,512]{2,1,0:T(8,128)} fusion(bf16[8,256,1024]{2,1,0:T(8,128)(2,1)} %bitcast.82, bf16[8,512,512]{2,1,0:T(8,128)(2,1)} %collective-permute-done, bf16[8,512,512]{2,1,0:T(8,128)(2,1)} %broadcast_select_fusion.1), kind=kOutput, calls=%fused_computation.8 | convolution fusion | flops 2164260864 | bytes 16777216 | tf_op jit(solution)/shard_map/mtw,mrw->mtr/dot_general | solution.py:59
  93.4 53.9 %reduce-scatter.3.cloned.1.call-done = f32[1,256,512]{2,1,0:T(8,128)} async-done(((f32[8,256,512]{2,1,0:T(8,128)}), f32[1,256,512]{2,1,0:T(8,128)}) %reduce-scatter.3.cloned.1.call-update) | async-done | bytes 524304 | tf_op jit(solution)/shard_map/reduce_scatter | solution.py:60
  151.0 23.0 %all-gather.4 = f32[16,2,256]{2,1,0:T(2,128)S(1)} all-gather(f32[1,2,256]{2,1,0:T(2,128)S(1)} %maximum_bitcast_fusion.1), channel_id=4, replica_groups=mesh['section'=16,'z'=8,'core'=2] {'section'}, dimensions={0}, use_global_device_ids=true | all-gather | bytes 34816 | tf_op jit(solution)/shard_map/all_gather | solution.py:63
  174.0 2.7 fusion.16
  176.8 38.3 %all-gather.8.cloned.1.call-done = bf16[8,256,512]{2,1,0:T(8,128)(2,1)} async-done(((bf16[1,256,512]{2,1,0:T(8,128)(2,1)}), bf16[8,256,512]{2,1,0:T(8,128)(2,1)}) %all-gather.8.cloned.1.call-update) | async-done | bytes 2097168 | tf_op jit(solution)/shard_map/all_gather | solution.py:71
  215.1 10.0 %fusion.3 = f32[256,8,1024]{0,2,1:T(8,128)} fusion(bf16[8,256,512]{2,1,0:T(8,128)(2,1)} %all-gather.8.cloned.1.call-done, bf16[8,512,512]{2,1,0:T(8,128)(2,1)} %collective-permute-done, bf16[8,512,512]{2,1,0:T(8,128)(2,1)} %broadcast_select_fusion.1), kind=kOutput, calls=%fused_computation.12 | convolution fusion | flops 2164260864 | bytes 18874368 | tf_op jit(solution)/shard_map/mtr,mrw->tmw/dot_general | solution.py:73
  225.1 9.0 %copy.68 = f32[256,8,1024]{2,1,0:T(8,128)} copy(f32[256,8,1024]{0,2,1:T(8,128)} %fusion.3) | data formatting | bytes 16777216 | tf_op jit(solution)/shard_map/optimization_barrier | solution.py:74
  234.1 1.6 copy-done
  235.6 4.9 %convolution_convert_fusion = bf16[8,512,512]{2,1,0:T(8,128)(2,1)} fusion(bf16[8,256,512]{2,1,0:T(8,128)(2,1)S(1)} %copy-done, bf16[8,256,1024]{2,1,0:T(8,128)(2,1)} %bitcast.83), kind=kOutput, calls=%fused_computation.13 | convolution fusion | flops 1075838976 | bytes 8388608 | tf_op jit(solution)/shard_map/mtr,mtw->mrw/dot_general | solution.py:75
  240.9 2.9 convert_bitcast_fusion
  243.8 2.4 copy.84
  248.0 4.5 %copy.85 = bf16[1,8,512,512]{3,1,2,0:T(8,128)(2,1)S(1)} copy(bf16[1,8,512,512]{3,2,1,0:T(8,128)(2,1)} %bitcast.29) | data formatting | bytes 8388608
  252.6 3.5 fusion
  256.1 67.0 %reduce-scatter.5.cloned.1.call-done = f32[16,8,1024]{2,1,0:T(8,128)} async-done(((f32[256,8,1024]{2,1,0:T(8,128)}), f32[16,8,1024]{2,1,0:T(8,128)}) %reduce-scatter.5.cloned.1.call-update) | async-done | bytes 524304 | tf_op jit(solution)/shard_map/reduce_scatter | solution.py:95
  325.0 7.1 %all-to-all-start.1 = ((bf16[16,8,1024]{2,0,1:T(8,128)(2,1)}), bf16[16,8,1024]{2,0,1:T(8,128)(2,1)S(1)}, u32[]{:S(2)}, u32[]{:S(2)}) async-start(bf16[16,8,1024]{2,0,1:T(8,128)(2,1)} %copy.73), calls=%async_computation.3 | async-start | bytes 524288 | tf_op jit(solution)/shard_map/all_to_all | solution.py:99
  332.0 6.1 %reshape.142 = bf16[4096,512]{1,0:T(8,128)(2,1)} reshape(bf16[8,262144]{1,0:T(8,128)(2,1)} %fusion) | data formatting | bytes 8388608 | tf_op jit(solution)/shard_map/reshape | solution.py:97
  338.1 4.6 %all-to-all-done.1 = bf16[16,8,1024]{2,0,1:T(8,128)(2,1)S(1)} async-done(((bf16[16,8,1024]{2,0,1:T(8,128)(2,1)}), bf16[16,8,1024]{2,0,1:T(8,128)(2,1)S(1)}, u32[]{:S(2)}, u32[]{:S(2)}) %all-to-all-start.1) | async-done | bytes 262176 | tf_op jit(solution)/shard_map/all_to_all | solution.py:99
  (73 shorter events, 17.0 us)
Async XLA Ops:
  7.2 23.2 %copy-start.2 = (s32[16,1]{0,1:T(1,128)S(1)}, s32[16,1]{0,1:T(1,128)}, u32[]{:S(2)}) copy-start(s32[16,1]{0,1:T(1,128)} %param.11) | copy-start | bytes 196
  7.2 75.7 %all-gather.10.cloned.1.call-start = ((), (), s32[]{:S(2)}) async-start(), calls=%async_computation.7 | async-start | bytes 4456448 | tf_op jit(solution)/shard_map/all_gather | solution.py:33
  29.8 117.4 %reduce-scatter.3.cloned.1.call-start = ((), (), s32[]{:S(2)}) async-start(), calls=%async_computation.4 | async-start | bytes 4718592 | tf_op jit(solution)/shard_map/reduce_scatter | solution.py:60
  41.1 41.8 %collective-permute-start = (bf16[8,512,512]{2,1,0:T(8,128)(2,1)}, bf16[8,512,512]{2,1,0:T(8,128)(2,1)}, u32[]{:S(2)}, u32[]{:S(2)}) collective-permute-start(bf16[8,512,512]{2,1,0:T(8,128)(2,1)} %broadcast_select_fusion), channel_id=1, source_target_pairs={{0,1},{1,0},{2,3},{3,2},{4,5},{5,4},{6,7},{7,6},{8,9},{9,8},{10,11... | collective-permute-start | bytes 12582920 | tf_op jit(solution)/shard_map/ppermute | solution.py:36
  41.1 5.0 %copy-start.3 = (s32[16,1]{0,1:T(1,128)S(1)}, s32[16,1]{0,1:T(1,128)}, u32[]{:S(2)}) copy-start(s32[16,1]{0,1:T(1,128)} %param.12) | copy-start | bytes 196
  41.1 6.4 %copy-start.1 = (bf16[1,256,512]{2,1,0:T(8,128)(2,1)S(1)}, bf16[1,256,512]{2,1,0:T(8,128)(2,1)}, u32[]{:S(2)}) copy-start(bf16[1,256,512]{2,1,0:T(8,128)(2,1)} %param.13) | copy-start | bytes 786436
  92.0 123.1 %all-gather.8.cloned.1.call-start = ((), (), s32[]{:S(2)}) async-start(), calls=%async_computation.5 | async-start | bytes 2359296 | tf_op jit(solution)/shard_map/all_gather | solution.py:71
  176.8 146.2 %reduce-scatter.5.cloned.1.call-start = ((), (), s32[]{:S(2)}) async-start(), calls=%async_computation.6 | async-start | bytes 8912896 | tf_op jit(solution)/shard_map/reduce_scatter | solution.py:95
  234.0 1.6 copy-start
  240.5 7.5 %collective-permute-start.1 = (bf16[8,512,512]{2,1,0:T(8,128)(2,1)}, bf16[8,512,512]{2,1,0:T(8,128)(2,1)}, u32[]{:S(2)}, u32[]{:S(2)}) collective-permute-start(bf16[8,512,512]{2,1,0:T(8,128)(2,1)} %convolution_convert_fusion), channel_id=1, source_target_pairs={{0,1},{1,0},{2,3},{3,2},{4,5},{5,4},{6,7},{7,6},{8,9},{9,8},{10,11... | collective-permute-start | bytes 12582920 | tf_op jit(solution)/shard_map/ppermute | solution.py:78
  325.0 17.7 %all-to-all-start.1 = ((bf16[16,8,1024]{2,0,1:T(8,128)(2,1)}), bf16[16,8,1024]{2,0,1:T(8,128)(2,1)S(1)}, u32[]{:S(2)}, u32[]{:S(2)}) async-start(bf16[16,8,1024]{2,0,1:T(8,128)(2,1)} %copy.73), calls=%async_computation.3 | async-start | bytes 524288 | tf_op jit(solution)/shard_map/all_to_all | solution.py:99
Sparse Core Ops, SparseCore 0:
  29.9 52.9 all-gather.9
  92.1 55.0 reduce-scatter.2
  176.9 38.1 all-gather.7
  234.2 88.7 reduce-scatter.4

commit v14 on v11

--- a/solution.py
+++ b/solution.py
@@ -55,6 +55,10 @@
     teach_all, hid_w = lax.optimization_barrier((teach_all, hid_w))
     teach_top, teach_total = merged(teach_all[:, 0], teach_all[:, 1])
     live_count = jnp.sum(teach_all[:, 2, 0])
+    teach_prob = jnp.where(
+        own_live, jnp.exp(teach - teach_top[:, None]) / teach_total[:, None], 0.0
+    )
+    teach_prob = lax.optimization_barrier(teach_prob)
 
     part = jnp.einsum("mtw,mrw->mtr", hid_w, rows, preferred_element_type=jnp.float32)
     logits = lax.psum_scatter(part, "z", scatter_dimension=0, tiled=True)[0]
@@ -64,9 +68,6 @@
     stud_top, stud_total = merged(stud_all[:, 0], stud_all[:, 1])
 
     student = jnp.where(own_live, jnp.exp(logits - stud_top[:, None]) / stud_total[:, None], 0.0)
-    teach_prob = jnp.where(
-        own_live, jnp.exp(teach - teach_top[:, None]) / teach_total[:, None], 0.0
-    )
     logit_grad = (block_rows * live_count * (student - teach_prob)).astype(jnp.bfloat16)
     grads = lax.all_gather(logit_grad[None], "z", axis=0, tiled=True)
 

time: 342 us -> 343 us (level)
  no operation moved by 1% of the time
where the time goes in v14:
time: 343 us; the launch traced here: 342 us
  waiting for transfers between devices  168 us (49%)
  blocking collectives  67.1 us (20%)
  matrix products  31.2 us (9%)
  local copies, waits for them, and re-layouts  29.9 us (9%)
  other arithmetic  22.7 us (7%)
  between operations  15.4 us (4%)
  starting transfers between devices  7.25 us (2%)
    reduce_scatter x1, waiting for transfers between devices, local(): ghid = lax.psum_scatter(ghid, 'section', scatter_dimension=1, tiled=True)  66.9 us
    reduce_scatter x1, waiting for transfers between devices, local(): logits = lax.psum_scatter(part, 'z', scatter_dimension=0, tiled=True)[0]  53 us
    all_gather x1, waiting for transfers between devices, local(): grads = lax.all_gather(logit_grad[None], 'z', axis=0, tiled=True)  38.3 us
    all_gather x1, blocking collectives, local(): lax.all_gather(jnp.stack([teach_top_s, teach_sum_s, live_row]), 'section')  23.9 us
    all_gather x1, blocking collectives, local(): stud_all = lax.all_gather(jnp.stack([stud_top_s, stud_sum_s]), 'section')  23 us
    all_to_all x1, blocking collectives, local(): lax.all_to_all(pieces, 'z', split_axis=2, concat_axis=0, tiled=True)  20.2 us
    unnamed x12, local copies, waits for them, and re-layouts  10.1 us
    dot_general x1, matrix products, local(): jnp.einsum('mtr,mrw->mtw', grads, rows, preferred_element_type=jnp.float32)  9.6 us
  transfers between devices with their start and end apart: 7, of which 6 were waited for; matrix products, arithmetic and copies ran while one was open for 15% of the time, Pallas kernels for 0%

profile of v14, /device:TPU:2, one launch (start us, length us, event | category | flops | bytes accessed | tf_op | source)
XLA Modules:
  0.0 341.8 jit_solution(1555788812362864932)
XLA Ops:
  9.5 20.2 %all_to_all.33 = bf16[1,16,8,1024]{3,1,0,2:T(8,128)(2,1)} all-to-all(bf16[1,16,8,1024]{3,1,0,2:T(8,128)(2,1)S(1)} %copy.37), channel_id=1, replica_groups=mesh['section'=16,'z'=8,'core'=2] {'z'}, dimensions={2} | all-to-all | bytes 524288 | tf_op jit(solution)/shard_map/all_to_all | solution.py:32
  31.4 5.0 %gather_fusion.2 = bf16[8,512,512]{2,1,0:T(8,128)(2,1)} fusion(bf16[8,512,512]{2,1,0:T(8,128)(2,1)} %bitcast.99, s32[1024]{0:T(1024)S(1)} %pad_clamp_fusion), kind=kCustom, calls=%fused_computation.3.clone | custom fusion | bytes 8388640 | tf_op jit(solution)/shard_map/jit(_take)/gather | solution.py:36
  36.4 4.7 %broadcast_select_fusion = bf16[8,512,512]{2,1,0:T(8,128)(2,1)} fusion(bf16[8,512,512]{2,1,0:T(8,128)(2,1)} %gather_fusion.2, pred[8]{0:T(512)(128)(4,1)S(1)} %compare_and_fusion.1), kind=kLoop, calls=%fused_computation.10 | loop fusion | flops 2097152 | bytes 8388616 | tf_op jit(solution)/shard_map/jit(_take)/select_n | solution.py:36
  41.2 5.0 %gather_fusion.1 = bf16[8,512,512]{2,1,0:T(8,128)(2,1)} fusion(bf16[8,512,512]{2,1,0:T(8,128)(2,1)} %bitcast.100, s32[1024]{0:T(1024)S(1)} %pad_clamp_fusion.1), kind=kCustom, calls=%fused_computation.1.clone | custom fusion | bytes 8388640 | tf_op jit(solution)/shard_map/jit(_take)/gather | solution.py:35
  49.4 23.9 %all-gather.4 = f32[16,3,256]{2,1,0:T(4,128)S(1)} all-gather(f32[1,3,256]{2,1,0:T(4,128)S(1)} %maximum_bitcast_fusion), channel_id=2, replica_groups=mesh['section'=16,'z'=8,'core'=2] {'section'}, dimensions={0}, use_global_device_ids=true | all-gather | bytes 52224 | tf_op jit(solution)/shard_map/all_gather | solution.py:54
  73.3 4.7 %broadcast_select_fusion.1 = bf16[8,512,512]{2,1,0:T(8,128)(2,1)} fusion(bf16[8,512,512]{2,1,0:T(8,128)(2,1)} %gather_fusion.1, pred[8]{0:T(512)(128)(4,1)S(1)} %compare_and_fusion.2), kind=kLoop, calls=%fused_computation.11 | loop fusion | flops 2097152 | bytes 8388616 | tf_op jit(solution)/shard_map/jit(_take)/select_n | solution.py:35
  78.0 5.0 %all-gather.9.cloned.1.call-done = bf16[8,1,256,1,1024]{4,2,0,3,1:T(8,128)(2,1)} async-done(((bf16[8,1,16,1,1024]{4,2,0,3,1:T(8,128)(2,1)}), bf16[8,1,256,1,1024]{4,2,0,3,1:T(8,128)(2,1)}) %all-gather.9.cloned.1.call-update) | async-done | bytes 4194320 | tf_op jit(solution)/shard_map/all_gather | solution.py:33
  82.9 9.0 %fusion.2 = f32[8,256,512]{2,1,0:T(8,128)} fusion(bf16[8,256,1024]{2,1,0:T(8,128)(2,1)} %bitcast.104, bf16[8,512,512]{2,1,0:T(8,128)(2,1)} %collective-permute-done, bf16[8,512,512]{2,1,0:T(8,128)(2,1)} %broadcast_select_fusion.1), kind=kOutput, calls=%fused_computation.8 | convolution fusion | flops 2164260864 | bytes 16777216 | tf_op jit(solution)/shard_map/mtw,mrw->mtr/dot_general | solution.py:63
  94.3 53.0 %reduce-scatter.3.cloned.1.call-done = f32[1,256,512]{2,1,0:T(8,128)} async-done(((f32[8,256,512]{2,1,0:T(8,128)}), f32[1,256,512]{2,1,0:T(8,128)}) %reduce-scatter.3.cloned.1.call-update) | async-done | bytes 524304 | tf_op jit(solution)/shard_map/reduce_scatter | solution.py:64
  151.1 23.0 %all-gather.5 = f32[16,2,256]{2,1,0:T(2,128)S(1)} all-gather(f32[1,2,256]{2,1,0:T(2,128)S(1)} %maximum_bitcast_fusion.1), channel_id=4, replica_groups=mesh['section'=16,'z'=8,'core'=2] {'section'}, dimensions={0}, use_global_device_ids=true | all-gather | bytes 34816 | tf_op jit(solution)/shard_map/all_gather | solution.py:67
  174.2 2.7 fusion.17
  176.9 38.3 %all-gather.11.cloned.1.call-done = bf16[2048,512]{1,0:T(8,128)(2,1)} async-done(((bf16[256,512]{1,0:T(8,128)(2,1)}), bf16[2048,512]{1,0:T(8,128)(2,1)}) %all-gather.11.cloned.1.call-update) | async-done | bytes 2097168 | tf_op jit(solution)/shard_map/all_gather | solution.py:72
  215.2 9.6 %fusion.1 = f32[8,256,1024]{2,1,0:T(8,128)} fusion(bf16[8,256,512]{2,1,0:T(8,128)(2,1)} %bitcast.101, bf16[8,512,512]{2,1,0:T(8,128)(2,1)} %collective-permute-done, bf16[8,512,512]{2,1,0:T(8,128)(2,1)} %broadcast_select_fusion.1), kind=kOutput, calls=%fused_computation.7 | convolution fusion | flops 2164260864 | bytes 18874368 | tf_op jit(solution)/shard_map/mtr,mrw->mtw/dot_general | solution.py:74
  224.8 1.6 copy-done
  226.4 4.9 %convolution_convert_fusion = bf16[8,512,512]{2,1,0:T(8,128)(2,1)} fusion(bf16[8,256,512]{2,1,0:T(8,128)(2,1)S(1)} %bitcast.102, bf16[8,256,1024]{2,1,0:T(8,128)(2,1)} %bitcast.105), kind=kOutput, calls=%fused_computation.12 | convolution fusion | flops 1075838976 | bytes 8388608 | tf_op jit(solution)/shard_map/mtr,mtw->mrw/dot_general | solution.py:76
  231.7 2.9 convert_bitcast_fusion
  234.6 2.4 copy.54
  238.8 4.5 %copy.55 = bf16[1,8,512,512]{3,1,2,0:T(8,128)(2,1)S(1)} copy(bf16[1,8,512,512]{3,2,1,0:T(8,128)(2,1)} %bitcast.36) | data formatting | bytes 8388608
  243.4 3.5 %fusion = bf16[8,262144]{1,0:T(8,128)(2,1)} fusion(f32[8,262144]{1,0:T(8,128)S(1)} %fusion.25, bf16[8,262144]{1,0:T(8,128)(2,1)S(1)} %bitcast.97, bf16[8,2,8]{2,0,1:T(8,128)(2,1)S(1)} %select_convert_fusion, s32[]{:T(128)S(6)} %select_n.126), kind=kOutput, calls=%fused_computation.5 | convolution fusion | flops 37748736 | bytes 16779268 | tf_op jit(solution)/shard_map/dot_general | solution.py:94
  246.8 66.9 %reduce-scatter.5.cloned.1.call-done = f32[8,16,1024]{2,1,0:T(8,128)} async-done(((f32[8,256,1024]{2,1,0:T(8,128)}), f32[8,16,1024]{2,1,0:T(8,128)}) %reduce-scatter.5.cloned.1.call-update) | async-done | bytes 524304 | tf_op jit(solution)/shard_map/reduce_scatter | solution.py:96
  313.7 1.8 convert_bitcast_fusion.1
  315.5 7.1 %all-to-all-start.1 = ((bf16[8,16,1,1024]{3,1,2,0:T(8,128)(2,1)}), bf16[8,16,1,1024]{3,1,2,0:T(8,128)(2,1)S(1)}, u32[]{:S(2)}, u32[]{:S(2)}) async-start(bf16[8,16,1,1024]{3,1,2,0:T(8,128)(2,1)} %convert_bitcast_fusion.1), calls=%async_computation.3 | async-start | bytes 524288 | tf_op jit(solution)/shard_map/all_to_all | solution.py:100
  322.5 6.1 %reshape.123 = bf16[4096,512]{1,0:T(8,128)(2,1)} reshape(bf16[8,262144]{1,0:T(8,128)(2,1)} %fusion) | data formatting | bytes 8388608 | tf_op jit(solution)/shard_map/reshape | solution.py:98
  328.6 4.6 %all-to-all-done.1 = bf16[8,16,1,1024]{3,1,2,0:T(8,128)(2,1)S(1)} async-done(((bf16[8,16,1,1024]{3,1,2,0:T(8,128)(2,1)}), bf16[8,16,1,1024]{3,1,2,0:T(8,128)(2,1)S(1)}, u32[]{:S(2)}, u32[]{:S(2)}) %all-to-all-start.1) | async-done | bytes 262176 | tf_op jit(solution)/shard_map/all_to_all | solution.py:100
  (72 shorter events, 16.3 us)
Async XLA Ops:
  7.2 23.2 %copy-start.2 = (s32[16,1]{0,1:T(1,128)S(1)}, s32[16,1]{0,1:T(1,128)}, u32[]{:S(2)}) copy-start(s32[16,1]{0,1:T(1,128)} %param.11) | copy-start | bytes 196
  7.2 75.8 %all-gather.9.cloned.1.call-start = ((), (), s32[]{:S(2)}) async-start(), calls=%async_computation.6 | async-start | bytes 4456448 | tf_op jit(solution)/shard_map/all_gather | solution.py:33
  29.8 117.5 %reduce-scatter.3.cloned.1.call-start = ((), (), s32[]{:S(2)}) async-start(), calls=%async_computation.4 | async-start | bytes 4718592 | tf_op jit(solution)/shard_map/reduce_scatter | solution.py:64
  41.1 41.8 %collective-permute-start = (bf16[8,512,512]{2,1,0:T(8,128)(2,1)}, bf16[8,512,512]{2,1,0:T(8,128)(2,1)}, u32[]{:S(2)}, u32[]{:S(2)}) collective-permute-start(bf16[8,512,512]{2,1,0:T(8,128)(2,1)} %broadcast_select_fusion), channel_id=1, source_target_pairs={{0,1},{1,0},{2,3},{3,2},{4,5},{5,4},{6,7},{7,6},{8,9},{9,8},{10,11... | collective-permute-start | bytes 12582920 | tf_op jit(solution)/shard_map/ppermute | solution.py:36
  41.1 5.0 %copy-start.3 = (s32[16,1]{0,1:T(1,128)S(1)}, s32[16,1]{0,1:T(1,128)}, u32[]{:S(2)}) copy-start(s32[16,1]{0,1:T(1,128)} %param.12) | copy-start | bytes 196
  41.1 6.4 %copy-start.1 = (bf16[1,256,512]{2,1,0:T(8,128)(2,1)S(1)}, bf16[1,256,512]{2,1,0:T(8,128)(2,1)}, u32[]{:S(2)}) copy-start(bf16[1,256,512]{2,1,0:T(8,128)(2,1)} %param.13) | copy-start | bytes 786436
  92.0 123.2 %all-gather.11.cloned.1.call-start = ((), (), s32[]{:S(2)}) async-start(), calls=%async_computation.7 | async-start | bytes 2359296 | tf_op jit(solution)/shard_map/all_gather | solution.py:72
  176.9 136.8 %reduce-scatter.5.cloned.1.call-start = ((), (), s32[]{:S(2)}) async-start(), calls=%async_computation.5 | async-start | bytes 8912896 | tf_op jit(solution)/shard_map/reduce_scatter | solution.py:96
  224.8 1.6 copy-start
  231.3 7.5 %collective-permute-start.1 = (bf16[8,512,512]{2,1,0:T(8,128)(2,1)}, bf16[8,512,512]{2,1,0:T(8,128)(2,1)}, u32[]{:S(2)}, u32[]{:S(2)}) collective-permute-start(bf16[8,512,512]{2,1,0:T(8,128)(2,1)} %convolution_convert_fusion), channel_id=1, source_target_pairs={{0,1},{1,0},{2,3},{3,2},{4,5},{5,4},{6,7},{7,6},{8,9},{9,8},{10,11... | collective-permute-start | bytes 12582920 | tf_op jit(solution)/shard_map/ppermute | solution.py:79
  315.5 17.8 %all-to-all-start.1 = ((bf16[8,16,1,1024]{3,1,2,0:T(8,128)(2,1)}), bf16[8,16,1,1024]{3,1,2,0:T(8,128)(2,1)S(1)}, u32[]{:S(2)}, u32[]{:S(2)}) async-start(bf16[8,16,1,1024]{3,1,2,0:T(8,128)(2,1)} %convert_bitcast_fusion.1), calls=%async_computation.3 | async-start | bytes 524288 | tf_op jit(solution)/shard_map/all_to_all | solution.py:100
Sparse Core Ops, SparseCore 0:
  29.9 52.9 all-gather.8
  92.1 55.0 reduce-scatter.2
  177.0 38.1 all-gather.10
  225.0 88.6 reduce-scatter.4

commit v15 on v11

--- a/solution.py
+++ b/solution.py
@@ -40,10 +40,12 @@
     teach = teacher[0].astype(jnp.float32)
     live_value = jnp.where(own_live, 1.0, 0.0).astype(jnp.float32)
 
+    dead_shift = jnp.where(own_live, 0.0, neg_fill).astype(jnp.float32)
+
     def local_stats(values):
-        top = jnp.where(own_live, jnp.max(values, axis=1), neg_fill)
-        total = jnp.where(own_live, jnp.sum(jnp.exp(values - top[:, None]), axis=1), 0.0)
-        return top, total
+        top = jnp.max(values, axis=1)
+        total = live_value * jnp.sum(jnp.exp(values - top[:, None]), axis=1)
+        return top + dead_shift, total
 
     def merged(tops, totals):
         top = jnp.max(tops, axis=0)
@@ -95,10 +97,9 @@
     ghid = lax.psum_scatter(ghid, "section", scatter_dimension=1, tiled=True)
     ghid, grad_head = lax.optimization_barrier((ghid, grad_head))
     grad_head = grad_head.reshape(blocks * block_rows, col_width)
-    ghid = ghid.astype(jnp.bfloat16)
     ghid = lax.all_to_all(ghid[:, :, None], "z", split_axis=0, concat_axis=2, tiled=True)
     ghid = jnp.take(ghid.reshape(tok_local, n_z * n_core, col_width), pair_swap, axis=1)
-    grad_hidden = ghid.reshape(1, tok_local, model_width)
+    grad_hidden = ghid.astype(jnp.bfloat16).reshape(1, tok_local, model_width)
 
     return (grad_hidden, grad_head)
 

time: 342 us -> 341 us (level)
    unnamed x12 -> x14, local copies, waits for them, and re-layouts: 10.1 us -> 10.2 us
  transfers between devices with their start and end apart: 7 -> 7, of which waited for: 6 -> 6; matrix products, arithmetic and copies ran while one was open for 15% -> 14% of each run, Pallas kernels for 0% -> 0%
where the time goes in v15:
time: 341 us
  waiting for transfers between devices  170 us (50%)
  blocking collectives  67 us (20%)
  matrix products  31.2 us (9%)
  local copies, waits for them, and re-layouts  29.4 us (9%)
  other arithmetic  19.9 us (6%)
  between operations  16 us (5%)
  starting transfers between devices  7.17 us (2%)
    reduce_scatter x1, waiting for transfers between devices, local(): ghid = lax.psum_scatter(ghid, 'section', scatter_dimension=1, tiled=True)  67 us
    reduce_scatter x1, waiting for transfers between devices, local(): logits = lax.psum_scatter(part, 'z', scatter_dimension=0, tiled=True)[0]  53.9 us
    all_gather x1, waiting for transfers between devices, local(): grads = lax.all_gather(logit_grad[None], 'z', axis=0, tiled=True)  38.3 us
    all_gather x1, blocking collectives, local(): lax.all_gather(jnp.stack([teach_top_s, teach_sum_s, live_row]), 'section')  23.8 us
    all_gather x1, blocking collectives, local(): stud_all = lax.all_gather(jnp.stack([stud_top_s, stud_sum_s]), 'section')  23 us
    all_to_all x1, blocking collectives, local(): lax.all_to_all(pieces, 'z', split_axis=2, concat_axis=0, tiled=True)  20.2 us
    unnamed x14, local copies, waits for them, and re-layouts  10.2 us
    dot_general x1, matrix products, local(): jnp.einsum('mtr,mrw->mtw', grads, rows, preferred_element_type=jnp.float32)  9.6 us
  transfers between devices with their start and end apart: 7, of which 6 were waited for; matrix products, arithmetic and copies ran while one was open for 14% of the time, Pallas kernels for 0%

profile of v15, /device:TPU:2, one launch (start us, length us, event | category | flops | bytes accessed | tf_op | source)
XLA Modules:
  0.0 340.5 jit_solution(8990817466309150667)
XLA Ops:
  9.6 20.2 %all_to_all.33 = bf16[1,16,8,1024]{3,1,0,2:T(8,128)(2,1)} all-to-all(bf16[1,16,8,1024]{3,1,0,2:T(8,128)(2,1)S(1)} %copy.37), channel_id=1, replica_groups=mesh['section'=16,'z'=8,'core'=2] {'z'}, dimensions={2} | all-to-all | bytes 524288 | tf_op jit(solution)/shard_map/all_to_all | solution.py:32
  31.4 5.0 %gather_fusion.3 = bf16[8,512,512]{2,1,0:T(8,128)(2,1)} fusion(bf16[8,512,512]{2,1,0:T(8,128)(2,1)} %bitcast.93, s32[1024]{0:T(1024)S(1)} %pad_clamp_fusion), kind=kCustom, calls=%fused_computation.1.clone | custom fusion | bytes 8388640 | tf_op jit(solution)/shard_map/jit(_take)/gather | solution.py:36
  36.4 4.8 %broadcast_select_fusion = bf16[8,512,512]{2,1,0:T(8,128)(2,1)} fusion(bf16[8,512,512]{2,1,0:T(8,128)(2,1)} %gather_fusion.3, pred[8]{0:T(512)(128)(4,1)S(1)} %compare_and_fusion), kind=kLoop, calls=%fused_computation.10 | loop fusion | flops 2097152 | bytes 8388616 | tf_op jit(solution)/shard_map/jit(_take)/select_n | solution.py:36
  43.4 5.0 %gather_fusion.2 = bf16[8,512,512]{2,1,0:T(8,128)(2,1)} fusion(bf16[8,512,512]{2,1,0:T(8,128)(2,1)} %bitcast.94, s32[1024]{0:T(1024)S(1)} %pad_clamp_fusion.1), kind=kCustom, calls=%fused_computation.clone | custom fusion | bytes 8388640 | tf_op jit(solution)/shard_map/jit(_take)/gather | solution.py:35
  48.8 23.8 %all-gather.3 = f32[16,3,256]{2,1,0:T(4,128)S(1)} all-gather(f32[1,3,256]{2,1,0:T(4,128)S(1)} %maximum_bitcast_fusion), channel_id=2, replica_groups=mesh['section'=16,'z'=8,'core'=2] {'section'}, dimensions={0}, use_global_device_ids=true | all-gather | bytes 52224 | tf_op jit(solution)/shard_map/all_gather | solution.py:56
  72.6 4.7 %broadcast_select_fusion.1 = bf16[8,512,512]{2,1,0:T(8,128)(2,1)} fusion(bf16[8,512,512]{2,1,0:T(8,128)(2,1)} %gather_fusion.2, pred[8]{0:T(512)(128)(4,1)S(1)} %compare_and_fusion.1), kind=kLoop, calls=%fused_computation.11 | loop fusion | flops 2097152 | bytes 8388616 | tf_op jit(solution)/shard_map/jit(_take)/select_n | solution.py:35
  77.3 5.7 %all-gather.10.cloned.1.call-done = bf16[8,1,256,1,1024]{4,2,0,3,1:T(8,128)(2,1)} async-done(((bf16[8,1,16,1,1024]{4,2,0,3,1:T(8,128)(2,1)}), bf16[8,1,256,1,1024]{4,2,0,3,1:T(8,128)(2,1)}) %all-gather.10.cloned.1.call-update) | async-done | bytes 4194320 | tf_op jit(solution)/shard_map/all_gather | solution.py:33
  82.9 9.0 %fusion.2 = f32[8,256,512]{2,1,0:T(8,128)} fusion(bf16[8,256,1024]{2,1,0:T(8,128)(2,1)} %bitcast.95, bf16[8,512,512]{2,1,0:T(8,128)(2,1)} %collective-permute-done, bf16[8,512,512]{2,1,0:T(8,128)(2,1)} %broadcast_select_fusion.1), kind=kOutput, calls=%fused_computation.8 | convolution fusion | flops 2164260864 | bytes 16777216 | tf_op jit(solution)/shard_map/mtw,mrw->mtr/dot_general | solution.py:61
  93.3 53.9 %reduce-scatter.3.cloned.1.call-done = f32[1,256,512]{2,1,0:T(8,128)} async-done(((f32[8,256,512]{2,1,0:T(8,128)}), f32[1,256,512]{2,1,0:T(8,128)}) %reduce-scatter.3.cloned.1.call-update) | async-done | bytes 524304 | tf_op jit(solution)/shard_map/reduce_scatter | solution.py:62
  149.7 23.0 %all-gather.4 = f32[16,2,256]{2,1,0:T(2,128)S(1)} all-gather(f32[1,2,256]{2,1,0:T(2,128)S(1)} %maximum_bitcast_fusion.1), channel_id=4, replica_groups=mesh['section'=16,'z'=8,'core'=2] {'section'}, dimensions={0}, use_global_device_ids=true | all-gather | bytes 34816 | tf_op jit(solution)/shard_map/all_gather | solution.py:65
  172.8 2.8 fusion.15
  175.6 38.3 %all-gather.8.cloned.1.call-done = bf16[8,256,512]{2,1,0:T(8,128)(2,1)} async-done(((bf16[1,256,512]{2,1,0:T(8,128)(2,1)}), bf16[8,256,512]{2,1,0:T(8,128)(2,1)}) %all-gather.8.cloned.1.call-update) | async-done | bytes 2097168 | tf_op jit(solution)/shard_map/all_gather | solution.py:73
  213.9 9.6 %fusion.1 = f32[8,256,1024]{2,1,0:T(8,128)} fusion(bf16[8,256,512]{2,1,0:T(8,128)(2,1)} %all-gather.8.cloned.1.call-done, bf16[8,512,512]{2,1,0:T(8,128)(2,1)} %collective-permute-done, bf16[8,512,512]{2,1,0:T(8,128)(2,1)} %broadcast_select_fusion.1), kind=kOutput, calls=%fused_computation.7 | convolution fusion | flops 2164260864 | bytes 18874368 | tf_op jit(solution)/shard_map/mtr,mrw->mtw/dot_general | solution.py:75
  223.5 1.6 copy-done
  225.1 4.9 %convolution_convert_fusion = bf16[8,512,512]{2,1,0:T(8,128)(2,1)} fusion(bf16[8,256,512]{2,1,0:T(8,128)(2,1)S(1)} %copy-done, bf16[8,256,1024]{2,1,0:T(8,128)(2,1)} %bitcast.96), kind=kOutput, calls=%fused_computation.12 | convolution fusion | flops 1075838976 | bytes 8388608 | tf_op jit(solution)/shard_map/mtr,mtw->mrw/dot_general | solution.py:77
  230.4 2.9 convert_bitcast_fusion
  233.3 2.4 copy.55
  237.5 4.5 %copy.56 = bf16[1,8,512,512]{3,1,2,0:T(8,128)(2,1)S(1)} copy(bf16[1,8,512,512]{3,2,1,0:T(8,128)(2,1)} %bitcast.38) | data formatting | bytes 8388608
  242.1 3.5 %fusion = bf16[8,262144]{1,0:T(8,128)(2,1)} fusion(f32[8,262144]{1,0:T(8,128)S(1)} %fusion.23, bf16[8,262144]{1,0:T(8,128)(2,1)S(1)} %bitcast.91, bf16[8,2,8]{2,0,1:T(8,128)(2,1)S(1)} %select_convert_fusion.1, s32[]{:T(128)S(6)} %select_n.99), kind=kOutput, calls=%fused_computation.5 | convolution fusion | flops 37748736 | bytes 16779268 | tf_op jit(solution)/shard_map/dot_general | solution.py:95
  245.5 67.0 %reduce-scatter.5.cloned.1.call-done = f32[8,16,1024]{2,1,0:T(8,128)} async-done(((f32[8,256,1024]{2,1,0:T(8,128)}), f32[8,16,1024]{2,1,0:T(8,128)}) %reduce-scatter.5.cloned.1.call-update) | async-done | bytes 524304 | tf_op jit(solution)/shard_map/reduce_scatter | solution.py:97
  312.5 1.8 bitcast_convert_fusion
  314.3 7.0 %all-to-all-start.1 = ((bf16[8,16,1,1024]{3,1,2,0:T(8,128)(2,1)}), bf16[8,16,1,1024]{3,1,2,0:T(8,128)(2,1)S(1)}, u32[]{:S(2)}, u32[]{:S(2)}) async-start(bf16[8,16,1,1024]{3,1,2,0:T(8,128)(2,1)} %bitcast_convert_fusion), calls=%async_computation.3 | async-start | bytes 524288 | tf_op jit(solution)/shard_map/all_to_all | solution.py:100
  321.4 6.1 %reshape.192 = bf16[4096,512]{1,0:T(8,128)(2,1)} reshape(bf16[8,262144]{1,0:T(8,128)(2,1)} %fusion) | data formatting | bytes 8388608 | tf_op jit(solution)/shard_map/reshape | solution.py:99
  327.5 4.5 %all-to-all-done.1 = bf16[8,16,1,1024]{3,1,2,0:T(8,128)(2,1)S(1)} async-done(((bf16[8,16,1,1024]{3,1,2,0:T(8,128)(2,1)}), bf16[8,16,1,1024]{3,1,2,0:T(8,128)(2,1)S(1)}, u32[]{:S(2)}, u32[]{:S(2)}) %all-to-all-start.1) | async-done | bytes 262176 | tf_op jit(solution)/shard_map/all_to_all | solution.py:100
  (76 shorter events, 12.7 us)
Async XLA Ops:
  7.2 23.2 %copy-start.2 = (s32[16,1]{0,1:T(1,128)S(1)}, s32[16,1]{0,1:T(1,128)}, u32[]{:S(2)}) copy-start(s32[16,1]{0,1:T(1,128)} %param.9) | copy-start | bytes 196
  7.2 75.8 %all-gather.10.cloned.1.call-start = ((), (), s32[]{:S(2)}) async-start(), calls=%async_computation.7 | async-start | bytes 4456448 | tf_op jit(solution)/shard_map/all_gather | solution.py:33
  29.8 117.4 %reduce-scatter.3.cloned.1.call-start = ((), (), s32[]{:S(2)}) async-start(), calls=%async_computation.4 | async-start | bytes 4718592 | tf_op jit(solution)/shard_map/reduce_scatter | solution.py:62
  36.4 4.8 %copy-start.1 = (bf16[1,256,512]{2,1,0:T(8,128)(2,1)S(1)}, bf16[1,256,512]{2,1,0:T(8,128)(2,1)}, u32[]{:S(2)}) copy-start(bf16[1,256,512]{2,1,0:T(8,128)(2,1)} %param.11) | copy-start | bytes 786436
  36.4 4.9 %copy-start.3 = (s32[16,1]{0,1:T(1,128)S(1)}, s32[16,1]{0,1:T(1,128)}, u32[]{:S(2)}) copy-start(s32[16,1]{0,1:T(1,128)} %param.10) | copy-start | bytes 196
  41.2 41.7 %collective-permute-start = (bf16[8,512,512]{2,1,0:T(8,128)(2,1)}, bf16[8,512,512]{2,1,0:T(8,128)(2,1)}, u32[]{:S(2)}, u32[]{:S(2)}) collective-permute-start(bf16[8,512,512]{2,1,0:T(8,128)(2,1)} %broadcast_select_fusion), channel_id=1, source_target_pairs={{0,1},{1,0},{2,3},{3,2},{4,5},{5,4},{6,7},{7,6},{8,9},{9,8},{10,11... | collective-permute-start | bytes 12582920 | tf_op jit(solution)/shard_map/ppermute | solution.py:36
  92.0 121.9 %all-gather.8.cloned.1.call-start = ((), (), s32[]{:S(2)}) async-start(), calls=%async_computation.5 | async-start | bytes 2359296 | tf_op jit(solution)/shard_map/all_gather | solution.py:73
  175.6 136.9 %reduce-scatter.5.cloned.1.call-start = ((), (), s32[]{:S(2)}) async-start(), calls=%async_computation.6 | async-start | bytes 8912896 | tf_op jit(solution)/shard_map/reduce_scatter | solution.py:97
  223.5 1.6 copy-start
  230.0 7.5 %collective-permute-start.1 = (bf16[8,512,512]{2,1,0:T(8,128)(2,1)}, bf16[8,512,512]{2,1,0:T(8,128)(2,1)}, u32[]{:S(2)}, u32[]{:S(2)}) collective-permute-start(bf16[8,512,512]{2,1,0:T(8,128)(2,1)} %convolution_convert_fusion), channel_id=1, source_target_pairs={{0,1},{1,0},{2,3},{3,2},{4,5},{5,4},{6,7},{7,6},{8,9},{9,8},{10,11... | collective-permute-start | bytes 12582920 | tf_op jit(solution)/shard_map/ppermute | solution.py:80
  314.3 17.7 %all-to-all-start.1 = ((bf16[8,16,1,1024]{3,1,2,0:T(8,128)(2,1)}), bf16[8,16,1,1024]{3,1,2,0:T(8,128)(2,1)S(1)}, u32[]{:S(2)}, u32[]{:S(2)}) async-start(bf16[8,16,1,1024]{3,1,2,0:T(8,128)(2,1)} %bitcast_convert_fusion), calls=%async_computation.3 | async-start | bytes 524288 | tf_op jit(solution)/shard_map/all_to_all | solution.py:100
Sparse Core Ops, SparseCore 0:
  29.9 52.9 all-gather.9
  92.1 55.0 reduce-scatter.2
  175.7 38.1 all-gather.7
  223.7 88.7 reduce-scatter.4

commit v16 on v15

--- a/solution.py
+++ b/solution.py
@@ -35,6 +35,10 @@
     own_rows = jnp.take(table, own_ids, axis=0)
     sib_rows = lax.ppermute(jnp.take(table, sib_ids, axis=0), "core", swap)
     rows = jnp.concatenate([own_rows, sib_rows], axis=2)
+    odd = core_at == 1
+    rows_natural = jnp.concatenate(
+        [jnp.where(odd, sib_rows, own_rows), jnp.where(odd, own_rows, sib_rows)], axis=2
+    )
 
     own_live = lax.dynamic_index_in_dim(live_flags, my_replica, 0, keepdims=False) > 0
     teach = teacher[0].astype(jnp.float32)
@@ -72,7 +76,7 @@
     logit_grad = (block_rows * live_count * (student - teach_prob)).astype(jnp.bfloat16)
     grads = lax.all_gather(logit_grad[None], "z", axis=0, tiled=True)
 
-    ghid = jnp.einsum("mtr,mrw->mtw", grads, rows, preferred_element_type=jnp.float32)
+    ghid = jnp.einsum("mtr,mrw->mtw", grads, rows_natural, preferred_element_type=jnp.float32)
     ghid, grads = lax.optimization_barrier((ghid, grads))
     contrib_sib = jnp.einsum(
         "mtr,mtw->mrw", grads, hid_w[:, :, col_width:], preferred_element_type=jnp.float32
@@ -98,7 +102,6 @@
     ghid, grad_head = lax.optimization_barrier((ghid, grad_head))
     grad_head = grad_head.reshape(blocks * block_rows, col_width)
     ghid = lax.all_to_all(ghid[:, :, None], "z", split_axis=0, concat_axis=2, tiled=True)
-    ghid = jnp.take(ghid.reshape(tok_local, n_z * n_core, col_width), pair_swap, axis=1)
     grad_hidden = ghid.astype(jnp.bfloat16).reshape(1, tok_local, model_width)
 
     return (grad_hidden, grad_head)

time: 341 us -> 340 us (level)
  waiting for transfers between devices: 170 us -> 164 us
  other arithmetic: 19.9 us -> 25.3 us
    select_n x1 -> x2, other arithmetic: 0.01 us -> 10.9 us  [the longest x1 6.29 us: local(): jnp.where(odd, sib_rows, own_rows)]
    select_n x2 -> x1, other arithmetic: 4.67 us -> 0.01 us  [local(): own_rows = jnp.take(table, own_ids, axis=0)]
    all_gather x1, waiting for transfers between devices: 38.3 us -> 33.7 us  [local(): grads = lax.all_gather(logit_grad[None], 'z', axis=0, tiled=True)]
    unnamed x14 -> x12, local copies, waits for them, and re-layouts: 10.2 us -> 10.1 us
  transfers between devices with their start and end apart: 7 -> 7, of which waited for: 6 -> 6; matrix products, arithmetic and copies ran while one was open for 14% -> 16% of each run, Pallas kernels for 0% -> 0%
where the time goes in v16:
time: 340 us; the launch traced here: 339 us
  waiting for transfers between devices  164 us (48%)
  blocking collectives  67 us (20%)
  matrix products  31.1 us (9%)
  local copies, waits for them, and re-layouts  29 us (9%)
  other arithmetic  25.3 us (7%)
  between operations  15.9 us (5%)
  starting transfers between devices  7.23 us (2%)
    reduce_scatter x1, waiting for transfers between devices, local(): ghid = lax.psum_scatter(ghid, 'section', scatter_dimension=1, tiled=True)  67.1 us
    reduce_scatter x1, waiting for transfers between devices, local(): logits = lax.psum_scatter(part, 'z', scatter_dimension=0, tiled=True)[0]  53.7 us
    all_gather x1, waiting for transfers between devices, local(): grads = lax.all_gather(logit_grad[None], 'z', axis=0, tiled=True)  33.7 us
    all_gather x1, blocking collectives, local(): lax.all_gather(jnp.stack([teach_top_s, teach_sum_s, live_row]), 'section')  23.8 us
    all_gather x1, blocking collectives, local(): stud_all = lax.all_gather(jnp.stack([stud_top_s, stud_sum_s]), 'section')  23 us
    all_to_all x1, blocking collectives, local(): lax.all_to_all(pieces, 'z', split_axis=2, concat_axis=0, tiled=True)  20.2 us
    unnamed x12, local copies, waits for them, and re-layouts  10.1 us
    dot_general x1, matrix products, local(): jnp.einsum('mtr,mrw->mtw', grads, rows_natural, preferred_element_type=jn...  9.66 us
  transfers between devices with their start and end apart: 7, of which 6 were waited for; matrix products, arithmetic and copies ran while one was open for 16% of the time, Pallas kernels for 0%

profile of v16, /device:TPU:2, one launch (start us, length us, event | category | flops | bytes accessed | tf_op | source)
XLA Modules:
  0.0 339.4 jit_solution(16772743393573401400)
XLA Ops:
  9.6 20.2 %all_to_all.27 = bf16[1,16,8,1024]{3,1,0,2:T(8,128)(2,1)} all-to-all(bf16[1,16,8,1024]{3,1,0,2:T(8,128)(2,1)S(1)} %copy.34), channel_id=1, replica_groups=mesh['section'=16,'z'=8,'core'=2] {'z'}, dimensions={2} | all-to-all | bytes 524288 | tf_op jit(solution)/shard_map/all_to_all | solution.py:32
  31.4 5.0 %gather_fusion.2 = bf16[8,512,512]{2,1,0:T(8,128)(2,1)} fusion(bf16[8,512,512]{2,1,0:T(8,128)(2,1)} %bitcast.91, s32[1024]{0:T(1024)S(1)} %pad_clamp_fusion), kind=kCustom, calls=%fused_computation.1.clone | custom fusion | bytes 8388640 | tf_op jit(solution)/shard_map/jit(_take)/gather | solution.py:36
  36.4 4.8 %broadcast_select_fusion = bf16[8,512,512]{2,1,0:T(8,128)(2,1)} fusion(bf16[8,512,512]{2,1,0:T(8,128)(2,1)} %gather_fusion.2, pred[8]{0:T(512)(128)(4,1)S(1)} %compare_and_fusion), kind=kLoop, calls=%fused_computation.14 | loop fusion | flops 2097152 | bytes 8388616 | tf_op jit(solution)/shard_map/jit(_take)/select_n | solution.py:36
  43.2 5.0 %gather_fusion.1 = bf16[8,512,512]{2,1,0:T(8,128)(2,1)} fusion(bf16[8,512,512]{2,1,0:T(8,128)(2,1)} %bitcast.92, s32[1024]{0:T(1024)S(1)} %pad_clamp_fusion.1), kind=kCustom, calls=%fused_computation.clone | custom fusion | bytes 8388640 | tf_op jit(solution)/shard_map/jit(_take)/gather | solution.py:35
  48.6 23.8 %all-gather.3 = f32[16,3,256]{2,1,0:T(4,128)S(1)} all-gather(f32[1,3,256]{2,1,0:T(4,128)S(1)} %maximum_bitcast_fusion), channel_id=2, replica_groups=mesh['section'=16,'z'=8,'core'=2] {'section'}, dimensions={0}, use_global_device_ids=true | all-gather | bytes 52224 | tf_op jit(solution)/shard_map/all_gather | solution.py:60
  72.4 6.3 %broadcast_select_fusion.3 = (bf16[8,512,512]{2,1,0:T(8,128)(2,1)}, bf16[8,512,512]{2,1,0:T(8,128)(2,1)}) fusion(bf16[8,512,512]{2,1,0:T(8,128)(2,1)} %collective-permute-done, pred[]{:T(512)S(6)} %eq.17, bf16[8,512,512]{2,1,0:T(8,128)(2,1)} %gather_fusion.1, pred[8]{0:T(512)(128)(4,1)S(1)} %compare_and_fusion.1), kind=kLoop, calls=%fused_computation.17 | loop fusion | flops 4194304 | bytes 16777224 | tf_op jit(solution)/shard_map/jit(_where)/select_n | solution.py:40
  78.7 4.2 %all-gather.10.cloned.1.call-done = bf16[8,1,256,1,1024]{4,2,0,3,1:T(8,128)(2,1)} async-done(((bf16[8,1,16,1,1024]{4,2,0,3,1:T(8,128)(2,1)}), bf16[8,1,256,1,1024]{4,2,0,3,1:T(8,128)(2,1)}) %all-gather.10.cloned.1.call-update) | async-done | bytes 4194320 | tf_op jit(solution)/shard_map/all_gather | solution.py:33
  82.9 9.0 %fusion.1 = f32[8,256,512]{2,1,0:T(8,128)} fusion(bf16[8,256,1024]{2,1,0:T(8,128)(2,1)} %bitcast.93, bf16[8,512,512]{2,1,0:T(8,128)(2,1)} %collective-permute-done, bf16[8,512,512]{2,1,0:T(8,128)(2,1)} %get-tuple-element.18), kind=kOutput, calls=%fused_computation.5 | convolution fusion | flops 2164260864 | bytes 16777216 | tf_op jit(solution)/shard_map/mtw,mrw->mtr/dot_general | solution.py:65
  93.5 53.7 %reduce-scatter.3.cloned.1.call-done = f32[1,256,512]{2,1,0:T(8,128)} async-done(((f32[8,256,512]{2,1,0:T(8,128)}), f32[1,256,512]{2,1,0:T(8,128)}) %reduce-scatter.3.cloned.1.call-update) | async-done | bytes 524304 | tf_op jit(solution)/shard_map/reduce_scatter | solution.py:66
  149.6 23.0 %all-gather.4 = f32[16,2,256]{2,1,0:T(2,128)S(1)} all-gather(f32[1,2,256]{2,1,0:T(2,128)S(1)} %maximum_bitcast_fusion.1), channel_id=4, replica_groups=mesh['section'=16,'z'=8,'core'=2] {'section'}, dimensions={0}, use_global_device_ids=true | all-gather | bytes 34816 | tf_op jit(solution)/shard_map/all_gather | solution.py:69
  172.7 2.7 fusion.21
  175.5 4.6 %broadcast_select_fusion.2 = bf16[8,512,512]{2,1,0:T(8,128)(2,1)} fusion(bf16[8,512,512]{2,1,0:T(8,128)(2,1)} %get-tuple-element.18, bf16[8,512,512]{2,1,0:T(8,128)(2,1)} %collective-permute-done, pred[]{:T(512)S(6)} %eq.17), kind=kLoop, calls=%fused_computation.16 | loop fusion | flops 2097152 | bytes 12582913 | tf_op jit(solution)/shard_map/jit(_where)/select_n | solution.py:40
  180.1 33.7 %all-gather.8.cloned.1.call-done = bf16[8,256,512]{2,1,0:T(8,128)(2,1)} async-done(((bf16[1,256,512]{2,1,0:T(8,128)(2,1)}), bf16[8,256,512]{2,1,0:T(8,128)(2,1)}) %all-gather.8.cloned.1.call-update) | async-done | bytes 2097168 | tf_op jit(solution)/shard_map/all_gather | solution.py:77
  213.8 9.7 %fusion.5 = f32[8,256,1024]{2,1,0:T(8,128)} fusion(bf16[8,256,512]{2,1,0:T(8,128)(2,1)} %all-gather.8.cloned.1.call-done, bf16[8,512,512]{2,1,0:T(8,128)(2,1)} %broadcast_select_fusion.2, bf16[8,512,512]{2,1,0:T(8,128)(2,1)} %get-tuple-element.17), kind=kOutput, calls=%fused_computation.9 | convolution fusion | flops 2164260864 | bytes 18874368 | tf_op jit(solution)/shard_map/mtr,mrw->mtw/dot_general | solution.py:79
  225.0 4.9 %convolution_convert_fusion = bf16[8,512,512]{2,1,0:T(8,128)(2,1)} fusion(bf16[8,256,512]{2,1,0:T(8,128)(2,1)S(1)} %copy-done, bf16[8,256,1024]{2,1,0:T(8,128)(2,1)} %bitcast.94), kind=kOutput, calls=%fused_computation.18 | convolution fusion | flops 1075838976 | bytes 8388608 | tf_op jit(solution)/shard_map/mtr,mtw->mrw/dot_general | solution.py:81
  230.3 2.9 convert_bitcast_fusion
  233.2 2.4 copy.49
  237.4 4.5 %copy.50 = bf16[1,8,512,512]{3,1,2,0:T(8,128)(2,1)S(1)} copy(bf16[1,8,512,512]{3,2,1,0:T(8,128)(2,1)} %bitcast.35) | data formatting | bytes 8388608
  242.0 3.4 fusion
  245.3 67.1 %reduce-scatter.5.cloned.1.call-done = f32[8,16,1024]{2,1,0:T(8,128)} async-done(((f32[8,256,1024]{2,1,0:T(8,128)}), f32[8,16,1024]{2,1,0:T(8,128)}) %reduce-scatter.5.cloned.1.call-update) | async-done | bytes 524304 | tf_op jit(solution)/shard_map/reduce_scatter | solution.py:101
  312.4 1.8 bitcast_convert_fusion
  314.2 7.1 %all-to-all-start.1 = ((bf16[8,16,1,1024]{3,1,2,0:T(8,128)(2,1)}), bf16[8,16,1,1024]{3,1,2,0:T(8,128)(2,1)S(1)}, u32[]{:S(2)}, u32[]{:S(2)}) async-start(bf16[8,16,1,1024]{3,1,2,0:T(8,128)(2,1)} %bitcast_convert_fusion), calls=%async_computation.3 | async-start | bytes 524288 | tf_op jit(solution)/shard_map/all_to_all | solution.py:104
  321.2 6.1 %reshape.170 = bf16[4096,512]{1,0:T(8,128)(2,1)} reshape(bf16[8,262144]{1,0:T(8,128)(2,1)} %fusion) | data formatting | bytes 8388608 | tf_op jit(solution)/shard_map/reshape | solution.py:103
  327.3 4.6 %all-to-all-done.1 = bf16[8,16,1,1024]{3,1,2,0:T(8,128)(2,1)S(1)} async-done(((bf16[8,16,1,1024]{3,1,2,0:T(8,128)(2,1)}), bf16[8,16,1,1024]{3,1,2,0:T(8,128)(2,1)S(1)}, u32[]{:S(2)}, u32[]{:S(2)}) %all-to-all-start.1) | async-done | bytes 262176 | tf_op jit(solution)/shard_map/all_to_all | solution.py:104
  (69 shorter events, 13.2 us)
Async XLA Ops:
  7.2 23.2 %copy-start.2 = (s32[16,1]{0,1:T(1,128)S(1)}, s32[16,1]{0,1:T(1,128)}, u32[]{:S(2)}) copy-start(s32[16,1]{0,1:T(1,128)} %param.9) | copy-start | bytes 196
  7.2 75.8 %all-gather.10.cloned.1.call-start = ((), (), s32[]{:S(2)}) async-start(), calls=%async_computation.7 | async-start | bytes 4456448 | tf_op jit(solution)/shard_map/all_gather | solution.py:33
  29.8 117.4 %reduce-scatter.3.cloned.1.call-start = ((), (), s32[]{:S(2)}) async-start(), calls=%async_computation.4 | async-start | bytes 4718592 | tf_op jit(solution)/shard_map/reduce_scatter | solution.py:66
  36.4 4.8 %copy-start.1 = (bf16[1,256,512]{2,1,0:T(8,128)(2,1)S(1)}, bf16[1,256,512]{2,1,0:T(8,128)(2,1)}, u32[]{:S(2)}) copy-start(bf16[1,256,512]{2,1,0:T(8,128)(2,1)} %param.11) | copy-start | bytes 786436
  36.4 4.9 %copy-start.3 = (s32[16,1]{0,1:T(1,128)S(1)}, s32[16,1]{0,1:T(1,128)}, u32[]{:S(2)}) copy-start(s32[16,1]{0,1:T(1,128)} %param.10) | copy-start | bytes 196
  41.2 31.2 %collective-permute-start = (bf16[8,512,512]{2,1,0:T(8,128)(2,1)}, bf16[8,512,512]{2,1,0:T(8,128)(2,1)}, u32[]{:S(2)}, u32[]{:S(2)}) collective-permute-start(bf16[8,512,512]{2,1,0:T(8,128)(2,1)} %broadcast_select_fusion), channel_id=1, source_target_pairs={{0,1},{1,0},{2,3},{3,2},{4,5},{5,4},{6,7},{7,6},{8,9},{9,8},{10,11... | collective-permute-start | bytes 12582920 | tf_op jit(solution)/shard_map/ppermute | solution.py:36
  91.9 121.8 %all-gather.8.cloned.1.call-start = ((), (), s32[]{:S(2)}) async-start(), calls=%async_computation.5 | async-start | bytes 2359296 | tf_op jit(solution)/shard_map/all_gather | solution.py:77
  175.4 137.0 %reduce-scatter.5.cloned.1.call-start = ((), (), s32[]{:S(2)}) async-start(), calls=%async_computation.6 | async-start | bytes 8912896 | tf_op jit(solution)/shard_map/reduce_scatter | solution.py:101
  223.4 1.6 copy-start
  229.9 7.5 %collective-permute-start.1 = (bf16[8,512,512]{2,1,0:T(8,128)(2,1)}, bf16[8,512,512]{2,1,0:T(8,128)(2,1)}, u32[]{:S(2)}, u32[]{:S(2)}) collective-permute-start(bf16[8,512,512]{2,1,0:T(8,128)(2,1)} %convolution_convert_fusion), channel_id=1, source_target_pairs={{0,1},{1,0},{2,3},{3,2},{4,5},{5,4},{6,7},{7,6},{8,9},{9,8},{10,11... | collective-permute-start | bytes 12582920 | tf_op jit(solution)/shard_map/ppermute | solution.py:84
  314.2 17.7 %all-to-all-start.1 = ((bf16[8,16,1,1024]{3,1,2,0:T(8,128)(2,1)}), bf16[8,16,1,1024]{3,1,2,0:T(8,128)(2,1)S(1)}, u32[]{:S(2)}, u32[]{:S(2)}) async-start(bf16[8,16,1,1024]{3,1,2,0:T(8,128)(2,1)} %bitcast_convert_fusion), calls=%async_computation.3 | async-start | bytes 524288 | tf_op jit(solution)/shard_map/all_to_all | solution.py:104
Sparse Core Ops, SparseCore 0:
  29.9 52.9 all-gather.9
  92.0 55.0 reduce-scatter.2
  175.5 38.1 all-gather.7
  223.6 88.7 reduce-scatter.4

commit v17 on v16

--- a/solution.py
+++ b/solution.py
@@ -26,15 +26,12 @@
     own_ids = lax.dynamic_index_in_dim(ids_by, core_at, 1, keepdims=False)
     sib_ids = lax.dynamic_index_in_dim(ids_by, 1 - core_at, 1, keepdims=False)
 
-    pair_swap = jnp.arange(n_z * n_core, dtype=jnp.int32) ^ core_at
-    pieces = jnp.take(hidden[0].reshape(tok_local, n_z * n_core, col_width), pair_swap, axis=1)
-    pieces = pieces.reshape(1, tok_local, n_z, n_core * col_width)
+    pieces = hidden.reshape(1, tok_local, n_z, n_core * col_width)
     pieces = lax.all_to_all(pieces, "z", split_axis=2, concat_axis=0, tiled=True)
     hid_w = lax.all_gather(pieces, "section", axis=1, tiled=True).reshape(n_z, -1, n_core * col_width)
 
     own_rows = jnp.take(table, own_ids, axis=0)
     sib_rows = lax.ppermute(jnp.take(table, sib_ids, axis=0), "core", swap)
-    rows = jnp.concatenate([own_rows, sib_rows], axis=2)
     odd = core_at == 1
     rows_natural = jnp.concatenate(
         [jnp.where(odd, sib_rows, own_rows), jnp.where(odd, own_rows, sib_rows)], axis=2
@@ -62,7 +59,7 @@
     teach_top, teach_total = merged(teach_all[:, 0], teach_all[:, 1])
     live_count = jnp.sum(teach_all[:, 2, 0])
 
-    part = jnp.einsum("mtw,mrw->mtr", hid_w, rows, preferred_element_type=jnp.float32)
+    part = jnp.einsum("mtw,mrw->mtr", hid_w, rows_natural, preferred_element_type=jnp.float32)
     logits = lax.psum_scatter(part, "z", scatter_dimension=0, tiled=True)[0]
 
     stud_top_s, stud_sum_s = local_stats(logits)
@@ -79,11 +76,11 @@
     ghid = jnp.einsum("mtr,mrw->mtw", grads, rows_natural, preferred_element_type=jnp.float32)
     ghid, grads = lax.optimization_barrier((ghid, grads))
     contrib_sib = jnp.einsum(
-        "mtr,mtw->mrw", grads, hid_w[:, :, col_width:], preferred_element_type=jnp.float32
+        "mtr,mtw->mrw", grads, lax.dynamic_slice_in_dim(hid_w, (1 - core_at) * col_width, col_width, 2), preferred_element_type=jnp.float32
     ).astype(jnp.bfloat16)
     contrib_got = lax.ppermute(contrib_sib, "core", swap)
     contrib_own = jnp.einsum(
-        "mtr,mtw->mrw", grads, hid_w[:, :, :col_width], preferred_element_type=jnp.float32
+        "mtr,mtw->mrw", grads, lax.dynamic_slice_in_dim(hid_w, core_at * col_width, col_width, 2), preferred_element_type=jnp.float32
     ).astype(jnp.bfloat16)
 
     block_range = jnp.arange(blocks, dtype=jnp.int32)[None, :]

time: 340 us -> 338 us (level)
  other arithmetic: 25.3 us -> 21 us
  waiting for transfers between devices: 164 us -> 168 us
    select_n x3 -> x0, other arithmetic: 4.65 us -> none  [the longest x1 4.61 us: local(): jnp.where(odd, own_rows, sib_rows)]
    all_gather x1, waiting for transfers between devices: 33.7 us -> 38.3 us  [local(): grads = lax.all_gather(logit_grad[None], 'z', axis=0, tiled=True)]
    unnamed x12 -> x9, local copies, waits for them, and re-layouts: 10.1 us -> 9.02 us
  transfers between devices with their start and end apart: 7 -> 7, of which waited for: 6 -> 6; matrix products, arithmetic and copies ran while one was open for 16% -> 15% of each run, Pallas kernels for 0% -> 0%
where the time goes in v17:
time: 338 us; the launch traced here: 337 us
  waiting for transfers between devices  168 us (50%)
  blocking collectives  67 us (20%)
  matrix products  31.1 us (9%)
  local copies, waits for them, and re-layouts  27.8 us (8%)
  other arithmetic  21 us (6%)
  between operations  15.7 us (5%)
  starting transfers between devices  7.2 us (2%)
    reduce_scatter x1, waiting for transfers between devices, local(): ghid = lax.psum_scatter(ghid, 'section', scatter_dimension=1, tiled=True)  66.5 us
    reduce_scatter x1, waiting for transfers between devices, local(): logits = lax.psum_scatter(part, 'z', scatter_dimension=0, tiled=True)[0]  53.8 us
    all_gather x1, waiting for transfers between devices, local(): grads = lax.all_gather(logit_grad[None], 'z', axis=0, tiled=True)  38.3 us
    all_gather x1, blocking collectives, local(): lax.all_gather(jnp.stack([teach_top_s, teach_sum_s, live_row]), 'section')  23.7 us
    all_gather x1, blocking collectives, local(): stud_all = lax.all_gather(jnp.stack([stud_top_s, stud_sum_s]), 'section')  23 us
    all_to_all x1, blocking collectives, local(): lax.all_to_all(pieces, 'z', split_axis=2, concat_axis=0, tiled=True)  20.2 us
    dot_general x1, matrix products, local(): jnp.einsum('mtr,mrw->mtw', grads, rows_natural, preferred_element_type=jn...  9.6 us
    unnamed x9, local copies, waits for them, and re-layouts  9.02 us
  transfers between devices with their start and end apart: 7, of which 6 were waited for; matrix products, arithmetic and copies ran while one was open for 15% of the time, Pallas kernels for 0%

profile of v17, /device:TPU:2, one launch (start us, length us, event | category | flops | bytes accessed | tf_op | source)
XLA Modules:
  0.0 337.4 jit_solution(10077072330613144883)
XLA Ops:
  8.2 20.2 %all_to_all.27 = bf16[1,16,8,1024]{3,1,0,2:T(8,128)(2,1)} all-to-all(bf16[1,16,8,1024]{3,1,0,2:T(8,128)(2,1)S(1)} %bitcast.95), channel_id=1, replica_groups=mesh['section'=16,'z'=8,'core'=2] {'z'}, dimensions={2} | all-to-all | bytes 524288 | tf_op jit(solution)/shard_map/all_to_all | solution.py:30
  30.7 5.0 %gather_fusion = bf16[8,512,512]{2,1,0:T(8,128)(2,1)} fusion(bf16[8,512,512]{2,1,0:T(8,128)(2,1)} %bitcast.88, s32[1024]{0:T(1024)S(1)} %pad_clamp_fusion.1), kind=kCustom, calls=%fused_computation.clone | custom fusion | bytes 8388640 | tf_op jit(solution)/shard_map/jit(_take)/gather | solution.py:34
  35.7 4.9 %broadcast_select_fusion.1 = bf16[8,512,512]{2,1,0:T(8,128)(2,1)} fusion(bf16[8,512,512]{2,1,0:T(8,128)(2,1)} %gather_fusion, pred[8]{0:T(512)(128)(4,1)S(1)} %compare_and_fusion.1), kind=kLoop, calls=%fused_computation.9 | loop fusion | flops 2097152 | bytes 8388616 | tf_op jit(solution)/shard_map/jit(_take)/select_n | solution.py:34
  42.4 5.0 %gather_fusion.1 = bf16[8,512,512]{2,1,0:T(8,128)(2,1)} fusion(bf16[8,512,512]{2,1,0:T(8,128)(2,1)} %bitcast.89, s32[1024]{0:T(1024)S(1)} %pad_clamp_fusion), kind=kCustom, calls=%fused_computation.1.clone | custom fusion | bytes 8388640 | tf_op jit(solution)/shard_map/jit(_take)/gather | solution.py:33
  47.8 23.7 %all-gather.3 = f32[16,3,256]{2,1,0:T(4,128)S(1)} all-gather(f32[1,3,256]{2,1,0:T(4,128)S(1)} %maximum_bitcast_fusion), channel_id=2, replica_groups=mesh['section'=16,'z'=8,'core'=2] {'section'}, dimensions={0}, use_global_device_ids=true | all-gather | bytes 52224 | tf_op jit(solution)/shard_map/all_gather | solution.py:57
  71.6 6.0 %broadcast_select_fusion.3 = (bf16[8,512,512]{2,1,0:T(8,128)(2,1)}, bf16[8,512,512]{2,1,0:T(8,128)(2,1)}) fusion(bf16[8,512,512]{2,1,0:T(8,128)(2,1)} %collective-permute-done, pred[]{:T(512)S(6)} %eq.17, bf16[8,512,512]{2,1,0:T(8,128)(2,1)} %gather_fusion.1, pred[8]{0:T(512)(128)(4,1)S(1)} %compare_and_fusion), kind=kLoop, calls=%fused_computation.11 | loop fusion | flops 6291456 | bytes 16777224 | tf_op jit(solution)/shard_map/jit(_where)/select_n | solution.py:37
  77.6 4.0 %all-gather.10.cloned.1.call-done = bf16[8,1,256,1,1024]{4,2,0,3,1:T(8,128)(2,1)} async-done(((bf16[8,1,16,1,1024]{4,2,0,3,1:T(8,128)(2,1)}), bf16[8,1,256,1,1024]{4,2,0,3,1:T(8,128)(2,1)}) %all-gather.10.cloned.1.call-update) | async-done | bytes 4194320 | tf_op jit(solution)/shard_map/all_gather | solution.py:31
  81.5 8.9 %fusion.2 = f32[8,256,512]{2,1,0:T(8,128)} fusion(bf16[8,256,1024]{2,1,0:T(8,128)(2,1)} %bitcast.90, bf16[8,512,512]{2,1,0:T(8,128)(2,1)} %get-tuple-element.18, bf16[8,512,512]{2,1,0:T(8,128)(2,1)} %get-tuple-element.17), kind=kOutput, calls=%fused_computation.6 | convolution fusion | flops 2164260864 | bytes 16777216 | tf_op jit(solution)/shard_map/mtw,mrw->mtr/dot_general | solution.py:62
  92.0 53.8 %reduce-scatter.3.cloned.1.call-done = f32[1,256,512]{2,1,0:T(8,128)} async-done(((f32[8,256,512]{2,1,0:T(8,128)}), f32[1,256,512]{2,1,0:T(8,128)}) %reduce-scatter.3.cloned.1.call-update) | async-done | bytes 524304 | tf_op jit(solution)/shard_map/reduce_scatter | solution.py:63
  148.2 23.0 %all-gather.4 = f32[16,2,256]{2,1,0:T(2,128)S(1)} all-gather(f32[1,2,256]{2,1,0:T(2,128)S(1)} %maximum_bitcast_fusion.1), channel_id=4, replica_groups=mesh['section'=16,'z'=8,'core'=2] {'section'}, dimensions={0}, use_global_device_ids=true | all-gather | bytes 34816 | tf_op jit(solution)/shard_map/all_gather | solution.py:66
  171.3 2.6 fusion.15
  174.0 38.3 %all-gather.8.cloned.1.call-done = bf16[8,256,512]{2,1,0:T(8,128)(2,1)} async-done(((bf16[1,256,512]{2,1,0:T(8,128)(2,1)}), bf16[8,256,512]{2,1,0:T(8,128)(2,1)}) %all-gather.8.cloned.1.call-update) | async-done | bytes 2097168 | tf_op jit(solution)/shard_map/all_gather | solution.py:74
  212.3 9.6 %fusion.1 = f32[8,256,1024]{2,1,0:T(8,128)} fusion(bf16[8,256,512]{2,1,0:T(8,128)(2,1)} %all-gather.8.cloned.1.call-done, bf16[8,512,512]{2,1,0:T(8,128)(2,1)} %get-tuple-element.18, bf16[8,512,512]{2,1,0:T(8,128)(2,1)} %get-tuple-element.17), kind=kOutput, calls=%fused_computation.5 | convolution fusion | flops 2164260864 | bytes 18874368 | tf_op jit(solution)/shard_map/mtr,mrw->mtw/dot_general | solution.py:76
  221.9 1.6 copy-done
  223.5 4.9 %convolution_convert_fusion = bf16[8,512,512]{2,1,0:T(8,128)(2,1)} fusion(bf16[8,256,512]{2,1,0:T(8,128)(2,1)S(1)} %copy-done, bf16[8,256,1024]{2,1,0:T(8,128)(2,1)} %bitcast.91, s32[]{:T(128)S(6)} %select_n.78), kind=kOutput, calls=%fused_computation.12 | convolution fusion | flops 1075838976 | bytes 8388612 | tf_op jit(solution)/shard_map/mtr,mtw->mrw/dot_general | solution.py:78
  228.8 2.9 convert_bitcast_fusion
  231.7 2.4 copy.36
  235.9 4.5 %copy.37 = bf16[1,8,512,512]{3,1,2,0:T(8,128)(2,1)S(1)} copy(bf16[1,8,512,512]{3,2,1,0:T(8,128)(2,1)} %bitcast.31) | data formatting | bytes 8388608
  240.4 3.5 %fusion = bf16[8,262144]{1,0:T(8,128)(2,1)} fusion(f32[8,262144]{1,0:T(8,128)S(1)} %fusion.23, bf16[8,262144]{1,0:T(8,128)(2,1)S(1)} %bitcast.86, bf16[8,2,8]{2,0,1:T(8,128)(2,1)S(1)} %select_convert_fusion, s32[]{:T(128)S(6)} %select_n.70), kind=kOutput, calls=%fused_computation.3 | convolution fusion | flops 37748736 | bytes 16779268 | tf_op jit(solution)/shard_map/dot_general | solution.py:96
  243.9 66.5 %reduce-scatter.5.cloned.1.call-done = f32[8,16,1024]{2,1,0:T(8,128)} async-done(((f32[8,256,1024]{2,1,0:T(8,128)}), f32[8,16,1024]{2,1,0:T(8,128)}) %reduce-scatter.5.cloned.1.call-update) | async-done | bytes 524304 | tf_op jit(solution)/shard_map/reduce_scatter | solution.py:98
  310.4 1.8 bitcast_convert_fusion
  312.2 7.0 %all-to-all-start.1 = ((bf16[8,16,1,1024]{3,1,2,0:T(8,128)(2,1)}), bf16[8,16,1,1024]{3,1,2,0:T(8,128)(2,1)S(1)}, u32[]{:S(2)}, u32[]{:S(2)}) async-start(bf16[8,16,1,1024]{3,1,2,0:T(8,128)(2,1)} %bitcast_convert_fusion), calls=%async_computation.3 | async-start | bytes 524288 | tf_op jit(solution)/shard_map/all_to_all | solution.py:101
  319.2 6.1 %reshape.138 = bf16[4096,512]{1,0:T(8,128)(2,1)} reshape(bf16[8,262144]{1,0:T(8,128)(2,1)} %fusion) | data formatting | bytes 8388608 | tf_op jit(solution)/shard_map/reshape | solution.py:100
  325.3 4.6 %all-to-all-done.1 = bf16[8,16,1,1024]{3,1,2,0:T(8,128)(2,1)S(1)} async-done(((bf16[8,16,1,1024]{3,1,2,0:T(8,128)(2,1)}), bf16[8,16,1,1024]{3,1,2,0:T(8,128)(2,1)S(1)}, u32[]{:S(2)}, u32[]{:S(2)}) %all-to-all-start.1) | async-done | bytes 262176 | tf_op jit(solution)/shard_map/all_to_all | solution.py:101
  (56 shorter events, 10.9 us)
Async XLA Ops:
  7.2 74.4 %all-gather.10.cloned.1.call-start = ((), (), s32[]{:S(2)}) async-start(), calls=%async_computation.7 | async-start | bytes 4456448 | tf_op jit(solution)/shard_map/all_gather | solution.py:31
  28.5 117.3 %reduce-scatter.3.cloned.1.call-start = ((), (), s32[]{:S(2)}) async-start(), calls=%async_computation.4 | async-start | bytes 4718592 | tf_op jit(solution)/shard_map/reduce_scatter | solution.py:63
  35.7 4.9 %copy-start.2 = (s32[16,1]{0,1:T(1,128)S(1)}, s32[16,1]{0,1:T(1,128)}, u32[]{:S(2)}) copy-start(s32[16,1]{0,1:T(1,128)} %param.10) | copy-start | bytes 196
  35.7 6.5 %copy-start.1 = (bf16[1,256,512]{2,1,0:T(8,128)(2,1)S(1)}, bf16[1,256,512]{2,1,0:T(8,128)(2,1)}, u32[]{:S(2)}) copy-start(bf16[1,256,512]{2,1,0:T(8,128)(2,1)} %param.11) | copy-start | bytes 786436
  40.6 31.0 %collective-permute-start = (bf16[8,512,512]{2,1,0:T(8,128)(2,1)}, bf16[8,512,512]{2,1,0:T(8,128)(2,1)}, u32[]{:S(2)}, u32[]{:S(2)}) collective-permute-start(bf16[8,512,512]{2,1,0:T(8,128)(2,1)} %broadcast_select_fusion.1), channel_id=1, source_target_pairs={{0,1},{1,0},{2,3},{3,2},{4,5},{5,4},{6,7},{7,6},{8,9},{9,8},{10,11... | collective-permute-start | bytes 12582920 | tf_op jit(solution)/shard_map/ppermute | solution.py:34
  90.5 121.8 %all-gather.8.cloned.1.call-start = ((), (), s32[]{:S(2)}) async-start(), calls=%async_computation.5 | async-start | bytes 2359296 | tf_op jit(solution)/shard_map/all_gather | solution.py:74
  174.0 136.5 %reduce-scatter.5.cloned.1.call-start = ((), (), s32[]{:S(2)}) async-start(), calls=%async_computation.6 | async-start | bytes 8912896 | tf_op jit(solution)/shard_map/reduce_scatter | solution.py:98
  221.9 1.6 copy-start
  228.4 7.5 %collective-permute-start.1 = (bf16[8,512,512]{2,1,0:T(8,128)(2,1)}, bf16[8,512,512]{2,1,0:T(8,128)(2,1)}, u32[]{:S(2)}, u32[]{:S(2)}) collective-permute-start(bf16[8,512,512]{2,1,0:T(8,128)(2,1)} %convolution_convert_fusion), channel_id=1, source_target_pairs={{0,1},{1,0},{2,3},{3,2},{4,5},{5,4},{6,7},{7,6},{8,9},{9,8},{10,11... | collective-permute-start | bytes 12582920 | tf_op jit(solution)/shard_map/ppermute | solution.py:81
  312.2 17.7 %all-to-all-start.1 = ((bf16[8,16,1,1024]{3,1,2,0:T(8,128)(2,1)}), bf16[8,16,1,1024]{3,1,2,0:T(8,128)(2,1)S(1)}, u32[]{:S(2)}, u32[]{:S(2)}) async-start(bf16[8,16,1,1024]{3,1,2,0:T(8,128)(2,1)} %bitcast_convert_fusion), calls=%async_computation.3 | async-start | bytes 524288 | tf_op jit(solution)/shard_map/all_to_all | solution.py:101
Sparse Core Ops, SparseCore 0:
  28.6 52.9 all-gather.9
  90.6 55.0 reduce-scatter.2
  174.1 38.1 all-gather.7
  222.0 88.3 reduce-scatter.4
